TPU v7x, 512 devices: a whole 4x4x16 slice. The times are simulated.
512 devices in a mesh: frame: 32 (over x, z_lo), row: 16 (over y, z_hi, core).
Axes of the slice: x: 4, y: 4, z: 16 (z_hi: 2, z_lo: 8; z = z_hi * 8 + z_lo), core: 2. Of those that a mesh axis runs over, the one named last changes fastest.
Arguments:
- tokens: bfloat16 [32, 4096, 512], P('frame', 'row'), may hold values from -15 to 15
- norm_spatial: float32 [512], replicated, may hold values from 0.25 to 1.75
- w_spatial: bfloat16 [512, 1536], replicated, may hold values from -10 to 10
- w_spatial_out: bfloat16 [512, 512], replicated, may hold values from -0.25 to 0.25
- norm_temporal: float32 [512], replicated, may hold values from 0.25 to 1.75
- w_temporal: bfloat16 [512, 1536], replicated, may hold values from -10 to 10
- w_temporal_out: bfloat16 [512, 512], replicated, may hold values from -0.25 to 0.25
Outputs:
- mixed: bfloat16 [32, 4096, 512], P('frame', 'row')
All inputs are finite; a program needn't handle non-finite values.
Results may differ from a plain program's by a relative error of at most 0.01.
The roundings to bfloat16 on the way count: a program that leaves them out, or rounds other values in their place, can miss the bound.
Values may be sent and summed in bfloat16 or wider, within the bound.
No kernel may reach another device: no remote copies, remote signals or barrier semaphores. Data moves between devices by JAX's collectives and lax.ppermute only.
A program may use at most 64 MiB of HBM per device.

v0:
```python
import math

import jax
import jax.numpy as jnp
from jax import lax
from jax.experimental import pallas as pl
from jax.experimental.pallas import tpu as pltpu
from jax.sharding import Mesh

from jax.sharding import PartitionSpec as P

HEADS = 8
PAIR = 2


def layer_norm(rows, gain):
    mean = jnp.mean(rows, axis=-1, keepdims=True)
    centred = rows - mean
    spread = jnp.mean(centred * centred, axis=-1, keepdims=True)
    return centred * lax.rsqrt(spread + 1e-05) * gain


def _head_scores(q_ref, k_ref, cols, scale):
    return (
        lax.dot_general(
            q_ref[:, cols], k_ref[:, cols], (((1,), (1,)), ((), ())),
            preferred_element_type=jnp.float32,
        )
        * scale
    )


def partial_kernel(q_ref, k_ref, v_ref, o_ref, m_ref, l_ref, *, size, scale):
    count = q_ref.shape[0]
    for h in range(PAIR):
        cols = slice(h * size, (h + 1) * size)
        scores = _head_scores(q_ref, k_ref, cols, scale)
        peak = jnp.max(scores, axis=1, keepdims=True)
        weights = jnp.exp(scores - peak)
        total = jnp.sum(weights, axis=1, keepdims=True)
        o_ref[:, cols] = jnp.dot(
            weights.astype(jnp.bfloat16), v_ref[:, cols], preferred_element_type=jnp.float32
        )
        m_ref[:, cols] = jnp.broadcast_to(peak, (count, size))
        l_ref[:, cols] = jnp.broadcast_to(total, (count, size))


def final_kernel(q_ref, k_ref, v_ref, o1_ref, m1_ref, l1_ref, out_ref, *, size, scale):
    for h in range(PAIR):
        cols = slice(h * size, (h + 1) * size)
        first = slice(h * size, h * size + 1)
        scores = _head_scores(q_ref, k_ref, cols, scale)
        before = m1_ref[:, first]
        peak = jnp.maximum(before, jnp.max(scores, axis=1, keepdims=True))
        weights = jnp.exp(scores - peak)
        fade = jnp.exp(before - peak)
        total = l1_ref[:, first] * fade + jnp.sum(weights, axis=1, keepdims=True)
        summed = o1_ref[:, cols] * fade + jnp.dot(
            weights.astype(jnp.bfloat16), v_ref[:, cols], preferred_element_type=jnp.float32
        )
        out_ref[:, cols] = (summed / total).astype(out_ref.dtype)


def _attention_call(kernel, query, keys, values, state, outs):
    count, width = query.shape
    length = keys.shape[0]
    size = width // HEADS
    block = PAIR * size
    body = lambda *refs: kernel(*refs, size=size, scale=1.0 / math.sqrt(size))
    row_block = pl.BlockSpec((count, block), lambda h: (0, h))
    key_block = pl.BlockSpec((length, block), lambda h: (0, h))
    return pl.pallas_call(
        body,
        grid=(width // block,),
        in_specs=[row_block, key_block, key_block] + [row_block] * len(state),
        out_specs=[row_block] * len(outs),
        out_shape=[jax.ShapeDtypeStruct((count, width), dtype) for dtype in outs],
        compiler_params=pltpu.CompilerParams(vmem_limit_bytes=48 * 1024 * 1024),
    )(query, keys, values, *state)


def spatial_partial(query, keys, values):
    return _attention_call(partial_kernel, query, keys, values, (), (jnp.float32,) * 3)


def spatial_final(query, keys, values, state):
    return _attention_call(final_kernel, query, keys, values, state, (jnp.bfloat16,))[0]


def spread_y(rows):
    rows = lax.all_gather(rows, "core", axis=0, tiled=True)
    ring = lax.axis_size("y")
    pieces = [rows]
    for shift in range(1, ring):
        pairs = [(i, (i + shift) % ring) for i in range(ring)]
        pieces.append(lax.ppermute(rows, "y", pairs))
    return jnp.concatenate(pieces, axis=0)


def attend_cells(block_qkv):
    frames, cells = (block_qkv.shape[0], block_qkv.shape[1])
    width = block_qkv.shape[2] // 3
    size = width // HEADS
    scale = 1.0 / math.sqrt(size)
    query = block_qkv[:, :, :width].reshape(frames, cells, HEADS, size)
    keys = block_qkv[:, :, width : 2 * width].reshape(frames, cells, HEADS, size)
    values = block_qkv[:, :, 2 * width :].reshape(frames, cells, HEADS, size)
    scores = jnp.einsum("fche,gche->chfg", query, keys, preferred_element_type=jnp.float32) * scale
    later = jnp.arange(frames)[:, None] >= jnp.arange(frames)[None, :]
    scores = jnp.where(later, scores, -1e30)
    peak = jnp.max(scores, axis=3, keepdims=True)
    weights = jnp.exp(scores - peak)
    total = jnp.sum(weights, axis=3)
    summed = jnp.einsum(
        "chfg,gche->fche", weights.astype(jnp.bfloat16), values, preferred_element_type=jnp.float32
    )
    context = summed / jnp.transpose(total, (2, 0, 1))[..., None]
    return context.reshape(frames, cells, width).astype(jnp.bfloat16)


def layer(
    tokens, norm_spatial, w_spatial, w_spatial_out, norm_temporal, w_temporal, w_temporal_out
):
    frames_here, rows, width = tokens.shape
    count = frames_here * rows
    resid = tokens.reshape(count, width).astype(jnp.float32)
    normed = layer_norm(resid, norm_spatial).astype(jnp.bfloat16)
    query = jnp.dot(normed, w_spatial[:, :width], preferred_element_type=jnp.float32).astype(
        jnp.bfloat16
    )
    partner = lax.ppermute(normed, "zhi", [(0, 1), (1, 0)])
    w_pairs = w_spatial[:, width:]
    near_rows = spread_y(normed)
    near = jnp.dot(near_rows, w_pairs, preferred_element_type=jnp.float32).astype(jnp.bfloat16)
    state = spatial_partial(query, near[:, :width], near[:, width:])
    far = jnp.dot(spread_y(partner), w_pairs, preferred_element_type=jnp.float32).astype(
        jnp.bfloat16
    )
    context = spatial_final(query, far[:, :width], far[:, width:], state)
    after = resid + jnp.dot(context, w_spatial_out, preferred_element_type=jnp.float32)
    second = layer_norm(after, norm_temporal).astype(jnp.bfloat16)
    owners = lax.axis_size(("x", "zlo"))
    share = rows // owners
    second = second.reshape(frames_here, owners, share, width)
    gathered = lax.all_to_all(second, ("x", "zlo"), split_axis=1, concat_axis=0, tiled=True)
    frames_all = gathered.shape[0]
    qkv_t = jnp.dot(
        gathered.reshape(frames_all * share, width), w_temporal, preferred_element_type=jnp.float32
    ).astype(jnp.bfloat16)
    context_t = attend_cells(qkv_t.reshape(frames_all, share, 3 * width))
    context_t = context_t.reshape(frames_all, 1, share, width)
    returned = lax.all_to_all(context_t, ("x", "zlo"), split_axis=0, concat_axis=1, tiled=True)
    mixed = after + jnp.dot(
        returned.reshape(count, width), w_temporal_out, preferred_element_type=jnp.float32
    )
    return mixed.reshape(frames_here, rows, width).astype(jnp.bfloat16)


def solution(mesh):
    frame_n, row_n = mesh.devices.shape
    devices = mesh.devices.reshape(4, frame_n // 4, row_n // 4, 2, 2)
    fine = Mesh(devices, ("x", "zlo", "y", "zhi", "core"))
    grid_spec = P(("x", "zlo"), ("y", "zhi", "core"), None)
    in_specs = (grid_spec, P(), P(), P(), P(), P(), P())
    return jax.shard_map(layer, mesh=fine, in_specs=in_specs, out_specs=grid_spec, check_vma=False)
```

profile of v0, /device:TPU:1, one launch (start us, length us, event | category | flops | bytes accessed | tf_op | source)
XLA Modules:
  0.0 163.9 jit_solution(18230292990535244096)
XLA Ops:
  0.0 0.0 copy-start
  0.0 0.0 copy-start.5
  0.0 1.2 convert_reduce_fusion
  1.2 1.2 fusion.27
  2.4 1.1 fusion.29
  3.5 8.6 %all_gather.7 = bf16[512,512]{1,0:T(8,128)(2,1)S(1)} all-gather(bf16[256,512]{1,0:T(8,128)(2,1)S(1)} %fusion.29), channel_id=1, replica_groups=mesh['x'=4,'zlo'=8,'y'=4,'zhi'=2,'core'=2] {'core'}, dimensions={0}, use_global_device_ids=true | all-gather | bytes 786432 | tf_op jit(solution)/shard_map/all_gather | solution.py:91
  12.2 1.9 %collective-permute-start.4 = (bf16[512,512]{1,0:T(8,128)(2,1)S(1)}, bf16[512,512]{1,0:T(8,128)(2,1)S(1)}, u32[]{:S(2)}, u32[]{:S(2)}) collective-permute-start(bf16[512,512]{1,0:T(8,128)(2,1)S(1)} %all_gather.7), channel_id=1, source_target_pairs={{0,4},{4,8},{8,12},{12,0},{1,5},{5,9},{9,13},{13,1},{2,6},{6,10},{... | collective-permute-start | bytes 1572872 | tf_op jit(solution)/shard_map/ppermute | solution.py:96
  14.1 1.9 %collective-permute-start.5 = (bf16[512,512]{1,0:T(8,128)(2,1)S(1)}, bf16[512,512]{1,0:T(8,128)(2,1)S(1)}, u32[]{:S(2)}, u32[]{:S(2)}) collective-permute-start(bf16[512,512]{1,0:T(8,128)(2,1)S(1)} %all_gather.7), channel_id=1, source_target_pairs={{0,8},{4,12},{8,0},{12,4},{1,9},{5,13},{9,1},{13,5},{2,10},{6,14},... | collective-permute-start | bytes 1572872 | tf_op jit(solution)/shard_map/ppermute | solution.py:96
  16.0 4.6 %collective-permute-start.6 = (bf16[512,512]{1,0:T(8,128)(2,1)S(1)}, bf16[512,512]{1,0:T(8,128)(2,1)S(1)}, u32[]{:S(2)}, u32[]{:S(2)}) collective-permute-start(bf16[512,512]{1,0:T(8,128)(2,1)S(1)} %all_gather.7), channel_id=1, source_target_pairs={{0,12},{4,0},{8,4},{12,8},{1,13},{5,1},{9,5},{13,9},{2,14},{6,2},{... | collective-permute-start | bytes 1572872 | tf_op jit(solution)/shard_map/ppermute | solution.py:96
  20.6 12.4 %collective-permute-start = (bf16[256,512]{1,0:T(8,128)(2,1)S(1)}, bf16[256,512]{1,0:T(8,128)(2,1)S(1)}, u32[]{:S(2)}, u32[]{:S(2)}) collective-permute-start(bf16[256,512]{1,0:T(8,128)(2,1)S(1)} %fusion.29), channel_id=1, source_target_pairs={{0,2},{2,0},{1,3},{3,1},{4,6},{6,4},{5,7},{7,5},{8,10},{10,8},{9,1... | collective-permute-start | bytes 786440 | tf_op jit(solution)/shard_map/ppermute | solution.py:131
  33.0 1.3 convolution_convert_fusion.3.refs_0_
  34.4 4.1 %collective-permute-done = bf16[256,512]{1,0:T(8,128)(2,1)S(1)} collective-permute-done((bf16[256,512]{1,0:T(8,128)(2,1)S(1)}, bf16[256,512]{1,0:T(8,128)(2,1)S(1)}, u32[]{:S(2)}, u32[]{:S(2)}) %collective-permute-start) | collective-permute-done | bytes 262176 | tf_op jit(solution)/shard_map/ppermute | solution.py:131
  38.5 3.9 %all_gather.6 = bf16[512,512]{1,0:T(8,128)(2,1)S(1)} all-gather(bf16[256,512]{1,0:T(8,128)(2,1)S(1)} %collective-permute-done), channel_id=1, replica_groups=mesh['x'=4,'zlo'=8,'y'=4,'zhi'=2,'core'=2] {'core'}, dimensions={0}, use_global_device_ids=true | all-gather | bytes 786432 | tf_op jit(solution)/shard_map/all_gather | solution.py:91
  42.4 2.3 %collective-permute-start.1 = (bf16[512,512]{1,0:T(8,128)(2,1)S(1)}, bf16[512,512]{1,0:T(8,128)(2,1)S(1)}, u32[]{:S(2)}, u32[]{:S(2)}) collective-permute-start(bf16[512,512]{1,0:T(8,128)(2,1)S(1)} %all_gather.6), channel_id=1, source_target_pairs={{0,4},{4,8},{8,12},{12,0},{1,5},{5,9},{9,13},{13,1},{2,6},{6,10},{... | collective-permute-start | bytes 1572872 | tf_op jit(solution)/shard_map/ppermute | solution.py:96
  44.7 9.5 %collective-permute-start.2 = (bf16[512,512]{1,0:T(8,128)(2,1)S(1)}, bf16[512,512]{1,0:T(8,128)(2,1)S(1)}, u32[]{:S(2)}, u32[]{:S(2)}) collective-permute-start(bf16[512,512]{1,0:T(8,128)(2,1)S(1)} %all_gather.6), channel_id=1, source_target_pairs={{0,8},{4,12},{8,0},{12,4},{1,9},{5,13},{9,1},{13,5},{2,10},{6,14},... | collective-permute-start | bytes 1572872 | tf_op jit(solution)/shard_map/ppermute | solution.py:96
  54.2 0.0 collective-permute-done.4
  54.2 4.0 %collective-permute-start.3 = (bf16[512,512]{1,0:T(8,128)(2,1)S(1)}, bf16[512,512]{1,0:T(8,128)(2,1)S(1)}, u32[]{:S(2)}, u32[]{:S(2)}) collective-permute-start(bf16[512,512]{1,0:T(8,128)(2,1)S(1)} %all_gather.6), channel_id=1, source_target_pairs={{0,12},{4,0},{8,4},{12,8},{1,13},{5,1},{9,5},{13,9},{2,14},{6,2},{... | collective-permute-start | bytes 1572872 | tf_op jit(solution)/shard_map/ppermute | solution.py:96
  58.2 0.0 collective-permute-done.5
  58.2 0.0 collective-permute-done.6
  58.2 0.0 copy-done.5
  58.2 2.3 %convolution_convert_fusion = bf16[2048,1024]{1,0:T(8,128)(2,1)S(1)} fusion(bf16[512,512]{1,0:T(8,128)(2,1)S(1)} %collective-permute-done.6, bf16[512,512]{1,0:T(8,128)(2,1)S(1)} %collective-permute-done.5, bf16[512,512]{1,0:T(8,128)(2,1)S(1)} %collective-permute-done.4, bf16[512,512]{1,0:T(8,128)(2,1)S(1)} %all_gather.7, bf16[512,1536]{1,0:T(8,128)(2,1)S(1)} %copy-done.5), kind=kOutput, calls=%fused_computation | convolution fusion | flops 2157969408 | bytes 7340032 | tf_op jit(solution)/shard_map/dot_general | solution.py:134
  60.6 0.3 fusion.41
  60.9 9.2 %shard_map.73 = (f32[256,512]{1,0:T(8,128)S(1)}, f32[256,512]{1,0:T(8,128)S(1)}, f32[256,512]{1,0:T(8,128)S(1)}) custom-call(bf16[256,512]{1,0:T(8,128)(2,1)S(1)} %convolution_convert_fusion.3.refs_0_, bf16[2048,512]{1,0:T(8,128)(2,1)S(1)} %get-tuple-element.12.refs_1_, bf16[2048,512]{1,0:T(8,128)(2,1)S(1)} %get-tuple-element.11.refs_2_), custom_call_target="tpu_custom_call" | custom-call | tf_op jit(solution)/shard_map/pallas_call | solution.py:72
  70.1 0.0 collective-permute-done.1
  70.1 5.3 %collective-permute-done.2 = bf16[512,512]{1,0:T(8,128)(2,1)S(1)} collective-permute-done((bf16[512,512]{1,0:T(8,128)(2,1)S(1)}, bf16[512,512]{1,0:T(8,128)(2,1)S(1)}, u32[]{:S(2)}, u32[]{:S(2)}) %collective-permute-start.2) | collective-permute-done | bytes 524320 | tf_op jit(solution)/shard_map/ppermute | solution.py:96
  75.4 1.4 collective-permute-done.3
  76.8 2.3 %convolution_convert_fusion.1 = bf16[2048,1024]{1,0:T(8,128)(2,1)S(1)} fusion(bf16[512,512]{1,0:T(8,128)(2,1)S(1)} %collective-permute-done.3, bf16[512,512]{1,0:T(8,128)(2,1)S(1)} %collective-permute-done.2, bf16[512,512]{1,0:T(8,128)(2,1)S(1)} %collective-permute-done.1, bf16[512,512]{1,0:T(8,128)(2,1)S(1)} %all_gather.6, bf16[512,1536]{1,0:T(8,128)(2,1)S(1)} %copy-done.5), kind=kOutput, calls=%fused_computation.1 | convolution fusion | flops 2157969408 | bytes 7340032 | tf_op jit(solution)/shard_map/dot_general | solution.py:136
  79.1 1.6 fusion.42
  80.7 0.0 copy-start.1
  80.7 0.0 copy-start.3
  80.7 10.9 %shard_map.74 = bf16[256,512]{1,0:T(8,128)(2,1)S(1)} custom-call(bf16[256,512]{1,0:T(8,128)(2,1)S(1)} %convolution_convert_fusion.3.refs_0_, bf16[2048,512]{1,0:T(8,128)(2,1)S(1)} %get-tuple-element.14.refs_1_, bf16[2048,512]{1,0:T(8,128)(2,1)} %get-tuple-element.13.refs_2_, f32[256,512]{1,0:T(8,128)S(1)} %get-tuple-element.8.refs_3_, ...), custom_call_target="tpu_custom_call" | custom-call | tf_op jit(solution)/shard_map/pallas_call | solution.py:72
  91.7 0.0 copy-done.1
  91.7 0.0 copy-done.3
  91.7 0.0 copy-start.4
  91.7 0.4 fusion.44
  92.1 0.2 multiply_reduce_fusion
  92.3 0.1 copy-done.4
  92.4 0.9 fusion.36
  93.2 21.7 %all-to-all-start = ((bf16[1,32,8,512]{3,2,0,1:T(8,128)(2,1)}), bf16[1,32,8,512]{3,2,0,1:T(8,128)(2,1)S(1)}, u32[]{:S(2)}, u32[]{:S(2)}) async-start(bf16[1,32,8,512]{3,2,0,1:T(8,128)(2,1)} %fusion.36), calls=%async_computation | async-start | bytes 524288 | tf_op jit(solution)/shard_map/all_to_all | solution.py:145
  114.9 18.5 %all-to-all-done = bf16[1,32,8,512]{3,2,0,1:T(8,128)(2,1)S(1)} async-done(((bf16[1,32,8,512]{3,2,0,1:T(8,128)(2,1)}), bf16[1,32,8,512]{3,2,0,1:T(8,128)(2,1)S(1)}, u32[]{:S(2)}, u32[]{:S(2)}) %all-to-all-start) | async-done | bytes 262176 | tf_op jit(solution)/shard_map/all_to_all | solution.py:145
  133.4 0.0 copy-done
  133.4 0.6 fusion
  134.0 0.1 fusion.43
  134.1 0.3 reshape.78
  134.4 1.1 reshape.79
  135.4 0.3 reshape.77
  135.7 1.9 %fusion.45 = (f32[8,8,32]{2,1,0:T(8,128)S(1)}, f32[8,8,32,32]{2,3,1,0:T(8,128)S(1)}) fusion(bf16[32,8,8,64]{3,2,1,0:T(8,128)(2,1)} %reshape.79, bf16[32,8,8,64]{3,2,1,0:T(8,128)(2,1)S(1)} %reshape.78, pred[32,32]{0,1:T(8,128)(4,1)S(1)} %iota_compare_fusion), kind=kOutput, calls=%fused_computation.62 | convolution fusion | flops 8583168 | bytes 795648 | tf_op jit(solution)/shard_map/fche,gche->chfg/dot_general | solution.py:108
  137.6 0.3 fusion.20
  137.9 0.8 fusion.17
  138.7 0.0 copy-start.2
  138.7 0.2 copy.19
  138.9 0.3 convert_element_type.56
  139.2 23.7 %all_to_all.8 = bf16[32,1,8,512]{3,2,1,0:T(8,128)(2,1)S(1)} all-to-all(bf16[32,1,8,512]{3,2,1,0:T(8,128)(2,1)S(1)} %bitcast.45), channel_id=1, replica_groups=mesh['x'=4,'zlo'=8,'y'=4,'zhi'=2,'core'=2] {'x','zlo'}, dimensions={0} | all-to-all | bytes 524288 | tf_op jit(solution)/shard_map/all_to_all | solution.py:152
  162.9 0.0 copy-done.2
  162.9 1.0 fusion.19
  (5 shorter events, 0.0 us)
Async XLA Ops:
  0.0 133.4 %copy-start = (bf16[512,1536]{1,0:T(8,128)(2,1)S(1)}, bf16[512,1536]{1,0:T(8,128)(2,1)}, u32[]{:S(2)}) copy-start(bf16[512,1536]{1,0:T(8,128)(2,1)} %param.12) | copy-start | bytes 4718596
  0.0 58.2 %copy-start.5 = (bf16[512,1536]{1,0:T(8,128)(2,1)S(1)}, bf16[512,1536]{1,0:T(8,128)(2,1)}, u32[]{:S(2)}) copy-start(bf16[512,1536]{1,0:T(8,128)(2,1)} %param.9) | copy-start | bytes 4718596
  12.2 42.0 %collective-permute-start.4 = (bf16[512,512]{1,0:T(8,128)(2,1)S(1)}, bf16[512,512]{1,0:T(8,128)(2,1)S(1)}, u32[]{:S(2)}, u32[]{:S(2)}) collective-permute-start(bf16[512,512]{1,0:T(8,128)(2,1)S(1)} %all_gather.7), channel_id=1, source_target_pairs={{0,4},{4,8},{8,12},{12,0},{1,5},{5,9},{9,13},{13,1},{2,6},{6,10},{... | collective-permute-start | bytes 1572872 | tf_op jit(solution)/shard_map/ppermute | solution.py:96
  14.1 44.1 %collective-permute-start.5 = (bf16[512,512]{1,0:T(8,128)(2,1)S(1)}, bf16[512,512]{1,0:T(8,128)(2,1)S(1)}, u32[]{:S(2)}, u32[]{:S(2)}) collective-permute-start(bf16[512,512]{1,0:T(8,128)(2,1)S(1)} %all_gather.7), channel_id=1, source_target_pairs={{0,8},{4,12},{8,0},{12,4},{1,9},{5,13},{9,1},{13,5},{2,10},{6,14},... | collective-permute-start | bytes 1572872 | tf_op jit(solution)/shard_map/ppermute | solution.py:96
  16.0 42.2 %collective-permute-start.6 = (bf16[512,512]{1,0:T(8,128)(2,1)S(1)}, bf16[512,512]{1,0:T(8,128)(2,1)S(1)}, u32[]{:S(2)}, u32[]{:S(2)}) collective-permute-start(bf16[512,512]{1,0:T(8,128)(2,1)S(1)} %all_gather.7), channel_id=1, source_target_pairs={{0,12},{4,0},{8,4},{12,8},{1,13},{5,1},{9,5},{13,9},{2,14},{6,2},{... | collective-permute-start | bytes 1572872 | tf_op jit(solution)/shard_map/ppermute | solution.py:96
  20.6 17.9 %collective-permute-start = (bf16[256,512]{1,0:T(8,128)(2,1)S(1)}, bf16[256,512]{1,0:T(8,128)(2,1)S(1)}, u32[]{:S(2)}, u32[]{:S(2)}) collective-permute-start(bf16[256,512]{1,0:T(8,128)(2,1)S(1)} %fusion.29), channel_id=1, source_target_pairs={{0,2},{2,0},{1,3},{3,1},{4,6},{6,4},{5,7},{7,5},{8,10},{10,8},{9,1... | collective-permute-start | bytes 786440 | tf_op jit(solution)/shard_map/ppermute | solution.py:131
  42.4 27.7 %collective-permute-start.1 = (bf16[512,512]{1,0:T(8,128)(2,1)S(1)}, bf16[512,512]{1,0:T(8,128)(2,1)S(1)}, u32[]{:S(2)}, u32[]{:S(2)}) collective-permute-start(bf16[512,512]{1,0:T(8,128)(2,1)S(1)} %all_gather.6), channel_id=1, source_target_pairs={{0,4},{4,8},{8,12},{12,0},{1,5},{5,9},{9,13},{13,1},{2,6},{6,10},{... | collective-permute-start | bytes 1572872 | tf_op jit(solution)/shard_map/ppermute | solution.py:96
  44.7 30.8 %collective-permute-start.2 = (bf16[512,512]{1,0:T(8,128)(2,1)S(1)}, bf16[512,512]{1,0:T(8,128)(2,1)S(1)}, u32[]{:S(2)}, u32[]{:S(2)}) collective-permute-start(bf16[512,512]{1,0:T(8,128)(2,1)S(1)} %all_gather.6), channel_id=1, source_target_pairs={{0,8},{4,12},{8,0},{12,4},{1,9},{5,13},{9,1},{13,5},{2,10},{6,14},... | collective-permute-start | bytes 1572872 | tf_op jit(solution)/shard_map/ppermute | solution.py:96
  54.2 22.6 %collective-permute-start.3 = (bf16[512,512]{1,0:T(8,128)(2,1)S(1)}, bf16[512,512]{1,0:T(8,128)(2,1)S(1)}, u32[]{:S(2)}, u32[]{:S(2)}) collective-permute-start(bf16[512,512]{1,0:T(8,128)(2,1)S(1)} %all_gather.6), channel_id=1, source_target_pairs={{0,12},{4,0},{8,4},{12,8},{1,13},{5,1},{9,5},{13,9},{2,14},{6,2},{... | collective-permute-start | bytes 1572872 | tf_op jit(solution)/shard_map/ppermute | solution.py:96
  80.7 10.9 %copy-start.1 = (bf16[1,256,512]{2,1,0:T(8,128)(2,1)S(1)}, bf16[1,256,512]{2,1,0:T(8,128)(2,1)}, u32[]{:S(2)}) copy-start(bf16[1,256,512]{2,1,0:T(8,128)(2,1)} %param.7) | copy-start | bytes 786436
  80.7 11.0 %copy-start.3 = (bf16[512,512]{1,0:T(8,128)(2,1)S(1)}, bf16[512,512]{1,0:T(8,128)(2,1)}, u32[]{:S(2)}) copy-start(bf16[512,512]{1,0:T(8,128)(2,1)} %param.10) | copy-start | bytes 1572868
  91.7 0.7 copy-start.4
  93.2 40.2 %all-to-all-start = ((bf16[1,32,8,512]{3,2,0,1:T(8,128)(2,1)}), bf16[1,32,8,512]{3,2,0,1:T(8,128)(2,1)S(1)}, u32[]{:S(2)}, u32[]{:S(2)}) async-start(bf16[1,32,8,512]{3,2,0,1:T(8,128)(2,1)} %fusion.36), calls=%async_computation | async-start | bytes 524288 | tf_op jit(solution)/shard_map/all_to_all | solution.py:145
  138.7 24.2 %copy-start.2 = (bf16[512,512]{1,0:T(8,128)(2,1)S(1)}, bf16[512,512]{1,0:T(8,128)(2,1)}, u32[]{:S(2)}) copy-start(bf16[512,512]{1,0:T(8,128)(2,1)} %param.13) | copy-start | bytes 1572868
where the time goes:
time: 166 us; the launch traced here: 164 us
  starting transfers between devices  58.3 us (35%)
  blocking collectives  36.2 us (22%)
  waiting for transfers between devices  29.3 us (18%)
  Pallas kernels  20.2 us (12%)
  matrix products  10.6 us (6%)
  other arithmetic  4.88 us (3%)
  local copies, waits for them, and re-layouts  4.17 us (3%)
    ppermute x6, starting transfers between devices, spread_y(): pieces.append(lax.ppermute(rows, 'y', pairs))  24.2 us
    all_to_all x1, blocking collectives, layer(): lax.all_to_all(context_t, ('x', 'zlo'), split_axis=0, concat_axis=1, tile...  23.7 us
    all_to_all x1, starting transfers between devices, layer(): lax.all_to_all(second, ('x', 'zlo'), split_axis=1, concat_axis=0, tiled=T...  21.7 us
    pallas_call x2, Pallas kernels, _attention_call(): pl.pallas_call(body, grid=(width // block,), in_specs=[row_block, key_blo...  20.2 us
    all_to_all x1, waiting for transfers between devices, layer(): lax.all_to_all(second, ('x', 'zlo'), split_axis=1, concat_axis=0, tiled=T...  18.5 us
    all_gather x2, blocking collectives, spread_y(): rows = lax.all_gather(rows, 'core', axis=0, tiled=True)  12.5 us
    ppermute x1, starting transfers between devices, layer(): partner = lax.ppermute(normed, 'zhi', [(0, 1), (1, 0)])  12.4 us
    ppermute x6, waiting for transfers between devices, spread_y(): pieces.append(lax.ppermute(rows, 'y', pairs))  6.69 us
  transfers between devices with their start and end apart: 8, of which 4 were waited for; matrix products, arithmetic and copies ran while one was open for 2% of the time, Pallas kernels for 6%

commit v1 on v0

--- a/solution.py
+++ b/solution.py
@@ -133,9 +133,8 @@
     near_rows = spread_y(normed)
     near = jnp.dot(near_rows, w_pairs, preferred_element_type=jnp.float32).astype(jnp.bfloat16)
     state = spatial_partial(query, near[:, :width], near[:, width:])
-    far = jnp.dot(spread_y(partner), w_pairs, preferred_element_type=jnp.float32).astype(
-        jnp.bfloat16
-    )
+    far_rows = spread_y(partner)
+    far = jnp.dot(far_rows, w_pairs, preferred_element_type=jnp.float32).astype(jnp.bfloat16)
     context = spatial_final(query, far[:, :width], far[:, width:], state)
     after = resid + jnp.dot(context, w_spatial_out, preferred_element_type=jnp.float32)
     second = layer_norm(after, norm_temporal).astype(jnp.bfloat16)

time: 166 us -> 166 us (level)
  no operation moved by 1% of the time
where the time goes in v1:
time: 166 us; the launch traced here: 164 us
  starting transfers between devices  58.3 us (35%)
  blocking collectives  36.2 us (22%)
  waiting for transfers between devices  29.3 us (18%)
  Pallas kernels  20.2 us (12%)
  matrix products  10.6 us (6%)
  other arithmetic  4.88 us (3%)
  local copies, waits for them, and re-layouts  4.17 us (3%)
    ppermute x6, starting transfers between devices, spread_y(): pieces.append(lax.ppermute(rows, 'y', pairs))  24.2 us
    all_to_all x1, blocking collectives, layer(): lax.all_to_all(context_t, ('x', 'zlo'), split_axis=0, concat_axis=1, tile...  23.7 us
    all_to_all x1, starting transfers between devices, layer(): lax.all_to_all(second, ('x', 'zlo'), split_axis=1, concat_axis=0, tiled=T...  21.7 us
    pallas_call x2, Pallas kernels, _attention_call(): pl.pallas_call(body, grid=(width // block,), in_specs=[row_block, key_blo...  20.2 us
    all_to_all x1, waiting for transfers between devices, layer(): lax.all_to_all(second, ('x', 'zlo'), split_axis=1, concat_axis=0, tiled=T...  18.5 us
    all_gather x2, blocking collectives, spread_y(): rows = lax.all_gather(rows, 'core', axis=0, tiled=True)  12.5 us
    ppermute x1, starting transfers between devices, layer(): partner = lax.ppermute(normed, 'zhi', [(0, 1), (1, 0)])  12.4 us
    ppermute x6, waiting for transfers between devices, spread_y(): pieces.append(lax.ppermute(rows, 'y', pairs))  6.69 us
  transfers between devices with their start and end apart: 8, of which 4 were waited for; matrix products, arithmetic and copies ran while one was open for 2% of the time, Pallas kernels for 6%

profile of v1, /device:TPU:1, one launch (start us, length us, event | category | flops | bytes accessed | tf_op | source)
XLA Modules:
  0.0 163.9 jit_solution(18230292990535244096)
XLA Ops:
  0.0 0.0 copy-start
  0.0 0.0 copy-start.5
  0.0 1.2 convert_reduce_fusion
  1.2 1.2 fusion.27
  2.4 1.1 fusion.29
  3.5 8.6 %all_gather.7 = bf16[512,512]{1,0:T(8,128)(2,1)S(1)} all-gather(bf16[256,512]{1,0:T(8,128)(2,1)S(1)} %fusion.29), channel_id=1, replica_groups=mesh['x'=4,'zlo'=8,'y'=4,'zhi'=2,'core'=2] {'core'}, dimensions={0}, use_global_device_ids=true | all-gather | bytes 786432 | tf_op jit(solution)/shard_map/all_gather | solution.py:91
  12.2 1.9 %collective-permute-start.4 = (bf16[512,512]{1,0:T(8,128)(2,1)S(1)}, bf16[512,512]{1,0:T(8,128)(2,1)S(1)}, u32[]{:S(2)}, u32[]{:S(2)}) collective-permute-start(bf16[512,512]{1,0:T(8,128)(2,1)S(1)} %all_gather.7), channel_id=1, source_target_pairs={{0,4},{4,8},{8,12},{12,0},{1,5},{5,9},{9,13},{13,1},{2,6},{6,10},{... | collective-permute-start | bytes 1572872 | tf_op jit(solution)/shard_map/ppermute | solution.py:96
  14.1 1.9 %collective-permute-start.5 = (bf16[512,512]{1,0:T(8,128)(2,1)S(1)}, bf16[512,512]{1,0:T(8,128)(2,1)S(1)}, u32[]{:S(2)}, u32[]{:S(2)}) collective-permute-start(bf16[512,512]{1,0:T(8,128)(2,1)S(1)} %all_gather.7), channel_id=1, source_target_pairs={{0,8},{4,12},{8,0},{12,4},{1,9},{5,13},{9,1},{13,5},{2,10},{6,14},... | collective-permute-start | bytes 1572872 | tf_op jit(solution)/shard_map/ppermute | solution.py:96
  16.0 4.6 %collective-permute-start.6 = (bf16[512,512]{1,0:T(8,128)(2,1)S(1)}, bf16[512,512]{1,0:T(8,128)(2,1)S(1)}, u32[]{:S(2)}, u32[]{:S(2)}) collective-permute-start(bf16[512,512]{1,0:T(8,128)(2,1)S(1)} %all_gather.7), channel_id=1, source_target_pairs={{0,12},{4,0},{8,4},{12,8},{1,13},{5,1},{9,5},{13,9},{2,14},{6,2},{... | collective-permute-start | bytes 1572872 | tf_op jit(solution)/shard_map/ppermute | solution.py:96
  20.6 12.4 %collective-permute-start = (bf16[256,512]{1,0:T(8,128)(2,1)S(1)}, bf16[256,512]{1,0:T(8,128)(2,1)S(1)}, u32[]{:S(2)}, u32[]{:S(2)}) collective-permute-start(bf16[256,512]{1,0:T(8,128)(2,1)S(1)} %fusion.29), channel_id=1, source_target_pairs={{0,2},{2,0},{1,3},{3,1},{4,6},{6,4},{5,7},{7,5},{8,10},{10,8},{9,1... | collective-permute-start | bytes 786440 | tf_op jit(solution)/shard_map/ppermute | solution.py:131
  33.0 1.3 convolution_convert_fusion.3.refs_0_
  34.4 4.1 %collective-permute-done = bf16[256,512]{1,0:T(8,128)(2,1)S(1)} collective-permute-done((bf16[256,512]{1,0:T(8,128)(2,1)S(1)}, bf16[256,512]{1,0:T(8,128)(2,1)S(1)}, u32[]{:S(2)}, u32[]{:S(2)}) %collective-permute-start) | collective-permute-done | bytes 262176 | tf_op jit(solution)/shard_map/ppermute | solution.py:131
  38.5 3.9 %all_gather.6 = bf16[512,512]{1,0:T(8,128)(2,1)S(1)} all-gather(bf16[256,512]{1,0:T(8,128)(2,1)S(1)} %collective-permute-done), channel_id=1, replica_groups=mesh['x'=4,'zlo'=8,'y'=4,'zhi'=2,'core'=2] {'core'}, dimensions={0}, use_global_device_ids=true | all-gather | bytes 786432 | tf_op jit(solution)/shard_map/all_gather | solution.py:91
  42.4 2.3 %collective-permute-start.1 = (bf16[512,512]{1,0:T(8,128)(2,1)S(1)}, bf16[512,512]{1,0:T(8,128)(2,1)S(1)}, u32[]{:S(2)}, u32[]{:S(2)}) collective-permute-start(bf16[512,512]{1,0:T(8,128)(2,1)S(1)} %all_gather.6), channel_id=1, source_target_pairs={{0,4},{4,8},{8,12},{12,0},{1,5},{5,9},{9,13},{13,1},{2,6},{6,10},{... | collective-permute-start | bytes 1572872 | tf_op jit(solution)/shard_map/ppermute | solution.py:96
  44.7 9.5 %collective-permute-start.2 = (bf16[512,512]{1,0:T(8,128)(2,1)S(1)}, bf16[512,512]{1,0:T(8,128)(2,1)S(1)}, u32[]{:S(2)}, u32[]{:S(2)}) collective-permute-start(bf16[512,512]{1,0:T(8,128)(2,1)S(1)} %all_gather.6), channel_id=1, source_target_pairs={{0,8},{4,12},{8,0},{12,4},{1,9},{5,13},{9,1},{13,5},{2,10},{6,14},... | collective-permute-start | bytes 1572872 | tf_op jit(solution)/shard_map/ppermute | solution.py:96
  54.2 0.0 collective-permute-done.4
  54.2 4.0 %collective-permute-start.3 = (bf16[512,512]{1,0:T(8,128)(2,1)S(1)}, bf16[512,512]{1,0:T(8,128)(2,1)S(1)}, u32[]{:S(2)}, u32[]{:S(2)}) collective-permute-start(bf16[512,512]{1,0:T(8,128)(2,1)S(1)} %all_gather.6), channel_id=1, source_target_pairs={{0,12},{4,0},{8,4},{12,8},{1,13},{5,1},{9,5},{13,9},{2,14},{6,2},{... | collective-permute-start | bytes 1572872 | tf_op jit(solution)/shard_map/ppermute | solution.py:96
  58.2 0.0 collective-permute-done.5
  58.2 0.0 collective-permute-done.6
  58.2 0.0 copy-done.5
  58.2 2.3 %convolution_convert_fusion = bf16[2048,1024]{1,0:T(8,128)(2,1)S(1)} fusion(bf16[512,512]{1,0:T(8,128)(2,1)S(1)} %collective-permute-done.6, bf16[512,512]{1,0:T(8,128)(2,1)S(1)} %collective-permute-done.5, bf16[512,512]{1,0:T(8,128)(2,1)S(1)} %collective-permute-done.4, bf16[512,512]{1,0:T(8,128)(2,1)S(1)} %all_gather.7, bf16[512,1536]{1,0:T(8,128)(2,1)S(1)} %copy-done.5), kind=kOutput, calls=%fused_computation | convolution fusion | flops 2157969408 | bytes 7340032 | tf_op jit(solution)/shard_map/dot_general | solution.py:134
  60.6 0.3 fusion.41
  60.9 9.2 %shard_map.73 = (f32[256,512]{1,0:T(8,128)S(1)}, f32[256,512]{1,0:T(8,128)S(1)}, f32[256,512]{1,0:T(8,128)S(1)}) custom-call(bf16[256,512]{1,0:T(8,128)(2,1)S(1)} %convolution_convert_fusion.3.refs_0_, bf16[2048,512]{1,0:T(8,128)(2,1)S(1)} %get-tuple-element.12.refs_1_, bf16[2048,512]{1,0:T(8,128)(2,1)S(1)} %get-tuple-element.11.refs_2_), custom_call_target="tpu_custom_call" | custom-call | tf_op jit(solution)/shard_map/pallas_call | solution.py:72
  70.1 0.0 collective-permute-done.1
  70.1 5.3 %collective-permute-done.2 = bf16[512,512]{1,0:T(8,128)(2,1)S(1)} collective-permute-done((bf16[512,512]{1,0:T(8,128)(2,1)S(1)}, bf16[512,512]{1,0:T(8,128)(2,1)S(1)}, u32[]{:S(2)}, u32[]{:S(2)}) %collective-permute-start.2) | collective-permute-done | bytes 524320 | tf_op jit(solution)/shard_map/ppermute | solution.py:96
  75.4 1.4 collective-permute-done.3
  76.8 2.3 %convolution_convert_fusion.1 = bf16[2048,1024]{1,0:T(8,128)(2,1)S(1)} fusion(bf16[512,512]{1,0:T(8,128)(2,1)S(1)} %collective-permute-done.3, bf16[512,512]{1,0:T(8,128)(2,1)S(1)} %collective-permute-done.2, bf16[512,512]{1,0:T(8,128)(2,1)S(1)} %collective-permute-done.1, bf16[512,512]{1,0:T(8,128)(2,1)S(1)} %all_gather.6, bf16[512,1536]{1,0:T(8,128)(2,1)S(1)} %copy-done.5), kind=kOutput, calls=%fused_computation.1 | convolution fusion | flops 2157969408 | bytes 7340032 | tf_op jit(solution)/shard_map/dot_general | solution.py:137
  79.1 1.6 fusion.42
  80.7 0.0 copy-start.1
  80.7 0.0 copy-start.3
  80.7 10.9 %shard_map.74 = bf16[256,512]{1,0:T(8,128)(2,1)S(1)} custom-call(bf16[256,512]{1,0:T(8,128)(2,1)S(1)} %convolution_convert_fusion.3.refs_0_, bf16[2048,512]{1,0:T(8,128)(2,1)S(1)} %get-tuple-element.14.refs_1_, bf16[2048,512]{1,0:T(8,128)(2,1)} %get-tuple-element.13.refs_2_, f32[256,512]{1,0:T(8,128)S(1)} %get-tuple-element.8.refs_3_, ...), custom_call_target="tpu_custom_call" | custom-call | tf_op jit(solution)/shard_map/pallas_call | solution.py:72
  91.7 0.0 copy-done.1
  91.7 0.0 copy-done.3
  91.7 0.0 copy-start.4
  91.7 0.4 fusion.44
  92.1 0.2 multiply_reduce_fusion
  92.3 0.1 copy-done.4
  92.4 0.9 fusion.36
  93.2 21.7 %all-to-all-start = ((bf16[1,32,8,512]{3,2,0,1:T(8,128)(2,1)}), bf16[1,32,8,512]{3,2,0,1:T(8,128)(2,1)S(1)}, u32[]{:S(2)}, u32[]{:S(2)}) async-start(bf16[1,32,8,512]{3,2,0,1:T(8,128)(2,1)} %fusion.36), calls=%async_computation | async-start | bytes 524288 | tf_op jit(solution)/shard_map/all_to_all | solution.py:144
  114.9 18.5 %all-to-all-done = bf16[1,32,8,512]{3,2,0,1:T(8,128)(2,1)S(1)} async-done(((bf16[1,32,8,512]{3,2,0,1:T(8,128)(2,1)}), bf16[1,32,8,512]{3,2,0,1:T(8,128)(2,1)S(1)}, u32[]{:S(2)}, u32[]{:S(2)}) %all-to-all-start) | async-done | bytes 262176 | tf_op jit(solution)/shard_map/all_to_all | solution.py:144
  133.4 0.0 copy-done
  133.4 0.6 fusion
  134.0 0.1 fusion.43
  134.1 0.3 reshape.78
  134.4 1.1 reshape.79
  135.4 0.3 reshape.77
  135.7 1.9 %fusion.45 = (f32[8,8,32]{2,1,0:T(8,128)S(1)}, f32[8,8,32,32]{2,3,1,0:T(8,128)S(1)}) fusion(bf16[32,8,8,64]{3,2,1,0:T(8,128)(2,1)} %reshape.79, bf16[32,8,8,64]{3,2,1,0:T(8,128)(2,1)S(1)} %reshape.78, pred[32,32]{0,1:T(8,128)(4,1)S(1)} %iota_compare_fusion), kind=kOutput, calls=%fused_computation.62 | convolution fusion | flops 8583168 | bytes 795648 | tf_op jit(solution)/shard_map/fche,gche->chfg/dot_general | solution.py:108
  137.6 0.3 fusion.20
  137.9 0.8 fusion.17
  138.7 0.0 copy-start.2
  138.7 0.2 copy.19
  138.9 0.3 convert_element_type.56
  139.2 23.7 %all_to_all.8 = bf16[32,1,8,512]{3,2,1,0:T(8,128)(2,1)S(1)} all-to-all(bf16[32,1,8,512]{3,2,1,0:T(8,128)(2,1)S(1)} %bitcast.45), channel_id=1, replica_groups=mesh['x'=4,'zlo'=8,'y'=4,'zhi'=2,'core'=2] {'x','zlo'}, dimensions={0} | all-to-all | bytes 524288 | tf_op jit(solution)/shard_map/all_to_all | solution.py:151
  162.9 0.0 copy-done.2
  162.9 1.0 fusion.19
  (5 shorter events, 0.0 us)
Async XLA Ops:
  0.0 133.4 %copy-start = (bf16[512,1536]{1,0:T(8,128)(2,1)S(1)}, bf16[512,1536]{1,0:T(8,128)(2,1)}, u32[]{:S(2)}) copy-start(bf16[512,1536]{1,0:T(8,128)(2,1)} %param.12) | copy-start | bytes 4718596
  0.0 58.2 %copy-start.5 = (bf16[512,1536]{1,0:T(8,128)(2,1)S(1)}, bf16[512,1536]{1,0:T(8,128)(2,1)}, u32[]{:S(2)}) copy-start(bf16[512,1536]{1,0:T(8,128)(2,1)} %param.9) | copy-start | bytes 4718596
  12.2 42.0 %collective-permute-start.4 = (bf16[512,512]{1,0:T(8,128)(2,1)S(1)}, bf16[512,512]{1,0:T(8,128)(2,1)S(1)}, u32[]{:S(2)}, u32[]{:S(2)}) collective-permute-start(bf16[512,512]{1,0:T(8,128)(2,1)S(1)} %all_gather.7), channel_id=1, source_target_pairs={{0,4},{4,8},{8,12},{12,0},{1,5},{5,9},{9,13},{13,1},{2,6},{6,10},{... | collective-permute-start | bytes 1572872 | tf_op jit(solution)/shard_map/ppermute | solution.py:96
  14.1 44.1 %collective-permute-start.5 = (bf16[512,512]{1,0:T(8,128)(2,1)S(1)}, bf16[512,512]{1,0:T(8,128)(2,1)S(1)}, u32[]{:S(2)}, u32[]{:S(2)}) collective-permute-start(bf16[512,512]{1,0:T(8,128)(2,1)S(1)} %all_gather.7), channel_id=1, source_target_pairs={{0,8},{4,12},{8,0},{12,4},{1,9},{5,13},{9,1},{13,5},{2,10},{6,14},... | collective-permute-start | bytes 1572872 | tf_op jit(solution)/shard_map/ppermute | solution.py:96
  16.0 42.2 %collective-permute-start.6 = (bf16[512,512]{1,0:T(8,128)(2,1)S(1)}, bf16[512,512]{1,0:T(8,128)(2,1)S(1)}, u32[]{:S(2)}, u32[]{:S(2)}) collective-permute-start(bf16[512,512]{1,0:T(8,128)(2,1)S(1)} %all_gather.7), channel_id=1, source_target_pairs={{0,12},{4,0},{8,4},{12,8},{1,13},{5,1},{9,5},{13,9},{2,14},{6,2},{... | collective-permute-start | bytes 1572872 | tf_op jit(solution)/shard_map/ppermute | solution.py:96
  20.6 17.9 %collective-permute-start = (bf16[256,512]{1,0:T(8,128)(2,1)S(1)}, bf16[256,512]{1,0:T(8,128)(2,1)S(1)}, u32[]{:S(2)}, u32[]{:S(2)}) collective-permute-start(bf16[256,512]{1,0:T(8,128)(2,1)S(1)} %fusion.29), channel_id=1, source_target_pairs={{0,2},{2,0},{1,3},{3,1},{4,6},{6,4},{5,7},{7,5},{8,10},{10,8},{9,1... | collective-permute-start | bytes 786440 | tf_op jit(solution)/shard_map/ppermute | solution.py:131
  42.4 27.7 %collective-permute-start.1 = (bf16[512,512]{1,0:T(8,128)(2,1)S(1)}, bf16[512,512]{1,0:T(8,128)(2,1)S(1)}, u32[]{:S(2)}, u32[]{:S(2)}) collective-permute-start(bf16[512,512]{1,0:T(8,128)(2,1)S(1)} %all_gather.6), channel_id=1, source_target_pairs={{0,4},{4,8},{8,12},{12,0},{1,5},{5,9},{9,13},{13,1},{2,6},{6,10},{... | collective-permute-start | bytes 1572872 | tf_op jit(solution)/shard_map/ppermute | solution.py:96
  44.7 30.8 %collective-permute-start.2 = (bf16[512,512]{1,0:T(8,128)(2,1)S(1)}, bf16[512,512]{1,0:T(8,128)(2,1)S(1)}, u32[]{:S(2)}, u32[]{:S(2)}) collective-permute-start(bf16[512,512]{1,0:T(8,128)(2,1)S(1)} %all_gather.6), channel_id=1, source_target_pairs={{0,8},{4,12},{8,0},{12,4},{1,9},{5,13},{9,1},{13,5},{2,10},{6,14},... | collective-permute-start | bytes 1572872 | tf_op jit(solution)/shard_map/ppermute | solution.py:96
  54.2 22.6 %collective-permute-start.3 = (bf16[512,512]{1,0:T(8,128)(2,1)S(1)}, bf16[512,512]{1,0:T(8,128)(2,1)S(1)}, u32[]{:S(2)}, u32[]{:S(2)}) collective-permute-start(bf16[512,512]{1,0:T(8,128)(2,1)S(1)} %all_gather.6), channel_id=1, source_target_pairs={{0,12},{4,0},{8,4},{12,8},{1,13},{5,1},{9,5},{13,9},{2,14},{6,2},{... | collective-permute-start | bytes 1572872 | tf_op jit(solution)/shard_map/ppermute | solution.py:96
  80.7 10.9 %copy-start.1 = (bf16[1,256,512]{2,1,0:T(8,128)(2,1)S(1)}, bf16[1,256,512]{2,1,0:T(8,128)(2,1)}, u32[]{:S(2)}) copy-start(bf16[1,256,512]{2,1,0:T(8,128)(2,1)} %param.7) | copy-start | bytes 786436
  80.7 11.0 %copy-start.3 = (bf16[512,512]{1,0:T(8,128)(2,1)S(1)}, bf16[512,512]{1,0:T(8,128)(2,1)}, u32[]{:S(2)}) copy-start(bf16[512,512]{1,0:T(8,128)(2,1)} %param.10) | copy-start | bytes 1572868
  91.7 0.7 copy-start.4
  93.2 40.2 %all-to-all-start = ((bf16[1,32,8,512]{3,2,0,1:T(8,128)(2,1)}), bf16[1,32,8,512]{3,2,0,1:T(8,128)(2,1)S(1)}, u32[]{:S(2)}, u32[]{:S(2)}) async-start(bf16[1,32,8,512]{3,2,0,1:T(8,128)(2,1)} %fusion.36), calls=%async_computation | async-start | bytes 524288 | tf_op jit(solution)/shard_map/all_to_all | solution.py:144
  138.7 24.2 %copy-start.2 = (bf16[512,512]{1,0:T(8,128)(2,1)S(1)}, bf16[512,512]{1,0:T(8,128)(2,1)}, u32[]{:S(2)}) copy-start(bf16[512,512]{1,0:T(8,128)(2,1)} %param.13) | copy-start | bytes 1572868

commit v2 on v1

--- a/solution.py
+++ b/solution.py
@@ -10,7 +10,6 @@
 from jax.sharding import PartitionSpec as P
 
 HEADS = 8
-PAIR = 2
 
 
 def layer_norm(rows, gain):
@@ -20,7 +19,7 @@
     return centred * lax.rsqrt(spread + 1e-05) * gain
 
 
-def _head_scores(q_ref, k_ref, cols, scale):
+def _scores(q_ref, k_ref, cols, scale):
     return (
         lax.dot_general(
             q_ref[:, cols], k_ref[:, cols], (((1,), (1,)), ((), ())),
@@ -31,64 +30,58 @@
 
 
 def partial_kernel(q_ref, k_ref, v_ref, o_ref, m_ref, l_ref, *, size, scale):
-    count = q_ref.shape[0]
-    for h in range(PAIR):
+    for h in range(HEADS):
         cols = slice(h * size, (h + 1) * size)
-        scores = _head_scores(q_ref, k_ref, cols, scale)
+        scores = _scores(q_ref, k_ref, cols, scale)
         peak = jnp.max(scores, axis=1, keepdims=True)
         weights = jnp.exp(scores - peak)
-        total = jnp.sum(weights, axis=1, keepdims=True)
+        l_ref[:, h : h + 1] = jnp.sum(weights, axis=1, keepdims=True)
+        m_ref[:, h : h + 1] = peak
         o_ref[:, cols] = jnp.dot(
             weights.astype(jnp.bfloat16), v_ref[:, cols], preferred_element_type=jnp.float32
         )
-        m_ref[:, cols] = jnp.broadcast_to(peak, (count, size))
-        l_ref[:, cols] = jnp.broadcast_to(total, (count, size))
 
 
-def final_kernel(q_ref, k_ref, v_ref, o1_ref, m1_ref, l1_ref, out_ref, *, size, scale):
-    for h in range(PAIR):
+def merge_kernel(q_ref, k_ref, v_ref, o1_ref, m1_ref, l1_ref, o_ref, m_ref, l_ref, *, size, scale):
+    for h in range(HEADS):
         cols = slice(h * size, (h + 1) * size)
-        first = slice(h * size, h * size + 1)
-        scores = _head_scores(q_ref, k_ref, cols, scale)
-        before = m1_ref[:, first]
+        scores = _scores(q_ref, k_ref, cols, scale)
+        before = m1_ref[:, h : h + 1]
         peak = jnp.maximum(before, jnp.max(scores, axis=1, keepdims=True))
         weights = jnp.exp(scores - peak)
         fade = jnp.exp(before - peak)
-        total = l1_ref[:, first] * fade + jnp.sum(weights, axis=1, keepdims=True)
-        summed = o1_ref[:, cols] * fade + jnp.dot(
+        l_ref[:, h : h + 1] = l1_ref[:, h : h + 1] * fade + jnp.sum(weights, axis=1, keepdims=True)
+        m_ref[:, h : h + 1] = peak
+        o_ref[:, cols] = o1_ref[:, cols] * fade + jnp.dot(
             weights.astype(jnp.bfloat16), v_ref[:, cols], preferred_element_type=jnp.float32
         )
-        out_ref[:, cols] = (summed / total).astype(out_ref.dtype)
 
 
-def _attention_call(kernel, query, keys, values, state, outs):
+def _attention_call(kernel, query, keys, values, state):
     count, width = query.shape
-    length = keys.shape[0]
     size = width // HEADS
-    block = PAIR * size
     body = lambda *refs: kernel(*refs, size=size, scale=1.0 / math.sqrt(size))
-    row_block = pl.BlockSpec((count, block), lambda h: (0, h))
-    key_block = pl.BlockSpec((length, block), lambda h: (0, h))
+    shapes = [
+        jax.ShapeDtypeStruct((count, width), jnp.float32),
+        jax.ShapeDtypeStruct((count, HEADS), jnp.float32),
+        jax.ShapeDtypeStruct((count, HEADS), jnp.float32),
+    ]
     return pl.pallas_call(
         body,
-        grid=(width // block,),
-        in_specs=[row_block, key_block, key_block] + [row_block] * len(state),
-        out_specs=[row_block] * len(outs),
-        out_shape=[jax.ShapeDtypeStruct((count, width), dtype) for dtype in outs],
+        out_shape=shapes,
         compiler_params=pltpu.CompilerParams(vmem_limit_bytes=48 * 1024 * 1024),
     )(query, keys, values, *state)
 
 
 def spatial_partial(query, keys, values):
-    return _attention_call(partial_kernel, query, keys, values, (), (jnp.float32,) * 3)
+    return _attention_call(partial_kernel, query, keys, values, ())
 
 
-def spatial_final(query, keys, values, state):
-    return _attention_call(final_kernel, query, keys, values, state, (jnp.bfloat16,))[0]
+def spatial_merge(query, keys, values, state):
+    return _attention_call(merge_kernel, query, keys, values, state)
 
 
 def spread_y(rows):
-    rows = lax.all_gather(rows, "core", axis=0, tiled=True)
     ring = lax.axis_size("y")
     pieces = [rows]
     for shift in range(1, ring):
@@ -129,13 +122,31 @@
         jnp.bfloat16
     )
     partner = lax.ppermute(normed, "zhi", [(0, 1), (1, 0)])
+    both = lax.all_gather(query, "core", axis=0, tiled=True)
     w_pairs = w_spatial[:, width:]
     near_rows = spread_y(normed)
     near = jnp.dot(near_rows, w_pairs, preferred_element_type=jnp.float32).astype(jnp.bfloat16)
-    state = spatial_partial(query, near[:, :width], near[:, width:])
+    state = spatial_partial(both, near[:, :width], near[:, width:])
     far_rows = spread_y(partner)
     far = jnp.dot(far_rows, w_pairs, preferred_element_type=jnp.float32).astype(jnp.bfloat16)
-    context = spatial_final(query, far[:, :width], far[:, width:], state)
+    summed, peak, total = spatial_merge(both, far[:, :width], far[:, width:], state)
+    mine = lax.axis_index("core")
+    other = 1 - mine
+    pick = lambda a, i: lax.dynamic_slice_in_dim(a, i * count, count, 0)
+    packed = jnp.concatenate([pick(peak, other), pick(total, other)], axis=1)
+    their_summed = lax.ppermute(pick(summed, other), "core", [(0, 1), (1, 0)])
+    their_packed = lax.ppermute(packed, "core", [(0, 1), (1, 0)])
+    own_peak, own_total, own_summed = pick(peak, mine), pick(total, mine), pick(summed, mine)
+    their_peak, their_total = their_packed[:, :HEADS], their_packed[:, HEADS:]
+    top = jnp.maximum(own_peak, their_peak)
+    own_fade, their_fade = jnp.exp(own_peak - top), jnp.exp(their_peak - top)
+    size = width // HEADS
+    merged = (
+        own_summed.reshape(count, HEADS, size) * own_fade[:, :, None]
+        + their_summed.reshape(count, HEADS, size) * their_fade[:, :, None]
+    )
+    denominator = own_total * own_fade + their_total * their_fade
+    context = (merged / denominator[:, :, None]).reshape(count, width).astype(jnp.bfloat16)
     after = resid + jnp.dot(context, w_spatial_out, preferred_element_type=jnp.float32)
     second = layer_norm(after, norm_temporal).astype(jnp.bfloat16)
     owners = lax.axis_size(("x", "zlo"))

time: 166 us -> 162 us (0.976)
  starting transfers between devices: 58.3 us -> 69.9 us
  blocking collectives: 36.2 us -> 27.4 us
  waiting for transfers between devices: 29.3 us -> 20.5 us
  Pallas kernels: 20.2 us -> 15.6 us
  local copies, waits for them, and re-layouts: 4.17 us -> 8.43 us
  matrix products: 10.6 us -> 13.4 us
    ppermute x0 -> x2, starting transfers between devices: none -> 11.8 us  [the longest x1 9.84 us: layer(): their_summed = lax.ppermute(pick(summed, other), 'core', [(0, 1), (1, 0)])]
    all_gather x2 -> x1, blocking collectives: 12.5 us -> 3.6 us  [layer(): both = lax.all_gather(query, 'core', axis=0, tiled=True)]
    ppermute x6, waiting for transfers between devices: 6.69 us -> 0.02 us  [spread_y(): pieces.append(lax.ppermute(rows, 'y', pairs))]
    pallas_call x2, Pallas kernels: 20.2 us -> 15.6 us  [_attention_call(): pl.pallas_call(body, out_shape=shapes, compiler_params=pltpu.CompilerPara...]
    ppermute x6, starting transfers between devices: 24.2 us -> 20 us  [spread_y(): pieces.append(lax.ppermute(rows, 'y', pairs))]
    ppermute x1, waiting for transfers between devices: 4.11 us -> 0.3 us  [layer(): partner = lax.ppermute(normed, 'zhi', [(0, 1), (1, 0)])]
    ppermute x1, starting transfers between devices: 12.4 us -> 15.4 us  [layer(): partner = lax.ppermute(normed, 'zhi', [(0, 1), (1, 0)])]
    mul x0 -> x4, local copies, waits for them, and re-layouts: none -> 2.11 us  [the longest x2 1.06 us: layer(): own_summed.reshape(count, HEADS, size) * own_fade[:, :, None]]
  transfers between devices with their start and end apart: 8 -> 10, of which waited for: 4 -> 3; matrix products, arithmetic and copies ran while one was open for 2% -> 6% of each run, Pallas kernels for 6% -> 4%
where the time goes in v2:
time: 162 us; the launch traced here: 161 us
  starting transfers between devices  69.9 us (43%)
  blocking collectives  27.4 us (17%)
  waiting for transfers between devices  20.5 us (13%)
  Pallas kernels  15.6 us (10%)
  matrix products  13.4 us (8%)
  local copies, waits for them, and re-layouts  8.43 us (5%)
  other arithmetic  5.68 us (4%)
    all_to_all x1, blocking collectives, layer(): lax.all_to_all(context_t, ('x', 'zlo'), split_axis=0, concat_axis=1, tile...  23.8 us
    all_to_all x1, starting transfers between devices, layer(): lax.all_to_all(second, ('x', 'zlo'), split_axis=1, concat_axis=0, tiled=T...  22.6 us
    ppermute x6, starting transfers between devices, spread_y(): pieces.append(lax.ppermute(rows, 'y', pairs))  20 us
    all_to_all x1, waiting for transfers between devices, layer(): lax.all_to_all(second, ('x', 'zlo'), split_axis=1, concat_axis=0, tiled=T...  18.9 us
    pallas_call x2, Pallas kernels, _attention_call(): pl.pallas_call(body, out_shape=shapes, compiler_params=pltpu.CompilerPara...  15.6 us
    ppermute x1, starting transfers between devices, layer(): partner = lax.ppermute(normed, 'zhi', [(0, 1), (1, 0)])  15.4 us
    ppermute x1, starting transfers between devices, layer(): their_summed = lax.ppermute(pick(summed, other), 'core', [(0, 1), (1, 0)])  9.84 us
    all_gather x1, blocking collectives, layer(): both = lax.all_gather(query, 'core', axis=0, tiled=True)  3.6 us
  transfers between devices with their start and end apart: 10, of which 3 were waited for; matrix products, arithmetic and copies ran while one was open for 6% of the time, Pallas kernels for 4%

profile of v2, /device:TPU:1, one launch (start us, length us, event | category | flops | bytes accessed | tf_op | source)
XLA Modules:
  0.0 161.3 jit_solution(10249508850799565517)
XLA Ops:
  0.0 0.0 copy-start
  0.0 1.2 convert_reduce_fusion
  1.2 1.2 fusion.27
  2.4 1.1 fusion.29
  3.5 4.0 %collective-permute-start.4 = (bf16[256,512]{1,0:T(8,128)(2,1)S(1)}, bf16[256,512]{1,0:T(8,128)(2,1)}, u32[]{:S(2)}, u32[]{:S(2)}) collective-permute-start(bf16[256,512]{1,0:T(8,128)(2,1)S(1)} %fusion.29), channel_id=1, source_target_pairs={{0,4},{4,8},{8,12},{12,0},{1,5},{5,9},{9,13},{13,1},{2,6},{6,10},{... | collective-permute-start | bytes 786440 | tf_op jit(solution)/shard_map/ppermute | solution.py:89
  7.6 4.5 %collective-permute-start.5 = (bf16[256,512]{1,0:T(8,128)(2,1)S(1)}, bf16[256,512]{1,0:T(8,128)(2,1)}, u32[]{:S(2)}, u32[]{:S(2)}) collective-permute-start(bf16[256,512]{1,0:T(8,128)(2,1)S(1)} %fusion.29), channel_id=1, source_target_pairs={{0,8},{4,12},{8,0},{12,4},{1,9},{5,13},{9,1},{13,5},{2,10},{6,14},... | collective-permute-start | bytes 786440 | tf_op jit(solution)/shard_map/ppermute | solution.py:89
  12.1 3.0 %collective-permute-start.6 = (bf16[256,512]{1,0:T(8,128)(2,1)S(1)}, bf16[256,512]{1,0:T(8,128)(2,1)}, u32[]{:S(2)}, u32[]{:S(2)}) collective-permute-start(bf16[256,512]{1,0:T(8,128)(2,1)S(1)} %fusion.29), channel_id=1, source_target_pairs={{0,12},{4,0},{8,4},{12,8},{1,13},{5,1},{9,5},{13,9},{2,14},{6,2},{... | collective-permute-start | bytes 786440 | tf_op jit(solution)/shard_map/ppermute | solution.py:89
  15.1 15.4 %collective-permute-start = (bf16[256,512]{1,0:T(8,128)(2,1)S(1)}, bf16[256,512]{1,0:T(8,128)(2,1)}, u32[]{:S(2)}, u32[]{:S(2)}) collective-permute-start(bf16[256,512]{1,0:T(8,128)(2,1)S(1)} %fusion.29), channel_id=1, source_target_pairs={{0,2},{2,0},{1,3},{3,1},{4,6},{6,4},{5,7},{7,5},{8,10},{10,8},{9,1... | collective-permute-start | bytes 786440 | tf_op jit(solution)/shard_map/ppermute | solution.py:124
  30.5 1.3 convolution_convert_fusion.3
  31.9 3.6 %all_gather.3.refs_0_ = bf16[512,512]{1,0:T(8,128)(2,1)S(1)} all-gather(bf16[256,512]{1,0:T(8,128)(2,1)S(1)} %convolution_convert_fusion.3), channel_id=1, replica_groups=mesh['x'=4,'zlo'=8,'y'=4,'zhi'=2,'core'=2] {'core'}, dimensions={0}, use_global_device_ids=true | all-gather | bytes 786432 | tf_op jit(solution)/shard_map/all_gather | solution.py:125
  35.5 0.3 collective-permute-done
  35.8 2.3 %collective-permute-start.1 = (bf16[256,512]{1,0:T(8,128)(2,1)}, bf16[256,512]{1,0:T(8,128)(2,1)S(1)}, u32[]{:S(2)}, u32[]{:S(2)}) collective-permute-start(bf16[256,512]{1,0:T(8,128)(2,1)} %collective-permute-done), channel_id=1, source_target_pairs={{0,4},{4,8},{8,12},{12,0},{1,5},{5,9},{9,13},{13,1},{2,6},{6,10},{... | collective-permute-start | bytes 786440 | tf_op jit(solution)/shard_map/ppermute | solution.py:89
  38.1 2.5 %collective-permute-start.2 = (bf16[256,512]{1,0:T(8,128)(2,1)}, bf16[256,512]{1,0:T(8,128)(2,1)S(1)}, u32[]{:S(2)}, u32[]{:S(2)}) collective-permute-start(bf16[256,512]{1,0:T(8,128)(2,1)} %collective-permute-done), channel_id=1, source_target_pairs={{0,8},{4,12},{8,0},{12,4},{1,9},{5,13},{9,1},{13,5},{2,10},{6,14},... | collective-permute-start | bytes 786440 | tf_op jit(solution)/shard_map/ppermute | solution.py:89
  40.6 0.0 collective-permute-done.4
  40.6 3.8 %collective-permute-start.3 = (bf16[256,512]{1,0:T(8,128)(2,1)}, bf16[256,512]{1,0:T(8,128)(2,1)S(1)}, u32[]{:S(2)}, u32[]{:S(2)}) collective-permute-start(bf16[256,512]{1,0:T(8,128)(2,1)} %collective-permute-done), channel_id=1, source_target_pairs={{0,12},{4,0},{8,4},{12,8},{1,13},{5,1},{9,5},{13,9},{2,14},{6,2},{... | collective-permute-start | bytes 786440 | tf_op jit(solution)/shard_map/ppermute | solution.py:89
  44.4 0.0 collective-permute-done.5
  44.4 0.0 collective-permute-done.6
  44.4 0.0 copy-done.3
  44.4 2.4 %convolution_convert_fusion.1 = bf16[1024,1024]{1,0:T(8,128)(2,1)S(1)} fusion(bf16[256,512]{1,0:T(8,128)(2,1)} %collective-permute-done.6, bf16[256,512]{1,0:T(8,128)(2,1)} %collective-permute-done.5, bf16[256,512]{1,0:T(8,128)(2,1)} %collective-permute-done.4, bf16[256,512]{1,0:T(8,128)(2,1)S(1)} %fusion.29, bf16[512,1536]{1,0:T(8,128)(2,1)S(1)} %copy-done.3), kind=kOutput, calls=%fused_computation.2 | convolution fusion | flops 1078984704 | bytes 4194304 | tf_op jit(solution)/shard_map/dot_general | solution.py:128
  46.7 0.2 fusion.47
  46.9 6.4 %shard_map.73 = (f32[512,512]{1,0:T(8,128)S(1)}, f32[512,8]{1,0:T(8,128)S(1)}, f32[512,8]{1,0:T(8,128)S(1)}) custom-call(bf16[512,512]{1,0:T(8,128)(2,1)S(1)} %all_gather.3.refs_0_, bf16[1024,512]{1,0:T(8,128)(2,1)S(1)} %get-tuple-element.21.refs_1_, bf16[1024,512]{1,0:T(8,128)(2,1)S(1)} %get-tuple-element.20.refs_2_), custom_call_target="tpu_custom_call" | custom-call | tf_op jit(solution)/shard_map/pallas_call | solution.py:69
  53.3 0.0 collective-permute-done.1
  53.3 0.0 collective-permute-done.2
  53.3 0.0 collective-permute-done.3
  53.3 2.2 %convolution_convert_fusion.2 = bf16[1024,1024]{1,0:T(8,128)(2,1)S(1)} fusion(bf16[256,512]{1,0:T(8,128)(2,1)S(1)} %collective-permute-done.3, bf16[256,512]{1,0:T(8,128)(2,1)S(1)} %collective-permute-done.2, bf16[256,512]{1,0:T(8,128)(2,1)S(1)} %collective-permute-done.1, bf16[256,512]{1,0:T(8,128)(2,1)} %collective-permute-done, ...), kind=kOutput, calls=%fused_computation.3 | convolution fusion | flops 1078984704 | bytes 4194304 | tf_op jit(solution)/shard_map/dot_general | solution.py:131
  55.5 0.2 fusion.48
  55.7 9.2 %shard_map.74 = (f32[512,512]{1,0:T(8,128)S(1)}, f32[512,8]{1,0:T(8,128)S(1)}, f32[512,8]{1,0:T(8,128)S(1)}) custom-call(bf16[512,512]{1,0:T(8,128)(2,1)S(1)} %all_gather.3.refs_0_, bf16[1024,512]{1,0:T(8,128)(2,1)S(1)} %get-tuple-element.23.refs_1_, bf16[1024,512]{1,0:T(8,128)(2,1)S(1)} %get-tuple-element.22.refs_2_, ...), custom_call_target="tpu_custom_call" | custom-call | tf_op jit(solution)/shard_map/pallas_call | solution.py:69
  64.9 0.8 constant_dynamic-slice_fusion
  65.7 9.8 %collective-permute-start.8 = (f32[256,512]{1,0:T(8,128)}, f32[256,512]{1,0:T(8,128)}, u32[]{:S(2)}, u32[]{:S(2)}) collective-permute-start(f32[256,512]{1,0:T(8,128)} %constant_dynamic-slice_fusion), channel_id=1, source_target_pairs={{0,1},{1,0},{2,3},{3,2},{4,5},{5,4},{6,7},{7,6},{8,9},{9,8},{10,11... | collective-permute-start | bytes 1572872 | tf_op jit(solution)/shard_map/ppermute | solution.py:137
  75.6 0.1 pad_maximum_fusion
  75.7 1.9 %collective-permute-start.7 = (f32[256,16]{1,0:T(8,128)S(1)}, f32[256,16]{1,0:T(8,128)S(1)}, u32[]{:S(2)}, u32[]{:S(2)}) collective-permute-start(f32[256,16]{1,0:T(8,128)S(1)} %pad_maximum_fusion), channel_id=1, source_target_pairs={{0,1},{1,0},{2,3},{3,2},{4,5},{5,4},{6,7},{7,6},{8,9},{9,8},{10,11... | collective-permute-start | bytes 49160 | tf_op jit(solution)/shard_map/ppermute | solution.py:138
  77.7 1.3 collective-permute-done.7
  79.0 0.7 fusion.41
  79.7 0.1 copy.49
  79.7 0.1 mul.89
  79.8 0.0 copy-start.1
  79.8 1.0 copy.50
  80.8 1.0 copy.51
  81.8 1.0 copy.52
  82.8 0.1 copy.53
  82.9 0.1 div.33
  82.9 1.0 copy.54
  83.9 0.0 copy-start.2
  83.9 0.0 collective-permute-done.8
  83.9 0.0 copy-done.1
  84.0 2.1 %fusion.50 = (f32[256]{0:T(256)S(1)}, f32[256,512]{1,0:T(8,128)S(1)}) fusion(bf16[512,512]{1,0:T(8,128)(2,1)} %param.10, f32[256,512]{1,0:T(8,128)} %copy.54, f32[256,512]{1,0:T(8,128)} %collective-permute-done.8, f32[256,512]{1,0:T(8,128)} %copy.52, f32[256,512]{1,0:T(8,128)} %copy.50, f32[512,512]{1,0:T(8,128)S(1)} %get-tuple-element.14, ...), kind=kOutput, calls=%fused_computation.73 | convolution fusion | flops 135266048 | bytes 3933188 | tf_op jit(solution)/shard_map/dot_general | solution.py:150
  86.1 0.2 multiply_reduce_fusion
  86.3 0.0 copy-done.2
  86.3 0.9 fusion.36
  87.1 22.6 %all-to-all-start = ((bf16[1,32,8,512]{3,2,0,1:T(8,128)(2,1)}), bf16[1,32,8,512]{3,2,0,1:T(8,128)(2,1)S(1)}, u32[]{:S(2)}, u32[]{:S(2)}) async-start(bf16[1,32,8,512]{3,2,0,1:T(8,128)(2,1)} %fusion.36), calls=%async_computation | async-start | bytes 524288 | tf_op jit(solution)/shard_map/all_to_all | solution.py:155
  109.8 18.9 %all-to-all-done = bf16[1,32,8,512]{3,2,0,1:T(8,128)(2,1)S(1)} async-done(((bf16[1,32,8,512]{3,2,0,1:T(8,128)(2,1)}), bf16[1,32,8,512]{3,2,0,1:T(8,128)(2,1)S(1)}, u32[]{:S(2)}, u32[]{:S(2)}) %all-to-all-start) | async-done | bytes 262176 | tf_op jit(solution)/shard_map/all_to_all | solution.py:155
  128.7 0.0 copy-done
  128.7 0.6 fusion
  129.3 0.1 fusion.49
  129.4 1.1 reshape.87
  130.4 1.1 reshape.88
  131.5 0.3 reshape.86
  131.8 2.1 %fusion.51 = (f32[8,8,32]{2,1,0:T(8,128)S(1)}, f32[8,8,32,32]{2,3,1,0:T(8,128)S(1)}) fusion(bf16[32,8,8,64]{3,2,1,0:T(8,128)(2,1)} %reshape.88, bf16[32,8,8,64]{3,2,1,0:T(8,128)(2,1)} %reshape.87, pred[32,32]{0,1:T(8,128)(4,1)S(1)} %iota_compare_fusion), kind=kOutput, calls=%fused_computation.74 | convolution fusion | flops 8583168 | bytes 795648 | tf_op jit(solution)/shard_map/fche,gche->chfg/dot_general | solution.py:101
  133.9 0.3 fusion.20
  134.2 0.8 fusion.3
  134.9 0.2 copy.60
  135.1 0.3 convert_element_type.60
  135.4 23.8 %all_to_all.8 = bf16[32,1,8,512]{3,2,1,0:T(8,128)(2,1)S(1)} all-to-all(bf16[32,1,8,512]{3,2,1,0:T(8,128)(2,1)S(1)} %bitcast.50), channel_id=1, replica_groups=mesh['x'=4,'zlo'=8,'y'=4,'zhi'=2,'core'=2] {'x','zlo'}, dimensions={0} | all-to-all | bytes 524288 | tf_op jit(solution)/shard_map/all_to_all | solution.py:162
  159.2 2.0 %fusion.5 = bf16[1,256,512]{2,1,0:T(8,128)(2,1)} fusion(f32[256,512]{1,0:T(8,128)S(1)} %get-tuple-element.28, bf16[512,512]{1,0:T(8,128)(2,1)} %param.13, bf16[32,1,8,512]{3,2,1,0:T(8,128)(2,1)S(1)} %all_to_all.8), kind=kOutput, calls=%fused_computation.13 | convolution fusion | flops 134479872 | bytes 1572864 | tf_op jit(solution)/shard_map/dot_general | solution.py:163
  (8 shorter events, 0.1 us)
Async XLA Ops:
  0.0 128.7 %copy-start = (bf16[512,1536]{1,0:T(8,128)(2,1)S(1)}, bf16[512,1536]{1,0:T(8,128)(2,1)}, u32[]{:S(2)}) copy-start(bf16[512,1536]{1,0:T(8,128)(2,1)} %param.12) | copy-start | bytes 4718596
  0.0 44.4 %copy-start.3 = (bf16[512,1536]{1,0:T(8,128)(2,1)S(1)}, bf16[512,1536]{1,0:T(8,128)(2,1)}, u32[]{:S(2)}) copy-start(bf16[512,1536]{1,0:T(8,128)(2,1)} %param.9) | copy-start | bytes 4718596
  3.5 37.0 %collective-permute-start.4 = (bf16[256,512]{1,0:T(8,128)(2,1)S(1)}, bf16[256,512]{1,0:T(8,128)(2,1)}, u32[]{:S(2)}, u32[]{:S(2)}) collective-permute-start(bf16[256,512]{1,0:T(8,128)(2,1)S(1)} %fusion.29), channel_id=1, source_target_pairs={{0,4},{4,8},{8,12},{12,0},{1,5},{5,9},{9,13},{13,1},{2,6},{6,10},{... | collective-permute-start | bytes 786440 | tf_op jit(solution)/shard_map/ppermute | solution.py:89
  7.6 36.8 %collective-permute-start.5 = (bf16[256,512]{1,0:T(8,128)(2,1)S(1)}, bf16[256,512]{1,0:T(8,128)(2,1)}, u32[]{:S(2)}, u32[]{:S(2)}) collective-permute-start(bf16[256,512]{1,0:T(8,128)(2,1)S(1)} %fusion.29), channel_id=1, source_target_pairs={{0,8},{4,12},{8,0},{12,4},{1,9},{5,13},{9,1},{13,5},{2,10},{6,14},... | collective-permute-start | bytes 786440 | tf_op jit(solution)/shard_map/ppermute | solution.py:89
  12.1 32.3 %collective-permute-start.6 = (bf16[256,512]{1,0:T(8,128)(2,1)S(1)}, bf16[256,512]{1,0:T(8,128)(2,1)}, u32[]{:S(2)}, u32[]{:S(2)}) collective-permute-start(bf16[256,512]{1,0:T(8,128)(2,1)S(1)} %fusion.29), channel_id=1, source_target_pairs={{0,12},{4,0},{8,4},{12,8},{1,13},{5,1},{9,5},{13,9},{2,14},{6,2},{... | collective-permute-start | bytes 786440 | tf_op jit(solution)/shard_map/ppermute | solution.py:89
  15.1 20.7 %collective-permute-start = (bf16[256,512]{1,0:T(8,128)(2,1)S(1)}, bf16[256,512]{1,0:T(8,128)(2,1)}, u32[]{:S(2)}, u32[]{:S(2)}) collective-permute-start(bf16[256,512]{1,0:T(8,128)(2,1)S(1)} %fusion.29), channel_id=1, source_target_pairs={{0,2},{2,0},{1,3},{3,1},{4,6},{6,4},{5,7},{7,5},{8,10},{10,8},{9,1... | collective-permute-start | bytes 786440 | tf_op jit(solution)/shard_map/ppermute | solution.py:124
  35.8 17.5 %collective-permute-start.1 = (bf16[256,512]{1,0:T(8,128)(2,1)}, bf16[256,512]{1,0:T(8,128)(2,1)S(1)}, u32[]{:S(2)}, u32[]{:S(2)}) collective-permute-start(bf16[256,512]{1,0:T(8,128)(2,1)} %collective-permute-done), channel_id=1, source_target_pairs={{0,4},{4,8},{8,12},{12,0},{1,5},{5,9},{9,13},{13,1},{2,6},{6,10},{... | collective-permute-start | bytes 786440 | tf_op jit(solution)/shard_map/ppermute | solution.py:89
  38.1 15.2 %collective-permute-start.2 = (bf16[256,512]{1,0:T(8,128)(2,1)}, bf16[256,512]{1,0:T(8,128)(2,1)S(1)}, u32[]{:S(2)}, u32[]{:S(2)}) collective-permute-start(bf16[256,512]{1,0:T(8,128)(2,1)} %collective-permute-done), channel_id=1, source_target_pairs={{0,8},{4,12},{8,0},{12,4},{1,9},{5,13},{9,1},{13,5},{2,10},{6,14},... | collective-permute-start | bytes 786440 | tf_op jit(solution)/shard_map/ppermute | solution.py:89
  40.6 12.7 %collective-permute-start.3 = (bf16[256,512]{1,0:T(8,128)(2,1)}, bf16[256,512]{1,0:T(8,128)(2,1)S(1)}, u32[]{:S(2)}, u32[]{:S(2)}) collective-permute-start(bf16[256,512]{1,0:T(8,128)(2,1)} %collective-permute-done), channel_id=1, source_target_pairs={{0,12},{4,0},{8,4},{12,8},{1,13},{5,1},{9,5},{13,9},{2,14},{6,2},{... | collective-permute-start | bytes 786440 | tf_op jit(solution)/shard_map/ppermute | solution.py:89
  65.7 18.2 %collective-permute-start.8 = (f32[256,512]{1,0:T(8,128)}, f32[256,512]{1,0:T(8,128)}, u32[]{:S(2)}, u32[]{:S(2)}) collective-permute-start(f32[256,512]{1,0:T(8,128)} %constant_dynamic-slice_fusion), channel_id=1, source_target_pairs={{0,1},{1,0},{2,3},{3,2},{4,5},{5,4},{6,7},{7,6},{8,9},{9,8},{10,11... | collective-permute-start | bytes 1572872 | tf_op jit(solution)/shard_map/ppermute | solution.py:137
  75.7 3.2 %collective-permute-start.7 = (f32[256,16]{1,0:T(8,128)S(1)}, f32[256,16]{1,0:T(8,128)S(1)}, u32[]{:S(2)}, u32[]{:S(2)}) collective-permute-start(f32[256,16]{1,0:T(8,128)S(1)} %pad_maximum_fusion), channel_id=1, source_target_pairs={{0,1},{1,0},{2,3},{3,2},{4,5},{5,4},{6,7},{7,6},{8,9},{9,8},{10,11... | collective-permute-start | bytes 49160 | tf_op jit(solution)/shard_map/ppermute | solution.py:138
  79.8 4.2 %copy-start.1 = (bf16[1,256,512]{2,1,0:T(8,128)(2,1)S(1)}, bf16[1,256,512]{2,1,0:T(8,128)(2,1)}, u32[]{:S(2)}) copy-start(bf16[1,256,512]{2,1,0:T(8,128)(2,1)} %param.7) | copy-start | bytes 786436
  83.9 2.3 %copy-start.2 = (f32[512]{0:T(512)S(1)}, f32[512]{0:T(512)}, u32[]{:S(2)}) copy-start(f32[512]{0:T(512)} %param.11) | copy-start | bytes 6148
  87.1 41.6 %all-to-all-start = ((bf16[1,32,8,512]{3,2,0,1:T(8,128)(2,1)}), bf16[1,32,8,512]{3,2,0,1:T(8,128)(2,1)S(1)}, u32[]{:S(2)}, u32[]{:S(2)}) async-start(bf16[1,32,8,512]{3,2,0,1:T(8,128)(2,1)} %fusion.36), calls=%async_computation | async-start | bytes 524288 | tf_op jit(solution)/shard_map/all_to_all | solution.py:155

commit v3 on v2

--- a/solution.py
+++ b/solution.py
@@ -20,12 +20,10 @@
 
 
 def _scores(q_ref, k_ref, cols, scale):
-    return (
-        lax.dot_general(
-            q_ref[:, cols], k_ref[:, cols], (((1,), (1,)), ((), ())),
-            preferred_element_type=jnp.float32,
-        )
-        * scale
+    del scale
+    return lax.dot_general(
+        q_ref[:, cols], k_ref[:, cols], (((1,), (1,)), ((), ())),
+        preferred_element_type=jnp.float32,
     )
 
 
@@ -73,6 +71,25 @@
     )(query, keys, values, *state)
 
 
+def combine_kernel(o1_ref, s1_ref, o2_ref, s2_ref, out_ref, *, size):
+    for h in range(HEADS):
+        cols = slice(h * size, (h + 1) * size)
+        m1, l1 = s1_ref[:, h : h + 1], s1_ref[:, HEADS + h : HEADS + h + 1]
+        m2, l2 = s2_ref[:, h : h + 1], s2_ref[:, HEADS + h : HEADS + h + 1]
+        top = jnp.maximum(m1, m2)
+        f1, f2 = jnp.exp(m1 - top), jnp.exp(m2 - top)
+        summed = o1_ref[:, cols] * f1 + o2_ref[:, cols] * f2
+        out_ref[:, cols] = (summed / (l1 * f1 + l2 * f2)).astype(out_ref.dtype)
+
+
+def combine(own_summed, own_stats, their_summed, their_stats):
+    count, width = own_summed.shape
+    body = lambda *refs: combine_kernel(*refs, size=width // HEADS)
+    return pl.pallas_call(body, out_shape=jax.ShapeDtypeStruct((count, width), jnp.bfloat16))(
+        own_summed, own_stats, their_summed, their_stats
+    )
+
+
 def spatial_partial(query, keys, values):
     return _attention_call(partial_kernel, query, keys, values, ())
 
@@ -98,7 +115,8 @@
     query = block_qkv[:, :, :width].reshape(frames, cells, HEADS, size)
     keys = block_qkv[:, :, width : 2 * width].reshape(frames, cells, HEADS, size)
     values = block_qkv[:, :, 2 * width :].reshape(frames, cells, HEADS, size)
-    scores = jnp.einsum("fche,gche->chfg", query, keys, preferred_element_type=jnp.float32) * scale
+    del scale
+    scores = jnp.einsum("fche,gche->chfg", query, keys, preferred_element_type=jnp.float32)
     later = jnp.arange(frames)[:, None] >= jnp.arange(frames)[None, :]
     scores = jnp.where(later, scores, -1e30)
     peak = jnp.max(scores, axis=3, keepdims=True)
@@ -118,9 +136,8 @@
     count = frames_here * rows
     resid = tokens.reshape(count, width).astype(jnp.float32)
     normed = layer_norm(resid, norm_spatial).astype(jnp.bfloat16)
-    query = jnp.dot(normed, w_spatial[:, :width], preferred_element_type=jnp.float32).astype(
-        jnp.bfloat16
-    )
+    w_query = w_spatial[:, :width] * jnp.asarray(1.0 / math.sqrt(width // HEADS), w_spatial.dtype)
+    query = jnp.dot(normed, w_query, preferred_element_type=jnp.float32).astype(jnp.bfloat16)
     partner = lax.ppermute(normed, "zhi", [(0, 1), (1, 0)])
     both = lax.all_gather(query, "core", axis=0, tiled=True)
     w_pairs = w_spatial[:, width:]
@@ -133,20 +150,10 @@
     mine = lax.axis_index("core")
     other = 1 - mine
     pick = lambda a, i: lax.dynamic_slice_in_dim(a, i * count, count, 0)
-    packed = jnp.concatenate([pick(peak, other), pick(total, other)], axis=1)
+    stats = jnp.concatenate([peak, total], axis=1)
     their_summed = lax.ppermute(pick(summed, other), "core", [(0, 1), (1, 0)])
-    their_packed = lax.ppermute(packed, "core", [(0, 1), (1, 0)])
-    own_peak, own_total, own_summed = pick(peak, mine), pick(total, mine), pick(summed, mine)
-    their_peak, their_total = their_packed[:, :HEADS], their_packed[:, HEADS:]
-    top = jnp.maximum(own_peak, their_peak)
-    own_fade, their_fade = jnp.exp(own_peak - top), jnp.exp(their_peak - top)
-    size = width // HEADS
-    merged = (
-        own_summed.reshape(count, HEADS, size) * own_fade[:, :, None]
-        + their_summed.reshape(count, HEADS, size) * their_fade[:, :, None]
-    )
-    denominator = own_total * own_fade + their_total * their_fade
-    context = (merged / denominator[:, :, None]).reshape(count, width).astype(jnp.bfloat16)
+    their_stats = lax.ppermute(pick(stats, other), "core", [(0, 1), (1, 0)])
+    context = combine(pick(summed, mine), pick(stats, mine), their_summed, their_stats)
     after = resid + jnp.dot(context, w_spatial_out, preferred_element_type=jnp.float32)
     second = layer_norm(after, norm_temporal).astype(jnp.bfloat16)
     owners = lax.axis_size(("x", "zlo"))
@@ -154,6 +161,9 @@
     second = second.reshape(frames_here, owners, share, width)
     gathered = lax.all_to_all(second, ("x", "zlo"), split_axis=1, concat_axis=0, tiled=True)
     frames_all = gathered.shape[0]
+    w_temporal = w_temporal.at[:, :width].multiply(
+        jnp.asarray(1.0 / math.sqrt(width // HEADS), w_temporal.dtype)
+    )
     qkv_t = jnp.dot(
         gathered.reshape(frames_all * share, width), w_temporal, preferred_element_type=jnp.float32
     ).astype(jnp.bfloat16)

time: 162 us -> 155 us (0.957)
  matrix products: 13.4 us -> 9.98 us
  Pallas kernels: 15.6 us -> 18.8 us
  other arithmetic: 5.68 us -> 3.31 us
  waiting for transfers between devices: 20.5 us -> 18.2 us
    pallas_call x0 -> x1, Pallas kernels: none -> 3.75 us  [combine(): pl.pallas_call(body, out_shape=jax.ShapeDtypeStruct((count, width), jnp.b...]
    unnamed x8 -> x26, local copies, waits for them, and re-layouts: 0.02 us -> 3.41 us
    mul x4 -> x0, local copies, waits for them, and re-layouts: 2.11 us -> none  [the longest x2 1.06 us: layer(): own_summed.reshape(count, HEADS, size) * own_fade[:, :, None]]
  transfers between devices with their start and end apart: 10 -> 10, of which waited for: 3 -> 3; matrix products, arithmetic and copies ran while one was open for 6% -> 4% of each run, Pallas kernels for 4% -> 4%
where the time goes in v3:
time: 155 us; the launch traced here: 154 us
  starting transfers between devices  68.9 us (44%)
  blocking collectives  27.4 us (18%)
  Pallas kernels  18.8 us (12%)
  waiting for transfers between devices  18.2 us (12%)
  matrix products  9.98 us (6%)
  local copies, waits for them, and re-layouts  7.01 us (5%)
  other arithmetic  3.31 us (2%)
    all_to_all x1, blocking collectives, layer(): lax.all_to_all(context_t, ('x', 'zlo'), split_axis=0, concat_axis=1, tile...  23.8 us
    all_to_all x1, starting transfers between devices, layer(): lax.all_to_all(second, ('x', 'zlo'), split_axis=1, concat_axis=0, tiled=T...  21.6 us
    ppermute x6, starting transfers between devices, spread_y(): pieces.append(lax.ppermute(rows, 'y', pairs))  20 us
    all_to_all x1, waiting for transfers between devices, layer(): lax.all_to_all(second, ('x', 'zlo'), split_axis=1, concat_axis=0, tiled=T...  17.4 us
    ppermute x1, starting transfers between devices, layer(): partner = lax.ppermute(normed, 'zhi', [(0, 1), (1, 0)])  15.4 us
    pallas_call x2, Pallas kernels, _attention_call(): pl.pallas_call(body, out_shape=shapes, compiler_params=pltpu.CompilerPara...  15 us
    ppermute x1, starting transfers between devices, layer(): their_summed = lax.ppermute(pick(summed, other), 'core', [(0, 1), (1, 0)])  9.85 us
    pallas_call x1, Pallas kernels, combine(): pl.pallas_call(body, out_shape=jax.ShapeDtypeStruct((count, width), jnp.b...  3.75 us
  transfers between devices with their start and end apart: 10, of which 3 were waited for; matrix products, arithmetic and copies ran while one was open for 4% of the time, Pallas kernels for 4%

profile of v3, /device:TPU:1, one launch (start us, length us, event | category | flops | bytes accessed | tf_op | source)
XLA Modules:
  0.0 153.9 jit_solution(3051759764049117005)
XLA Ops:
  0.0 1.0 copy-done.2
  1.0 0.1 convert_reduce_fusion
  1.1 0.2 fusion.26
  1.4 0.1 fusion.28
  1.5 4.0 %collective-permute-start.4 = (bf16[256,512]{1,0:T(8,128)(2,1)S(1)}, bf16[256,512]{1,0:T(8,128)(2,1)S(1)}, u32[]{:S(2)}, u32[]{:S(2)}) collective-permute-start(bf16[256,512]{1,0:T(8,128)(2,1)S(1)} %fusion.28), channel_id=1, source_target_pairs={{0,4},{4,8},{8,12},{12,0},{1,5},{5,9},{9,13},{13,1},{2,6},{6,10},{... | collective-permute-start | bytes 786440 | tf_op jit(solution)/shard_map/ppermute | solution.py:106
  5.6 4.5 %collective-permute-start.5 = (bf16[256,512]{1,0:T(8,128)(2,1)S(1)}, bf16[256,512]{1,0:T(8,128)(2,1)S(1)}, u32[]{:S(2)}, u32[]{:S(2)}) collective-permute-start(bf16[256,512]{1,0:T(8,128)(2,1)S(1)} %fusion.28), channel_id=1, source_target_pairs={{0,8},{4,12},{8,0},{12,4},{1,9},{5,13},{9,1},{13,5},{2,10},{6,14},... | collective-permute-start | bytes 786440 | tf_op jit(solution)/shard_map/ppermute | solution.py:106
  10.1 3.0 %collective-permute-start.6 = (bf16[256,512]{1,0:T(8,128)(2,1)S(1)}, bf16[256,512]{1,0:T(8,128)(2,1)}, u32[]{:S(2)}, u32[]{:S(2)}) collective-permute-start(bf16[256,512]{1,0:T(8,128)(2,1)S(1)} %fusion.28), channel_id=1, source_target_pairs={{0,12},{4,0},{8,4},{12,8},{1,13},{5,1},{9,5},{13,9},{2,14},{6,2},{... | collective-permute-start | bytes 786440 | tf_op jit(solution)/shard_map/ppermute | solution.py:106
  13.1 15.4 %collective-permute-start = (bf16[256,512]{1,0:T(8,128)(2,1)S(1)}, bf16[256,512]{1,0:T(8,128)(2,1)S(1)}, u32[]{:S(2)}, u32[]{:S(2)}) collective-permute-start(bf16[256,512]{1,0:T(8,128)(2,1)S(1)} %fusion.28), channel_id=1, source_target_pairs={{0,2},{2,0},{1,3},{3,1},{4,6},{6,4},{5,7},{7,5},{8,10},{10,8},{9,1... | collective-permute-start | bytes 786440 | tf_op jit(solution)/shard_map/ppermute | solution.py:141
  28.5 1.3 convolution_convert_fusion.3
  29.9 3.6 %all_gather.3.refs_0_ = bf16[512,512]{1,0:T(8,128)(2,1)S(1)} all-gather(bf16[256,512]{1,0:T(8,128)(2,1)S(1)} %convolution_convert_fusion.3), channel_id=1, replica_groups=mesh['x'=4,'zlo'=8,'y'=4,'zhi'=2,'core'=2] {'core'}, dimensions={0}, use_global_device_ids=true | all-gather | bytes 786432 | tf_op jit(solution)/shard_map/all_gather | solution.py:142
  33.5 0.2 collective-permute-done
  33.7 2.3 %collective-permute-start.1 = (bf16[256,512]{1,0:T(8,128)(2,1)S(1)}, bf16[256,512]{1,0:T(8,128)(2,1)S(1)}, u32[]{:S(2)}, u32[]{:S(2)}) collective-permute-start(bf16[256,512]{1,0:T(8,128)(2,1)S(1)} %collective-permute-done), channel_id=1, source_target_pairs={{0,4},{4,8},{8,12},{12,0},{1,5},{5,9},{9,13},{13,1},{2,6},{6,10},{... | collective-permute-start | bytes 786440 | tf_op jit(solution)/shard_map/ppermute | solution.py:106
  36.0 2.5 %collective-permute-start.2 = (bf16[256,512]{1,0:T(8,128)(2,1)S(1)}, bf16[256,512]{1,0:T(8,128)(2,1)S(1)}, u32[]{:S(2)}, u32[]{:S(2)}) collective-permute-start(bf16[256,512]{1,0:T(8,128)(2,1)S(1)} %collective-permute-done), channel_id=1, source_target_pairs={{0,8},{4,12},{8,0},{12,4},{1,9},{5,13},{9,1},{13,5},{2,10},{6,14},... | collective-permute-start | bytes 786440 | tf_op jit(solution)/shard_map/ppermute | solution.py:106
  38.5 0.0 collective-permute-done.4
  38.5 0.0 copy-start.10
  38.5 3.8 %collective-permute-start.3 = (bf16[256,512]{1,0:T(8,128)(2,1)S(1)}, bf16[256,512]{1,0:T(8,128)(2,1)S(1)}, u32[]{:S(2)}, u32[]{:S(2)}) collective-permute-start(bf16[256,512]{1,0:T(8,128)(2,1)S(1)} %collective-permute-done), channel_id=1, source_target_pairs={{0,12},{4,0},{8,4},{12,8},{1,13},{5,1},{9,5},{13,9},{2,14},{6,2},{... | collective-permute-start | bytes 786440 | tf_op jit(solution)/shard_map/ppermute | solution.py:106
  42.2 0.0 collective-permute-done.5
  42.3 0.0 copy-start.11
  42.3 0.7 copy-done.11
  43.0 0.0 collective-permute-done.6
  43.0 2.7 %convolution_convert_fusion.1 = bf16[1024,1024]{1,0:T(8,128)(2,1)S(1)} fusion(bf16[256,512]{1,0:T(8,128)(2,1)} %collective-permute-done.6, bf16[256,512]{1,0:T(8,128)(2,1)} %copy-done.11, bf16[256,512]{1,0:T(8,128)(2,1)} %copy-done.10, bf16[256,512]{1,0:T(8,128)(2,1)S(1)} %fusion.28, bf16[512,1536]{1,0:T(8,128)(2,1)} %param.11), kind=kOutput, calls=%fused_computation.2 | convolution fusion | flops 1078984704 | bytes 4194304 | tf_op jit(solution)/shard_map/dot_general | solution.py:145
  45.7 0.2 fusion.46
  45.9 0.0 copy-start.9
  45.9 6.1 %shard_map.73 = (f32[512,512]{1,0:T(8,128)S(1)}, f32[512,8]{1,0:T(8,128)S(1)}, f32[512,8]{1,0:T(8,128)S(1)}) custom-call(bf16[512,512]{1,0:T(8,128)(2,1)S(1)} %all_gather.3.refs_0_, bf16[1024,512]{1,0:T(8,128)(2,1)S(1)} %get-tuple-element.30.refs_1_, bf16[1024,512]{1,0:T(8,128)(2,1)S(1)} %get-tuple-element.29.refs_2_), custom_call_target="tpu_custom_call" | custom-call | tf_op jit(solution)/shard_map/pallas_call | solution.py:67
  52.0 0.0 collective-permute-done.1
  52.0 0.0 collective-permute-done.2
  52.0 0.0 collective-permute-done.3
  52.0 1.2 convolution_convert_fusion.2
  53.3 0.2 fusion.47
  53.4 8.9 %shard_map.74 = (f32[512,512]{1,0:T(8,128)S(1)}, f32[512,8]{1,0:T(8,128)S(1)}, f32[512,8]{1,0:T(8,128)S(1)}) custom-call(bf16[512,512]{1,0:T(8,128)(2,1)S(1)} %all_gather.3.refs_0_, bf16[1024,512]{1,0:T(8,128)(2,1)S(1)} %get-tuple-element.32.refs_1_, bf16[1024,512]{1,0:T(8,128)(2,1)S(1)} %get-tuple-element.31.refs_2_, ...), custom_call_target="tpu_custom_call" | custom-call | tf_op jit(solution)/shard_map/pallas_call | solution.py:67
  62.4 0.9 constant_dynamic-slice_fusion
  63.3 9.8 %collective-permute-start.7 = (f32[256,512]{1,0:T(8,128)S(1)}, f32[256,512]{1,0:T(8,128)S(1)}, u32[]{:S(2)}, u32[]{:S(2)}) collective-permute-start(f32[256,512]{1,0:T(8,128)S(1)} %get-tuple-element.33), channel_id=1, source_target_pairs={{0,1},{1,0},{2,3},{3,2},{4,5},{5,4},{6,7},{7,6},{8,9},{9,8},{10,11... | collective-permute-start | bytes 1572872 | tf_op jit(solution)/shard_map/ppermute | solution.py:154
  73.1 0.1 copy.14
  73.2 0.1 copy.15
  73.3 0.1 copy.27
  73.4 1.9 %collective-permute-start.8 = (f32[256,16]{1,0:T(8,128)S(1)}, f32[256,16]{1,0:T(8,128)S(1)}, u32[]{:S(2)}, u32[]{:S(2)}) collective-permute-start(f32[256,16]{1,0:T(8,128)S(1)} %copy.27), channel_id=1, source_target_pairs={{0,1},{1,0},{2,3},{3,2},{4,5},{5,4},{6,7},{7,6},{8,9},{9,8},{10,11... | collective-permute-start | bytes 49160 | tf_op jit(solution)/shard_map/ppermute | solution.py:155
  75.3 0.7 copy.26.refs_1_
  76.1 0.6 collective-permute-done.8.refs_3_
  76.7 0.0 collective-permute-done.7.refs_2_
  76.7 0.6 copy-done.6
  77.3 0.2 copy-done.4
  77.5 3.8 %shard_map.75 = bf16[256,512]{1,0:T(8,128)(2,1)} custom-call(f32[256,512]{1,0:T(8,128)} %get-tuple-element.34.refs_0_, f32[256,16]{1,0:T(8,128)} %copy.26.refs_1_, f32[256,512]{1,0:T(8,128)} %copy-done.4, f32[256,16]{1,0:T(8,128)} %copy-done.6), custom_call_target="tpu_custom_call" | custom-call | tf_op jit(solution)/shard_map/pallas_call | solution.py:88
  81.3 1.4 fusion.49
  82.7 0.2 multiply_reduce_fusion
  83.0 0.9 fusion.37
  83.8 21.6 %all-to-all-start = ((bf16[1,32,8,512]{3,2,0,1:T(8,128)(2,1)}), bf16[1,32,8,512]{3,2,0,1:T(8,128)(2,1)S(1)}, u32[]{:S(2)}, u32[]{:S(2)}) async-start(bf16[1,32,8,512]{3,2,0,1:T(8,128)(2,1)} %fusion.37), calls=%async_computation | async-start | bytes 524288 | tf_op jit(solution)/shard_map/all_to_all | solution.py:162
  105.4 0.7 compare_reduce_fusion
  106.2 0.8 fusion.29
  106.9 17.4 %all-to-all-done = bf16[1,32,8,512]{3,2,0,1:T(8,128)(2,1)S(1)} async-done(((bf16[1,32,8,512]{3,2,0,1:T(8,128)(2,1)}), bf16[1,32,8,512]{3,2,0,1:T(8,128)(2,1)S(1)}, u32[]{:S(2)}, u32[]{:S(2)}) %all-to-all-start) | async-done | bytes 262176 | tf_op jit(solution)/shard_map/all_to_all | solution.py:162
  124.4 0.6 fusion
  124.9 0.1 fusion.48
  125.0 0.3 reshape.102
  125.3 0.3 reshape.103
  125.6 1.1 reshape.101
  126.6 0.9 fusion.50
  127.5 0.3 fusion.19
  127.8 0.0 copy-done.5
  127.8 0.8 fusion.2
  128.6 0.0 copy-start.3
  128.6 0.2 copy.23
  128.8 0.3 convert_element_type.56
  129.1 23.8 %all_to_all.8 = bf16[32,1,8,512]{3,2,1,0:T(8,128)(2,1)S(1)} all-to-all(bf16[32,1,8,512]{3,2,1,0:T(8,128)(2,1)S(1)} %bitcast.45), channel_id=1, replica_groups=mesh['x'=4,'zlo'=8,'y'=4,'zhi'=2,'core'=2] {'x','zlo'}, dimensions={0} | all-to-all | bytes 524288 | tf_op jit(solution)/shard_map/all_to_all | solution.py:172
  152.9 0.0 copy-done.3
  152.9 1.0 fusion.4
  (20 shorter events, 0.1 us)
Async XLA Ops:
  0.0 81.3 %copy-start = (bf16[512,512]{1,0:T(8,128)(2,1)S(1)}, bf16[512,512]{1,0:T(8,128)(2,1)}, u32[]{:S(2)}) copy-start(bf16[512,512]{1,0:T(8,128)(2,1)} %param.12) | copy-start | bytes 1572868
  0.0 1.0 copy-start.2
  0.0 1.4 copy-start.7
  1.5 36.9 %collective-permute-start.4 = (bf16[256,512]{1,0:T(8,128)(2,1)S(1)}, bf16[256,512]{1,0:T(8,128)(2,1)S(1)}, u32[]{:S(2)}, u32[]{:S(2)}) collective-permute-start(bf16[256,512]{1,0:T(8,128)(2,1)S(1)} %fusion.28), channel_id=1, source_target_pairs={{0,4},{4,8},{8,12},{12,0},{1,5},{5,9},{9,13},{13,1},{2,6},{6,10},{... | collective-permute-start | bytes 786440 | tf_op jit(solution)/shard_map/ppermute | solution.py:106
  5.6 36.7 %collective-permute-start.5 = (bf16[256,512]{1,0:T(8,128)(2,1)S(1)}, bf16[256,512]{1,0:T(8,128)(2,1)S(1)}, u32[]{:S(2)}, u32[]{:S(2)}) collective-permute-start(bf16[256,512]{1,0:T(8,128)(2,1)S(1)} %fusion.28), channel_id=1, source_target_pairs={{0,8},{4,12},{8,0},{12,4},{1,9},{5,13},{9,1},{13,5},{2,10},{6,14},... | collective-permute-start | bytes 786440 | tf_op jit(solution)/shard_map/ppermute | solution.py:106
  10.1 32.9 %collective-permute-start.6 = (bf16[256,512]{1,0:T(8,128)(2,1)S(1)}, bf16[256,512]{1,0:T(8,128)(2,1)}, u32[]{:S(2)}, u32[]{:S(2)}) collective-permute-start(bf16[256,512]{1,0:T(8,128)(2,1)S(1)} %fusion.28), channel_id=1, source_target_pairs={{0,12},{4,0},{8,4},{12,8},{1,13},{5,1},{9,5},{13,9},{2,14},{6,2},{... | collective-permute-start | bytes 786440 | tf_op jit(solution)/shard_map/ppermute | solution.py:106
  13.1 20.6 %collective-permute-start = (bf16[256,512]{1,0:T(8,128)(2,1)S(1)}, bf16[256,512]{1,0:T(8,128)(2,1)S(1)}, u32[]{:S(2)}, u32[]{:S(2)}) collective-permute-start(bf16[256,512]{1,0:T(8,128)(2,1)S(1)} %fusion.28), channel_id=1, source_target_pairs={{0,2},{2,0},{1,3},{3,1},{4,6},{6,4},{5,7},{7,5},{8,10},{10,8},{9,1... | collective-permute-start | bytes 786440 | tf_op jit(solution)/shard_map/ppermute | solution.py:141
  33.7 18.3 %collective-permute-start.1 = (bf16[256,512]{1,0:T(8,128)(2,1)S(1)}, bf16[256,512]{1,0:T(8,128)(2,1)S(1)}, u32[]{:S(2)}, u32[]{:S(2)}) collective-permute-start(bf16[256,512]{1,0:T(8,128)(2,1)S(1)} %collective-permute-done), channel_id=1, source_target_pairs={{0,4},{4,8},{8,12},{12,0},{1,5},{5,9},{9,13},{13,1},{2,6},{6,10},{... | collective-permute-start | bytes 786440 | tf_op jit(solution)/shard_map/ppermute | solution.py:106
  36.0 16.0 %collective-permute-start.2 = (bf16[256,512]{1,0:T(8,128)(2,1)S(1)}, bf16[256,512]{1,0:T(8,128)(2,1)S(1)}, u32[]{:S(2)}, u32[]{:S(2)}) collective-permute-start(bf16[256,512]{1,0:T(8,128)(2,1)S(1)} %collective-permute-done), channel_id=1, source_target_pairs={{0,8},{4,12},{8,0},{12,4},{1,9},{5,13},{9,1},{13,5},{2,10},{6,14},... | collective-permute-start | bytes 786440 | tf_op jit(solution)/shard_map/ppermute | solution.py:106
  38.5 3.8 %copy-start.10 = (bf16[256,512]{1,0:T(8,128)(2,1)}, bf16[256,512]{1,0:T(8,128)(2,1)S(1)}, u32[]{:S(2)}) copy-start(bf16[256,512]{1,0:T(8,128)(2,1)S(1)} %collective-permute-done.4) | copy-start | bytes 786436
  38.5 13.5 %collective-permute-start.3 = (bf16[256,512]{1,0:T(8,128)(2,1)S(1)}, bf16[256,512]{1,0:T(8,128)(2,1)S(1)}, u32[]{:S(2)}, u32[]{:S(2)}) collective-permute-start(bf16[256,512]{1,0:T(8,128)(2,1)S(1)} %collective-permute-done), channel_id=1, source_target_pairs={{0,12},{4,0},{8,4},{12,8},{1,13},{5,1},{9,5},{13,9},{2,14},{6,2},{... | collective-permute-start | bytes 786440 | tf_op jit(solution)/shard_map/ppermute | solution.py:106
  42.3 0.7 copy-start.11
  45.9 6.1 %copy-start.9 = (bf16[512,1536]{1,0:T(8,128)(2,1)S(1)}, bf16[512,1536]{1,0:T(8,128)(2,1)}, u32[]{:S(2)}) copy-start(bf16[512,1536]{1,0:T(8,128)(2,1)} %param.11) | copy-start | bytes 4718596
  63.3 13.4 %collective-permute-start.7 = (f32[256,512]{1,0:T(8,128)S(1)}, f32[256,512]{1,0:T(8,128)S(1)}, u32[]{:S(2)}, u32[]{:S(2)}) collective-permute-start(f32[256,512]{1,0:T(8,128)S(1)} %get-tuple-element.33), channel_id=1, source_target_pairs={{0,1},{1,0},{2,3},{3,2},{4,5},{5,4},{6,7},{7,6},{8,9},{9,8},{10,11... | collective-permute-start | bytes 1572872 | tf_op jit(solution)/shard_map/ppermute | solution.py:154
  73.2 9.7 %copy-start.8 = (f32[512]{0:T(512)S(1)}, f32[512]{0:T(512)}, u32[]{:S(2)}) copy-start(f32[512]{0:T(512)} %param.13) | copy-start | bytes 6148
  73.4 3.2 %collective-permute-start.8 = (f32[256,16]{1,0:T(8,128)S(1)}, f32[256,16]{1,0:T(8,128)S(1)}, u32[]{:S(2)}, u32[]{:S(2)}) collective-permute-start(f32[256,16]{1,0:T(8,128)S(1)} %copy.27), channel_id=1, source_target_pairs={{0,1},{1,0},{2,3},{3,2},{4,5},{5,4},{6,7},{7,6},{8,9},{9,8},{10,11... | collective-permute-start | bytes 49160 | tf_op jit(solution)/shard_map/ppermute | solution.py:155
  76.7 0.7 copy-start.6
  76.7 0.8 copy-start.4
  81.3 24.9 %copy-start.1 = (bf16[512,1536]{1,0:T(8,128)(2,1)S(1)}, bf16[512,1536]{1,0:T(8,128)(2,1)}, u32[]{:S(2)}) copy-start(bf16[512,1536]{1,0:T(8,128)(2,1)} %param.14) | copy-start | bytes 4718596
  83.8 40.6 %all-to-all-start = ((bf16[1,32,8,512]{3,2,0,1:T(8,128)(2,1)}), bf16[1,32,8,512]{3,2,0,1:T(8,128)(2,1)S(1)}, u32[]{:S(2)}, u32[]{:S(2)}) async-start(bf16[1,32,8,512]{3,2,0,1:T(8,128)(2,1)} %fusion.37), calls=%async_computation | async-start | bytes 524288 | tf_op jit(solution)/shard_map/all_to_all | solution.py:162
  126.6 1.2 copy-start.5
  128.6 24.3 %copy-start.3 = (bf16[512,512]{1,0:T(8,128)(2,1)S(1)}, bf16[512,512]{1,0:T(8,128)(2,1)}, u32[]{:S(2)}) copy-start(bf16[512,512]{1,0:T(8,128)(2,1)} %param.15) | copy-start | bytes 1572868

commit v4 on v3

--- a/solution.py
+++ b/solution.py
@@ -40,19 +40,24 @@
         )
 
 
-def merge_kernel(q_ref, k_ref, v_ref, o1_ref, m1_ref, l1_ref, o_ref, m_ref, l_ref, *, size, scale):
+def merge_kernel(q_ref, k_ref, v_ref, o1_ref, m1_ref, l1_ref, out_ref, *, size, rows):
+    width = HEADS * size
     for h in range(HEADS):
         cols = slice(h * size, (h + 1) * size)
-        scores = _scores(q_ref, k_ref, cols, scale)
-        before = m1_ref[:, h : h + 1]
+        scores = lax.dot_general(
+            q_ref[rows, cols], k_ref[:, cols], (((1,), (1,)), ((), ())),
+            preferred_element_type=jnp.float32,
+        )
+        before = m1_ref[rows, h : h + 1]
         peak = jnp.maximum(before, jnp.max(scores, axis=1, keepdims=True))
         weights = jnp.exp(scores - peak)
         fade = jnp.exp(before - peak)
-        l_ref[:, h : h + 1] = l1_ref[:, h : h + 1] * fade + jnp.sum(weights, axis=1, keepdims=True)
-        m_ref[:, h : h + 1] = peak
-        o_ref[:, cols] = o1_ref[:, cols] * fade + jnp.dot(
+        total = l1_ref[rows, h : h + 1] * fade + jnp.sum(weights, axis=1, keepdims=True)
+        out_ref[:, cols] = o1_ref[rows, cols] * fade + jnp.dot(
             weights.astype(jnp.bfloat16), v_ref[:, cols], preferred_element_type=jnp.float32
         )
+        out_ref[:, width + h : width + h + 1] = peak
+        out_ref[:, width + HEADS + h : width + HEADS + h + 1] = total
 
 
 def _attention_call(kernel, query, keys, values, state):
@@ -71,22 +76,25 @@
     )(query, keys, values, *state)
 
 
-def combine_kernel(o1_ref, s1_ref, o2_ref, s2_ref, out_ref, *, size):
+def combine_kernel(a_ref, b_ref, out_ref, *, size):
+    width = HEADS * size
     for h in range(HEADS):
         cols = slice(h * size, (h + 1) * size)
-        m1, l1 = s1_ref[:, h : h + 1], s1_ref[:, HEADS + h : HEADS + h + 1]
-        m2, l2 = s2_ref[:, h : h + 1], s2_ref[:, HEADS + h : HEADS + h + 1]
+        m1, m2 = a_ref[:, width + h : width + h + 1], b_ref[:, width + h : width + h + 1]
+        l1 = a_ref[:, width + HEADS + h : width + HEADS + h + 1]
+        l2 = b_ref[:, width + HEADS + h : width + HEADS + h + 1]
         top = jnp.maximum(m1, m2)
         f1, f2 = jnp.exp(m1 - top), jnp.exp(m2 - top)
-        summed = o1_ref[:, cols] * f1 + o2_ref[:, cols] * f2
+        summed = a_ref[:, cols] * f1 + b_ref[:, cols] * f2
         out_ref[:, cols] = (summed / (l1 * f1 + l2 * f2)).astype(out_ref.dtype)
 
 
-def combine(own_summed, own_stats, their_summed, their_stats):
-    count, width = own_summed.shape
+def combine(own, theirs):
+    count, packed = own.shape
+    width = packed - 2 * HEADS
     body = lambda *refs: combine_kernel(*refs, size=width // HEADS)
     return pl.pallas_call(body, out_shape=jax.ShapeDtypeStruct((count, width), jnp.bfloat16))(
-        own_summed, own_stats, their_summed, their_stats
+        own, theirs
     )
 
 
@@ -94,8 +102,15 @@
     return _attention_call(partial_kernel, query, keys, values, ())
 
 
-def spatial_merge(query, keys, values, state):
-    return _attention_call(merge_kernel, query, keys, values, state)
+def spatial_merge(query, keys, values, state, start, count):
+    width = query.shape[1]
+    size = width // HEADS
+    body = lambda *refs: merge_kernel(*refs, size=size, rows=slice(start, start + count))
+    return pl.pallas_call(
+        body,
+        out_shape=jax.ShapeDtypeStruct((count, width + 2 * HEADS), jnp.float32),
+        compiler_params=pltpu.CompilerParams(vmem_limit_bytes=48 * 1024 * 1024),
+    )(query, keys, values, *state)
 
 
 def spread_y(rows):
@@ -139,21 +154,18 @@
     w_query = w_spatial[:, :width] * jnp.asarray(1.0 / math.sqrt(width // HEADS), w_spatial.dtype)
     query = jnp.dot(normed, w_query, preferred_element_type=jnp.float32).astype(jnp.bfloat16)
     partner = lax.ppermute(normed, "zhi", [(0, 1), (1, 0)])
-    both = lax.all_gather(query, "core", axis=0, tiled=True)
+    swap = [(0, 1), (1, 0)]
+    both = jnp.concatenate([lax.ppermute(query, "core", swap), query], axis=0)
     w_pairs = w_spatial[:, width:]
     near_rows = spread_y(normed)
     near = jnp.dot(near_rows, w_pairs, preferred_element_type=jnp.float32).astype(jnp.bfloat16)
     state = spatial_partial(both, near[:, :width], near[:, width:])
     far_rows = spread_y(partner)
     far = jnp.dot(far_rows, w_pairs, preferred_element_type=jnp.float32).astype(jnp.bfloat16)
-    summed, peak, total = spatial_merge(both, far[:, :width], far[:, width:], state)
-    mine = lax.axis_index("core")
-    other = 1 - mine
-    pick = lambda a, i: lax.dynamic_slice_in_dim(a, i * count, count, 0)
-    stats = jnp.concatenate([peak, total], axis=1)
-    their_summed = lax.ppermute(pick(summed, other), "core", [(0, 1), (1, 0)])
-    their_stats = lax.ppermute(pick(stats, other), "core", [(0, 1), (1, 0)])
-    context = combine(pick(summed, mine), pick(stats, mine), their_summed, their_stats)
+    theirs = spatial_merge(both, far[:, :width], far[:, width:], state, 0, count)
+    theirs = lax.ppermute(theirs, "core", swap)
+    own = spatial_merge(both, far[:, :width], far[:, width:], state, count, count)
+    context = combine(own, theirs)
     after = resid + jnp.dot(context, w_spatial_out, preferred_element_type=jnp.float32)
     second = layer_norm(after, norm_temporal).astype(jnp.bfloat16)
     owners = lax.axis_size(("x", "zlo"))

time: 155 us -> 149 us (0.961)
  starting transfers between devices: 68.9 us -> 60.3 us
  local copies, waits for them, and re-layouts: 7.01 us -> 11 us
  blocking collectives: 27.4 us -> 23.9 us
  matrix products: 9.98 us -> 7.45 us
  waiting for transfers between devices: 18.2 us -> 20.6 us
    pallas_call x0 -> x2, Pallas kernels: none -> 10.3 us  [spatial_merge(): pl.pallas_call(body, out_shape=jax.ShapeDtypeStruct((count, width + 2 * H...]
    pallas_call x2 -> x1, Pallas kernels: 15 us -> 6.08 us  [_attention_call(): pl.pallas_call(body, out_shape=shapes, compiler_params=pltpu.CompilerPara...]
    ppermute x2, starting transfers between devices: 11.8 us -> 6.2 us  [the longest x1 3.34 us: layer(): theirs = lax.ppermute(theirs, 'core', swap)]
    all_gather x1 -> x0, blocking collectives: 3.6 us -> none  [layer(): both = lax.all_gather(query, 'core', axis=0, tiled=True)]
    all_to_all x1, starting transfers between devices: 21.6 us -> 18.6 us  [layer(): lax.all_to_all(second, ('x', 'zlo'), split_axis=1, concat_axis=0, tiled=T...]
    ppermute x6, waiting for transfers between devices: 0.02 us -> 2.94 us  [spread_y(): pieces.append(lax.ppermute(rows, 'y', pairs))]
    ppermute x0 -> x1, local copies, waits for them, and re-layouts: none -> 2.19 us  [layer(): theirs = lax.ppermute(theirs, 'core', swap)]
    pallas_call x2 -> x1, local copies, waits for them, and re-layouts: 0.2 us -> 2.13 us  [spatial_merge(): pl.pallas_call(body, out_shape=jax.ShapeDtypeStruct((count, width + 2 * H...]
  transfers between devices with their start and end apart: 10 -> 10, of which waited for: 3 -> 3; matrix products, arithmetic and copies ran while one was open for 4% -> 2% of each run, Pallas kernels for 4% -> 8%
where the time goes in v4:
time: 149 us; the launch traced here: 147 us
  starting transfers between devices  60.3 us (40%)
  blocking collectives  23.9 us (16%)
  waiting for transfers between devices  20.6 us (14%)
  Pallas kernels  20.1 us (13%)
  local copies, waits for them, and re-layouts  11 us (7%)
  matrix products  7.45 us (5%)
  other arithmetic  3.33 us (2%)
    all_to_all x1, blocking collectives, layer(): lax.all_to_all(context_t, ('x', 'zlo'), split_axis=0, concat_axis=1, tile...  23.9 us
    ppermute x6, starting transfers between devices, spread_y(): pieces.append(lax.ppermute(rows, 'y', pairs))  19.2 us
    all_to_all x1, starting transfers between devices, layer(): lax.all_to_all(second, ('x', 'zlo'), split_axis=1, concat_axis=0, tiled=T...  18.6 us
    all_to_all x1, waiting for transfers between devices, layer(): lax.all_to_all(second, ('x', 'zlo'), split_axis=1, concat_axis=0, tiled=T...  17.6 us
    ppermute x1, starting transfers between devices, layer(): partner = lax.ppermute(normed, 'zhi', [(0, 1), (1, 0)])  16.3 us
    pallas_call x2, Pallas kernels, spatial_merge(): pl.pallas_call(body, out_shape=jax.ShapeDtypeStruct((count, width + 2 * H...  10.3 us
    pallas_call x1, Pallas kernels, _attention_call(): pl.pallas_call(body, out_shape=shapes, compiler_params=pltpu.CompilerPara...  6.08 us
    unnamed x28, local copies, waits for them, and re-layouts  4.9 us
  transfers between devices with their start and end apart: 10, of which 3 were waited for; matrix products, arithmetic and copies ran while one was open for 2% of the time, Pallas kernels for 8%

profile of v4, /device:TPU:1, one launch (start us, length us, event | category | flops | bytes accessed | tf_op | source)
XLA Modules:
  0.0 147.1 jit_solution(17694298672318505784)
XLA Ops:
  0.0 0.0 copy-start
  0.0 0.0 copy-start.13
  0.0 1.0 copy-done.8
  1.0 0.1 convert_reduce_fusion
  1.1 0.2 fusion.26
  1.4 0.0 copy-done.11
  1.4 0.1 fusion.28
  1.5 16.3 %collective-permute-start.1 = (bf16[256,512]{1,0:T(8,128)(2,1)S(1)}, bf16[256,512]{1,0:T(8,128)(2,1)S(1)}, u32[]{:S(2)}, u32[]{:S(2)}) collective-permute-start(bf16[256,512]{1,0:T(8,128)(2,1)S(1)} %fusion.28), channel_id=1, source_target_pairs={{0,2},{2,0},{1,3},{3,1},{4,6},{6,4},{5,7},{7,5},{8,10},{10,8},{9,1... | collective-permute-start | bytes 786440 | tf_op jit(solution)/shard_map/ppermute | solution.py:156
  17.8 0.0 copy-done.13
  17.8 0.3 convolution_convert_fusion.3
  18.1 2.9 %collective-permute-start = (bf16[256,512]{1,0:T(8,128)(2,1)S(1)}, bf16[256,512]{1,0:T(8,128)(2,1)S(1)}, u32[]{:S(2)}, u32[]{:S(2)}) collective-permute-start(bf16[256,512]{1,0:T(8,128)(2,1)S(1)} %convolution_convert_fusion.3), channel_id=1, source_target_pairs={{0,1},{1,0},{2,3},{3,2},{4,5},{5,4},{6,7},{7,6},{8,9},{9,8},{10,11... | collective-permute-start | bytes 786440 | tf_op jit(solution)/shard_map/ppermute | solution.py:158
  21.0 3.2 %collective-permute-start.5 = (bf16[256,512]{1,0:T(8,128)(2,1)S(1)}, bf16[256,512]{1,0:T(8,128)(2,1)S(1)}, u32[]{:S(2)}, u32[]{:S(2)}) collective-permute-start(bf16[256,512]{1,0:T(8,128)(2,1)S(1)} %fusion.28), channel_id=1, source_target_pairs={{0,4},{4,8},{8,12},{12,0},{1,5},{5,9},{9,13},{13,1},{2,6},{6,10},{... | collective-permute-start | bytes 786440 | tf_op jit(solution)/shard_map/ppermute | solution.py:121
  24.2 4.5 %collective-permute-start.6 = (bf16[256,512]{1,0:T(8,128)(2,1)S(1)}, bf16[256,512]{1,0:T(8,128)(2,1)S(1)}, u32[]{:S(2)}, u32[]{:S(2)}) collective-permute-start(bf16[256,512]{1,0:T(8,128)(2,1)S(1)} %fusion.28), channel_id=1, source_target_pairs={{0,8},{4,12},{8,0},{12,4},{1,9},{5,13},{9,1},{13,5},{2,10},{6,14},... | collective-permute-start | bytes 786440 | tf_op jit(solution)/shard_map/ppermute | solution.py:121
  28.7 3.0 %collective-permute-start.7 = (bf16[256,512]{1,0:T(8,128)(2,1)S(1)}, bf16[256,512]{1,0:T(8,128)(2,1)S(1)}, u32[]{:S(2)}, u32[]{:S(2)}) collective-permute-start(bf16[256,512]{1,0:T(8,128)(2,1)S(1)} %fusion.28), channel_id=1, source_target_pairs={{0,12},{4,0},{8,4},{12,8},{1,13},{5,1},{9,5},{13,9},{2,14},{6,2},{... | collective-permute-start | bytes 786440 | tf_op jit(solution)/shard_map/ppermute | solution.py:121
  31.7 0.0 collective-permute-done.1
  31.7 2.3 %collective-permute-start.2 = (bf16[256,512]{1,0:T(8,128)(2,1)S(1)}, bf16[256,512]{1,0:T(8,128)(2,1)S(1)}, u32[]{:S(2)}, u32[]{:S(2)}) collective-permute-start(bf16[256,512]{1,0:T(8,128)(2,1)S(1)} %collective-permute-done.1), channel_id=1, source_target_pairs={{0,4},{4,8},{8,12},{12,0},{1,5},{5,9},{9,13},{13,1},{2,6},{6,10},{... | collective-permute-start | bytes 786440 | tf_op jit(solution)/shard_map/ppermute | solution.py:121
  34.0 0.0 collective-permute-done
  34.1 2.7 %collective-permute-start.3 = (bf16[256,512]{1,0:T(8,128)(2,1)S(1)}, bf16[256,512]{1,0:T(8,128)(2,1)S(1)}, u32[]{:S(2)}, u32[]{:S(2)}) collective-permute-start(bf16[256,512]{1,0:T(8,128)(2,1)S(1)} %collective-permute-done.1), channel_id=1, source_target_pairs={{0,8},{4,12},{8,0},{12,4},{1,9},{5,13},{9,1},{13,5},{2,10},{6,14},... | collective-permute-start | bytes 786440 | tf_op jit(solution)/shard_map/ppermute | solution.py:121
  36.8 0.0 collective-permute-done.5
  36.8 3.5 %collective-permute-start.4 = (bf16[256,512]{1,0:T(8,128)(2,1)S(1)}, bf16[256,512]{1,0:T(8,128)(2,1)S(1)}, u32[]{:S(2)}, u32[]{:S(2)}) collective-permute-start(bf16[256,512]{1,0:T(8,128)(2,1)S(1)} %collective-permute-done.1), channel_id=1, source_target_pairs={{0,12},{4,0},{8,4},{12,8},{1,13},{5,1},{9,5},{13,9},{2,14},{6,2},{... | collective-permute-start | bytes 786440 | tf_op jit(solution)/shard_map/ppermute | solution.py:121
  40.3 0.0 collective-permute-done.6
  40.4 0.0 collective-permute-done.7
  40.4 1.2 convolution_convert_fusion.1
  41.6 0.2 fusion.44
  41.8 6.1 %shard_map.73 = (f32[512,512]{1,0:T(8,128)S(1)}, f32[512,8]{1,0:T(8,128)S(1)}, f32[512,8]{1,0:T(8,128)S(1)}) custom-call(bf16[512,512]{1,0:T(8,128)(2,1)S(1)} %pad_maximum_fusion.refs_0_, bf16[1024,512]{1,0:T(8,128)(2,1)S(1)} %get-tuple-element.24.refs_1_, bf16[1024,512]{1,0:T(8,128)(2,1)S(1)} %get-tuple-element.23.refs_2_), custom_call_target="tpu_custom_call" | custom-call | tf_op jit(solution)/shard_map/pallas_call | solution.py:72
  47.9 0.0 copy-start.5
  47.9 0.0 collective-permute-done.2
  47.9 2.1 %collective-permute-done.3 = bf16[256,512]{1,0:T(8,128)(2,1)S(1)} collective-permute-done((bf16[256,512]{1,0:T(8,128)(2,1)S(1)}, bf16[256,512]{1,0:T(8,128)(2,1)S(1)}, u32[]{:S(2)}, u32[]{:S(2)}) %collective-permute-start.3) | collective-permute-done | bytes 262176 | tf_op jit(solution)/shard_map/ppermute | solution.py:121
  50.0 0.8 collective-permute-done.4
  50.8 1.2 convolution_convert_fusion.2
  52.1 0.2 fusion.45
  52.3 5.3 %shard_map.75 = f32[256,528]{1,0:T(8,128)S(1)} custom-call(bf16[512,512]{1,0:T(8,128)(2,1)S(1)} %pad_maximum_fusion.refs_0_, bf16[1024,512]{1,0:T(8,128)(2,1)S(1)} %get-tuple-element.26.refs_1_, bf16[1024,512]{1,0:T(8,128)(2,1)S(1)} %get-tuple-element.25.refs_2_, f32[512,512]{1,0:T(8,128)S(1)} %get-tuple-element.20.refs_3_, ...), custom_call_target="tpu_custom_call" | custom-call | tf_op jit(solution)/shard_map/pallas_call | solution.py:109
  57.5 0.0 copy-start.4
  57.5 0.9 copy-done.4
  58.4 2.1 %copy.14 = f32[256,528]{0,1:T(8,128)} copy(f32[256,528]{1,0:T(8,128)} %copy-done.4) | data formatting | bytes 1081344 | tf_op jit(solution)/shard_map/pallas_call | solution.py:109
  60.5 3.3 %collective-permute-start.8 = (f32[256,528]{0,1:T(8,128)}, f32[256,528]{0,1:T(8,128)}, u32[]{:S(2)}, u32[]{:S(2)}) collective-permute-start(f32[256,528]{0,1:T(8,128)} %copy.14), channel_id=1, source_target_pairs={{0,1},{1,0},{2,3},{3,2},{4,5},{5,4},{6,7},{7,6},{8,9},{9,8},{10,11... | collective-permute-start | bytes 1622024 | tf_op jit(solution)/shard_map/ppermute | solution.py:166
  63.9 1.2 copy-done.2
  65.1 0.9 copy-done.6
  66.0 5.0 %shard_map.74.refs_0_ = f32[256,528]{1,0:T(8,128)S(1)} custom-call(bf16[512,512]{1,0:T(8,128)(2,1)S(1)} %pad_maximum_fusion.refs_0_, bf16[1024,512]{1,0:T(8,128)(2,1)S(1)} %get-tuple-element.26.refs_1_, bf16[1024,512]{1,0:T(8,128)(2,1)S(1)} %get-tuple-element.25.refs_2_, f32[512,512]{1,0:T(8,128)S(1)} %copy-done.2, f32[512,8]{1,0:T(8,128)S(1)} %get-tuple-element.21.refs_4_, ...), custom_call_target="tpu_custom_call" | custom-call | tf_op jit(solution)/shard_map/pallas_call | solution.py:109
  71.1 0.8 copy-done.3
  72.0 0.0 collective-permute-done.8
  72.0 2.2 %copy.15.refs_1_ = f32[256,528]{1,0:T(8,128)} copy(f32[256,528]{0,1:T(8,128)} %collective-permute-done.8) | data formatting | bytes 1081344 | tf_op jit(solution)/shard_map/ppermute | solution.py:166
  74.1 3.7 %shard_map.76 = bf16[256,512]{1,0:T(8,128)(2,1)} custom-call(f32[256,528]{1,0:T(8,128)} %copy-done.3, f32[256,528]{1,0:T(8,128)} %copy.15.refs_1_), custom_call_target="tpu_custom_call" | custom-call | tf_op jit(solution)/shard_map/pallas_call | solution.py:96
  77.9 1.4 fusion.47
  79.4 0.2 multiply_reduce_fusion
  79.6 0.9 fusion.37
  80.5 18.6 %all-to-all-start = ((bf16[1,32,8,512]{3,2,0,1:T(8,128)(2,1)}), bf16[1,32,8,512]{3,2,0,1:T(8,128)(2,1)S(1)}, u32[]{:S(2)}, u32[]{:S(2)}) async-start(bf16[1,32,8,512]{3,2,0,1:T(8,128)(2,1)} %fusion.37), calls=%async_computation | async-start | bytes 524288 | tf_op jit(solution)/shard_map/all_to_all | solution.py:174
  99.1 0.7 compare_reduce_fusion
  99.7 0.8 fusion.29
  100.5 17.6 %all-to-all-done = bf16[1,32,8,512]{3,2,0,1:T(8,128)(2,1)S(1)} async-done(((bf16[1,32,8,512]{3,2,0,1:T(8,128)(2,1)}), bf16[1,32,8,512]{3,2,0,1:T(8,128)(2,1)S(1)}, u32[]{:S(2)}, u32[]{:S(2)}) %all-to-all-start) | async-done | bytes 262176 | tf_op jit(solution)/shard_map/all_to_all | solution.py:174
  118.1 0.6 fusion
  118.7 0.1 fusion.46
  118.8 0.3 reshape.102
  119.1 0.3 reshape.103
  119.4 0.3 reshape.101
  119.6 0.9 fusion.48
  120.5 0.3 fusion.19
  120.8 0.8 fusion.2
  121.6 0.0 copy-start.10
  121.6 0.2 copy.21
  121.8 0.3 convert_element_type.56
  122.1 23.9 %all_to_all.8 = bf16[32,1,8,512]{3,2,1,0:T(8,128)(2,1)S(1)} all-to-all(bf16[32,1,8,512]{3,2,1,0:T(8,128)(2,1)S(1)} %bitcast.45), channel_id=1, replica_groups=mesh['x'=4,'zlo'=8,'y'=4,'zhi'=2,'core'=2] {'x','zlo'}, dimensions={0} | all-to-all | bytes 524288 | tf_op jit(solution)/shard_map/all_to_all | solution.py:184
  146.1 0.0 copy-done.10
  146.1 1.0 fusion.4
  (21 shorter events, 0.1 us)
Async XLA Ops:
  0.0 77.9 %copy-start = (bf16[512,512]{1,0:T(8,128)(2,1)S(1)}, bf16[512,512]{1,0:T(8,128)(2,1)}, u32[]{:S(2)}) copy-start(bf16[512,512]{1,0:T(8,128)(2,1)} %param.12) | copy-start | bytes 1572868
  0.0 1.0 copy-start.8
  0.0 1.4 copy-start.11
  0.0 17.8 %copy-start.13 = (bf16[512,1536]{1,0:T(8,128)(2,1)S(1)}, bf16[512,1536]{1,0:T(8,128)(2,1)}, u32[]{:S(2)}) copy-start(bf16[512,1536]{1,0:T(8,128)(2,1)} %param.11) | copy-start | bytes 4718596
  1.5 30.2 %collective-permute-start.1 = (bf16[256,512]{1,0:T(8,128)(2,1)S(1)}, bf16[256,512]{1,0:T(8,128)(2,1)S(1)}, u32[]{:S(2)}, u32[]{:S(2)}) collective-permute-start(bf16[256,512]{1,0:T(8,128)(2,1)S(1)} %fusion.28), channel_id=1, source_target_pairs={{0,2},{2,0},{1,3},{3,1},{4,6},{6,4},{5,7},{7,5},{8,10},{10,8},{9,1... | collective-permute-start | bytes 786440 | tf_op jit(solution)/shard_map/ppermute | solution.py:156
  18.1 15.9 %collective-permute-start = (bf16[256,512]{1,0:T(8,128)(2,1)S(1)}, bf16[256,512]{1,0:T(8,128)(2,1)S(1)}, u32[]{:S(2)}, u32[]{:S(2)}) collective-permute-start(bf16[256,512]{1,0:T(8,128)(2,1)S(1)} %convolution_convert_fusion.3), channel_id=1, source_target_pairs={{0,1},{1,0},{2,3},{3,2},{4,5},{5,4},{6,7},{7,6},{8,9},{9,8},{10,11... | collective-permute-start | bytes 786440 | tf_op jit(solution)/shard_map/ppermute | solution.py:158
  21.0 15.8 %collective-permute-start.5 = (bf16[256,512]{1,0:T(8,128)(2,1)S(1)}, bf16[256,512]{1,0:T(8,128)(2,1)S(1)}, u32[]{:S(2)}, u32[]{:S(2)}) collective-permute-start(bf16[256,512]{1,0:T(8,128)(2,1)S(1)} %fusion.28), channel_id=1, source_target_pairs={{0,4},{4,8},{8,12},{12,0},{1,5},{5,9},{9,13},{13,1},{2,6},{6,10},{... | collective-permute-start | bytes 786440 | tf_op jit(solution)/shard_map/ppermute | solution.py:121
  24.2 16.2 %collective-permute-start.6 = (bf16[256,512]{1,0:T(8,128)(2,1)S(1)}, bf16[256,512]{1,0:T(8,128)(2,1)S(1)}, u32[]{:S(2)}, u32[]{:S(2)}) collective-permute-start(bf16[256,512]{1,0:T(8,128)(2,1)S(1)} %fusion.28), channel_id=1, source_target_pairs={{0,8},{4,12},{8,0},{12,4},{1,9},{5,13},{9,1},{13,5},{2,10},{6,14},... | collective-permute-start | bytes 786440 | tf_op jit(solution)/shard_map/ppermute | solution.py:121
  28.7 11.6 %collective-permute-start.7 = (bf16[256,512]{1,0:T(8,128)(2,1)S(1)}, bf16[256,512]{1,0:T(8,128)(2,1)S(1)}, u32[]{:S(2)}, u32[]{:S(2)}) collective-permute-start(bf16[256,512]{1,0:T(8,128)(2,1)S(1)} %fusion.28), channel_id=1, source_target_pairs={{0,12},{4,0},{8,4},{12,8},{1,13},{5,1},{9,5},{13,9},{2,14},{6,2},{... | collective-permute-start | bytes 786440 | tf_op jit(solution)/shard_map/ppermute | solution.py:121
  31.7 16.2 %collective-permute-start.2 = (bf16[256,512]{1,0:T(8,128)(2,1)S(1)}, bf16[256,512]{1,0:T(8,128)(2,1)S(1)}, u32[]{:S(2)}, u32[]{:S(2)}) collective-permute-start(bf16[256,512]{1,0:T(8,128)(2,1)S(1)} %collective-permute-done.1), channel_id=1, source_target_pairs={{0,4},{4,8},{8,12},{12,0},{1,5},{5,9},{9,13},{13,1},{2,6},{6,10},{... | collective-permute-start | bytes 786440 | tf_op jit(solution)/shard_map/ppermute | solution.py:121
  34.1 16.0 %collective-permute-start.3 = (bf16[256,512]{1,0:T(8,128)(2,1)S(1)}, bf16[256,512]{1,0:T(8,128)(2,1)S(1)}, u32[]{:S(2)}, u32[]{:S(2)}) collective-permute-start(bf16[256,512]{1,0:T(8,128)(2,1)S(1)} %collective-permute-done.1), channel_id=1, source_target_pairs={{0,8},{4,12},{8,0},{12,4},{1,9},{5,13},{9,1},{13,5},{2,10},{6,14},... | collective-permute-start | bytes 786440 | tf_op jit(solution)/shard_map/ppermute | solution.py:121
  36.8 14.0 %collective-permute-start.4 = (bf16[256,512]{1,0:T(8,128)(2,1)S(1)}, bf16[256,512]{1,0:T(8,128)(2,1)S(1)}, u32[]{:S(2)}, u32[]{:S(2)}) collective-permute-start(bf16[256,512]{1,0:T(8,128)(2,1)S(1)} %collective-permute-done.1), channel_id=1, source_target_pairs={{0,12},{4,0},{8,4},{12,8},{1,13},{5,1},{9,5},{13,9},{2,14},{6,2},{... | collective-permute-start | bytes 786440 | tf_op jit(solution)/shard_map/ppermute | solution.py:121
  47.9 4.4 %copy-start.1 = (f32[512,512]{1,0:T(8,128)}, f32[512,512]{1,0:T(8,128)S(1)}, u32[]{:S(2)}) copy-start(f32[512,512]{1,0:T(8,128)S(1)} %get-tuple-element.20.refs_3_) | copy-start | bytes 3145732
  47.9 4.4 %copy-start.5 = (f32[512,8]{1,0:T(8,128)}, f32[512,8]{1,0:T(8,128)S(1)}, u32[]{:S(2)}) copy-start(f32[512,8]{1,0:T(8,128)S(1)} %get-tuple-element.22.refs_5_) | copy-start | bytes 49156
  57.5 0.9 copy-start.4
  60.5 11.4 %collective-permute-start.8 = (f32[256,528]{0,1:T(8,128)}, f32[256,528]{0,1:T(8,128)}, u32[]{:S(2)}, u32[]{:S(2)}) collective-permute-start(f32[256,528]{0,1:T(8,128)} %copy.14), channel_id=1, source_target_pairs={{0,1},{1,0},{2,3},{3,2},{4,5},{5,4},{6,7},{7,6},{8,9},{9,8},{10,11... | collective-permute-start | bytes 1622024 | tf_op jit(solution)/shard_map/ppermute | solution.py:166
  63.9 1.2 copy-start.2
  65.1 0.9 copy-start.6
  71.1 0.8 copy-start.3
  71.9 6.0 %copy-start.9 = (bf16[1,256,512]{2,1,0:T(8,128)(2,1)S(1)}, bf16[1,256,512]{2,1,0:T(8,128)(2,1)}, u32[]{:S(2)}) copy-start(bf16[1,256,512]{2,1,0:T(8,128)(2,1)} %param.9) | copy-start | bytes 786436
  74.1 5.4 %copy-start.12 = (f32[512]{0:T(512)S(1)}, f32[512]{0:T(512)}, u32[]{:S(2)}) copy-start(f32[512]{0:T(512)} %param.13) | copy-start | bytes 6148
  77.9 21.8 %copy-start.7 = (bf16[512,1536]{1,0:T(8,128)(2,1)S(1)}, bf16[512,1536]{1,0:T(8,128)(2,1)}, u32[]{:S(2)}) copy-start(bf16[512,1536]{1,0:T(8,128)(2,1)} %param.14) | copy-start | bytes 4718596
  80.5 37.7 %all-to-all-start = ((bf16[1,32,8,512]{3,2,0,1:T(8,128)(2,1)}), bf16[1,32,8,512]{3,2,0,1:T(8,128)(2,1)S(1)}, u32[]{:S(2)}, u32[]{:S(2)}) async-start(bf16[1,32,8,512]{3,2,0,1:T(8,128)(2,1)} %fusion.37), calls=%async_computation | async-start | bytes 524288 | tf_op jit(solution)/shard_map/all_to_all | solution.py:174
  121.6 24.5 %copy-start.10 = (bf16[512,512]{1,0:T(8,128)(2,1)S(1)}, bf16[512,512]{1,0:T(8,128)(2,1)}, u32[]{:S(2)}) copy-start(bf16[512,512]{1,0:T(8,128)(2,1)} %param.15) | copy-start | bytes 1572868

commit v5 on v4

--- a/solution.py
+++ b/solution.py
@@ -10,6 +10,7 @@
 from jax.sharding import PartitionSpec as P
 
 HEADS = 8
+STATS = 64
 
 
 def layer_norm(rows, gain):
@@ -57,7 +58,7 @@
             weights.astype(jnp.bfloat16), v_ref[:, cols], preferred_element_type=jnp.float32
         )
         out_ref[:, width + h : width + h + 1] = peak
-        out_ref[:, width + HEADS + h : width + HEADS + h + 1] = total
+        out_ref[:, width + STATS + h : width + STATS + h + 1] = total
 
 
 def _attention_call(kernel, query, keys, values, state):
@@ -81,8 +82,8 @@
     for h in range(HEADS):
         cols = slice(h * size, (h + 1) * size)
         m1, m2 = a_ref[:, width + h : width + h + 1], b_ref[:, width + h : width + h + 1]
-        l1 = a_ref[:, width + HEADS + h : width + HEADS + h + 1]
-        l2 = b_ref[:, width + HEADS + h : width + HEADS + h + 1]
+        l1 = a_ref[:, width + STATS + h : width + STATS + h + 1]
+        l2 = b_ref[:, width + STATS + h : width + STATS + h + 1]
         top = jnp.maximum(m1, m2)
         f1, f2 = jnp.exp(m1 - top), jnp.exp(m2 - top)
         summed = a_ref[:, cols] * f1 + b_ref[:, cols] * f2
@@ -91,7 +92,7 @@
 
 def combine(own, theirs):
     count, packed = own.shape
-    width = packed - 2 * HEADS
+    width = packed - 2 * STATS
     body = lambda *refs: combine_kernel(*refs, size=width // HEADS)
     return pl.pallas_call(body, out_shape=jax.ShapeDtypeStruct((count, width), jnp.bfloat16))(
         own, theirs
@@ -108,7 +109,7 @@
     body = lambda *refs: merge_kernel(*refs, size=size, rows=slice(start, start + count))
     return pl.pallas_call(
         body,
-        out_shape=jax.ShapeDtypeStruct((count, width + 2 * HEADS), jnp.float32),
+        out_shape=jax.ShapeDtypeStruct((count, width + 2 * STATS), jnp.float32),
         compiler_params=pltpu.CompilerParams(vmem_limit_bytes=48 * 1024 * 1024),
     )(query, keys, values, *state)
 

time: 149 us -> 143 us (0.960)
  local copies, waits for them, and re-layouts: 11 us -> 5.23 us
    unnamed x28 -> x20, local copies, waits for them, and re-layouts: 4.9 us -> 2.7 us
    ppermute x1 -> x0, local copies, waits for them, and re-layouts: 2.19 us -> none  [layer(): theirs = lax.ppermute(theirs, 'core', swap)]
    pallas_call x1 -> x0, local copies, waits for them, and re-layouts: 2.13 us -> none  [spatial_merge(): pl.pallas_call(body, out_shape=jax.ShapeDtypeStruct((count, width + 2 * H...]
where the time goes in v5:
time: 143 us; the launch traced here: 141 us
  starting transfers between devices  60.3 us (42%)
  blocking collectives  23.9 us (17%)
  waiting for transfers between devices  20.5 us (14%)
  Pallas kernels  20.1 us (14%)
  matrix products  7.45 us (5%)
  local copies, waits for them, and re-layouts  5.23 us (4%)
  other arithmetic  3.43 us (2%)
    all_to_all x1, blocking collectives, layer(): lax.all_to_all(context_t, ('x', 'zlo'), split_axis=0, concat_axis=1, tile...  23.9 us
    ppermute x6, starting transfers between devices, spread_y(): pieces.append(lax.ppermute(rows, 'y', pairs))  19.2 us
    all_to_all x1, starting transfers between devices, layer(): lax.all_to_all(second, ('x', 'zlo'), split_axis=1, concat_axis=0, tiled=T...  18.6 us
    all_to_all x1, waiting for transfers between devices, layer(): lax.all_to_all(second, ('x', 'zlo'), split_axis=1, concat_axis=0, tiled=T...  17.5 us
    ppermute x1, starting transfers between devices, layer(): partner = lax.ppermute(normed, 'zhi', [(0, 1), (1, 0)])  16.3 us
    pallas_call x2, Pallas kernels, spatial_merge(): pl.pallas_call(body, out_shape=jax.ShapeDtypeStruct((count, width + 2 * S...  10.3 us
    pallas_call x1, Pallas kernels, _attention_call(): pl.pallas_call(body, out_shape=shapes, compiler_params=pltpu.CompilerPara...  6.08 us
    pallas_call x1, Pallas kernels, combine(): pl.pallas_call(body, out_shape=jax.ShapeDtypeStruct((count, width), jnp.b...  3.74 us
  transfers between devices with their start and end apart: 10, of which 3 were waited for; matrix products, arithmetic and copies ran while one was open for 2% of the time, Pallas kernels for 8%

profile of v5, /device:TPU:1, one launch (start us, length us, event | category | flops | bytes accessed | tf_op | source)
XLA Modules:
  0.0 141.3 jit_solution(7853142792010582764)
XLA Ops:
  0.0 0.0 copy-start
  0.0 0.0 copy-start.7
  0.0 0.0 copy-start.9
  0.0 1.0 copy-done.3
  1.0 0.1 convert_reduce_fusion
  1.1 0.2 fusion.26
  1.4 0.0 copy-done.7
  1.4 0.1 fusion.28
  1.5 16.3 %collective-permute-start.1 = (bf16[256,512]{1,0:T(8,128)(2,1)S(1)}, bf16[256,512]{1,0:T(8,128)(2,1)S(1)}, u32[]{:S(2)}, u32[]{:S(2)}) collective-permute-start(bf16[256,512]{1,0:T(8,128)(2,1)S(1)} %fusion.28), channel_id=1, source_target_pairs={{0,2},{2,0},{1,3},{3,1},{4,6},{6,4},{5,7},{7,5},{8,10},{10,8},{9,1... | collective-permute-start | bytes 786440 | tf_op jit(solution)/shard_map/ppermute | solution.py:157
  17.8 0.0 copy-done.9
  17.8 0.3 convolution_convert_fusion.3
  18.1 2.9 %collective-permute-start = (bf16[256,512]{1,0:T(8,128)(2,1)S(1)}, bf16[256,512]{1,0:T(8,128)(2,1)S(1)}, u32[]{:S(2)}, u32[]{:S(2)}) collective-permute-start(bf16[256,512]{1,0:T(8,128)(2,1)S(1)} %convolution_convert_fusion.3), channel_id=1, source_target_pairs={{0,1},{1,0},{2,3},{3,2},{4,5},{5,4},{6,7},{7,6},{8,9},{9,8},{10,11... | collective-permute-start | bytes 786440 | tf_op jit(solution)/shard_map/ppermute | solution.py:159
  21.0 3.2 %collective-permute-start.5 = (bf16[256,512]{1,0:T(8,128)(2,1)S(1)}, bf16[256,512]{1,0:T(8,128)(2,1)S(1)}, u32[]{:S(2)}, u32[]{:S(2)}) collective-permute-start(bf16[256,512]{1,0:T(8,128)(2,1)S(1)} %fusion.28), channel_id=1, source_target_pairs={{0,4},{4,8},{8,12},{12,0},{1,5},{5,9},{9,13},{13,1},{2,6},{6,10},{... | collective-permute-start | bytes 786440 | tf_op jit(solution)/shard_map/ppermute | solution.py:122
  24.2 4.5 %collective-permute-start.6 = (bf16[256,512]{1,0:T(8,128)(2,1)S(1)}, bf16[256,512]{1,0:T(8,128)(2,1)S(1)}, u32[]{:S(2)}, u32[]{:S(2)}) collective-permute-start(bf16[256,512]{1,0:T(8,128)(2,1)S(1)} %fusion.28), channel_id=1, source_target_pairs={{0,8},{4,12},{8,0},{12,4},{1,9},{5,13},{9,1},{13,5},{2,10},{6,14},... | collective-permute-start | bytes 786440 | tf_op jit(solution)/shard_map/ppermute | solution.py:122
  28.7 3.0 %collective-permute-start.7 = (bf16[256,512]{1,0:T(8,128)(2,1)S(1)}, bf16[256,512]{1,0:T(8,128)(2,1)S(1)}, u32[]{:S(2)}, u32[]{:S(2)}) collective-permute-start(bf16[256,512]{1,0:T(8,128)(2,1)S(1)} %fusion.28), channel_id=1, source_target_pairs={{0,12},{4,0},{8,4},{12,8},{1,13},{5,1},{9,5},{13,9},{2,14},{6,2},{... | collective-permute-start | bytes 786440 | tf_op jit(solution)/shard_map/ppermute | solution.py:122
  31.7 0.0 collective-permute-done.1
  31.7 2.3 %collective-permute-start.2 = (bf16[256,512]{1,0:T(8,128)(2,1)S(1)}, bf16[256,512]{1,0:T(8,128)(2,1)S(1)}, u32[]{:S(2)}, u32[]{:S(2)}) collective-permute-start(bf16[256,512]{1,0:T(8,128)(2,1)S(1)} %collective-permute-done.1), channel_id=1, source_target_pairs={{0,4},{4,8},{8,12},{12,0},{1,5},{5,9},{9,13},{13,1},{2,6},{6,10},{... | collective-permute-start | bytes 786440 | tf_op jit(solution)/shard_map/ppermute | solution.py:122
  34.0 0.0 collective-permute-done
  34.1 2.7 %collective-permute-start.3 = (bf16[256,512]{1,0:T(8,128)(2,1)S(1)}, bf16[256,512]{1,0:T(8,128)(2,1)S(1)}, u32[]{:S(2)}, u32[]{:S(2)}) collective-permute-start(bf16[256,512]{1,0:T(8,128)(2,1)S(1)} %collective-permute-done.1), channel_id=1, source_target_pairs={{0,8},{4,12},{8,0},{12,4},{1,9},{5,13},{9,1},{13,5},{2,10},{6,14},... | collective-permute-start | bytes 786440 | tf_op jit(solution)/shard_map/ppermute | solution.py:122
  36.8 0.0 collective-permute-done.5
  36.8 3.5 %collective-permute-start.4 = (bf16[256,512]{1,0:T(8,128)(2,1)S(1)}, bf16[256,512]{1,0:T(8,128)(2,1)S(1)}, u32[]{:S(2)}, u32[]{:S(2)}) collective-permute-start(bf16[256,512]{1,0:T(8,128)(2,1)S(1)} %collective-permute-done.1), channel_id=1, source_target_pairs={{0,12},{4,0},{8,4},{12,8},{1,13},{5,1},{9,5},{13,9},{2,14},{6,2},{... | collective-permute-start | bytes 786440 | tf_op jit(solution)/shard_map/ppermute | solution.py:122
  40.3 0.0 collective-permute-done.6
  40.4 0.0 collective-permute-done.7
  40.4 1.2 convolution_convert_fusion.1
  41.6 0.2 fusion.44
  41.8 6.1 %shard_map.73 = (f32[512,512]{1,0:T(8,128)S(1)}, f32[512,8]{1,0:T(8,128)S(1)}, f32[512,8]{1,0:T(8,128)S(1)}) custom-call(bf16[512,512]{1,0:T(8,128)(2,1)S(1)} %pad_maximum_fusion.refs_0_, bf16[1024,512]{1,0:T(8,128)(2,1)S(1)} %get-tuple-element.24.refs_1_, bf16[1024,512]{1,0:T(8,128)(2,1)S(1)} %get-tuple-element.23.refs_2_), custom_call_target="tpu_custom_call" | custom-call | tf_op jit(solution)/shard_map/pallas_call | solution.py:73
  47.9 0.0 collective-permute-done.2
  47.9 2.2 %collective-permute-done.3 = bf16[256,512]{1,0:T(8,128)(2,1)S(1)} collective-permute-done((bf16[256,512]{1,0:T(8,128)(2,1)S(1)}, bf16[256,512]{1,0:T(8,128)(2,1)S(1)}, u32[]{:S(2)}, u32[]{:S(2)}) %collective-permute-start.3) | collective-permute-done | bytes 262176 | tf_op jit(solution)/shard_map/ppermute | solution.py:122
  50.0 0.8 collective-permute-done.4
  50.8 1.2 convolution_convert_fusion.2
  52.1 0.2 fusion.45
  52.3 5.2 %shard_map.75 = f32[256,640]{1,0:T(8,128)S(1)} custom-call(bf16[512,512]{1,0:T(8,128)(2,1)S(1)} %pad_maximum_fusion.refs_0_, bf16[1024,512]{1,0:T(8,128)(2,1)S(1)} %get-tuple-element.26.refs_1_, bf16[1024,512]{1,0:T(8,128)(2,1)S(1)} %get-tuple-element.25.refs_2_, f32[512,512]{1,0:T(8,128)S(1)} %get-tuple-element.20.refs_3_, ...), custom_call_target="tpu_custom_call" | custom-call | tf_op jit(solution)/shard_map/pallas_call | solution.py:110
  57.5 3.3 %collective-permute-start.8 = (f32[256,640]{1,0:T(8,128)S(1)}, f32[256,640]{1,0:T(8,128)S(1)}, u32[]{:S(2)}, u32[]{:S(2)}) collective-permute-start(f32[256,640]{1,0:T(8,128)S(1)} %shard_map.75), channel_id=1, source_target_pairs={{0,1},{1,0},{2,3},{3,2},{4,5},{5,4},{6,7},{7,6},{8,9},{9,8},{10,11... | collective-permute-start | bytes 1966088 | tf_op jit(solution)/shard_map/ppermute | solution.py:167
  60.8 5.0 %shard_map.74.refs_0_ = f32[256,640]{1,0:T(8,128)S(1)} custom-call(bf16[512,512]{1,0:T(8,128)(2,1)S(1)} %pad_maximum_fusion.refs_0_, bf16[1024,512]{1,0:T(8,128)(2,1)S(1)} %get-tuple-element.26.refs_1_, bf16[1024,512]{1,0:T(8,128)(2,1)S(1)} %get-tuple-element.25.refs_2_, f32[512,512]{1,0:T(8,128)S(1)} %get-tuple-element.20.refs_3_, ...), custom_call_target="tpu_custom_call" | custom-call | tf_op jit(solution)/shard_map/pallas_call | solution.py:110
  65.9 0.0 copy-start.1
  65.9 0.8 copy-done.1
  66.7 0.0 collective-permute-done.8.refs_1_
  66.8 0.8 copy-done.4
  67.6 3.7 %shard_map.76 = bf16[256,512]{1,0:T(8,128)(2,1)} custom-call(f32[256,640]{1,0:T(8,128)} %copy-done.1, f32[256,640]{1,0:T(8,128)} %copy-done.4), custom_call_target="tpu_custom_call" | custom-call | tf_op jit(solution)/shard_map/pallas_call | solution.py:97
  71.3 0.0 copy-done
  71.3 1.4 %fusion.47 = (f32[256]{0:T(256)S(1)}, f32[256,512]{1,0:T(8,128)S(1)}) fusion(bf16[256,512]{1,0:T(8,128)(2,1)} %shard_map.76, bf16[512,512]{1,0:T(8,128)(2,1)S(1)} %copy-done, bf16[1,256,512]{2,1,0:T(8,128)(2,1)S(1)} %copy-done.3), kind=kOutput, calls=%fused_computation.67 | convolution fusion | flops 134610688 | bytes 1573888 | tf_op jit(solution)/shard_map/dot_general | solution.py:170
  72.8 0.2 multiply_reduce_fusion
  73.0 0.0 copy-done.8
  73.0 0.9 fusion.37
  73.9 18.6 %all-to-all-start = ((bf16[1,32,8,512]{3,2,0,1:T(8,128)(2,1)}), bf16[1,32,8,512]{3,2,0,1:T(8,128)(2,1)S(1)}, u32[]{:S(2)}, u32[]{:S(2)}) async-start(bf16[1,32,8,512]{3,2,0,1:T(8,128)(2,1)} %fusion.37), calls=%async_computation | async-start | bytes 524288 | tf_op jit(solution)/shard_map/all_to_all | solution.py:175
  92.5 0.7 compare_reduce_fusion
  93.2 0.0 copy-done.2
  93.2 0.8 fusion.29
  94.1 17.5 %all-to-all-done = bf16[1,32,8,512]{3,2,0,1:T(8,128)(2,1)S(1)} async-done(((bf16[1,32,8,512]{3,2,0,1:T(8,128)(2,1)}), bf16[1,32,8,512]{3,2,0,1:T(8,128)(2,1)S(1)}, u32[]{:S(2)}, u32[]{:S(2)}) %all-to-all-start) | async-done | bytes 262176 | tf_op jit(solution)/shard_map/all_to_all | solution.py:175
  111.6 0.6 fusion
  112.2 0.1 fusion.46
  112.2 0.3 reshape.102
  112.5 0.3 reshape.103
  112.8 1.1 reshape.101
  113.9 0.9 fusion.48
  114.7 0.3 fusion.19
  115.0 0.0 copy-done.6
  115.0 0.8 fusion.2
  115.8 0.0 copy-start.5
  115.8 0.2 copy.19
  116.0 0.3 convert_element_type.56
  116.3 23.9 %all_to_all.8 = bf16[32,1,8,512]{3,2,1,0:T(8,128)(2,1)S(1)} all-to-all(bf16[32,1,8,512]{3,2,1,0:T(8,128)(2,1)S(1)} %bitcast.45), channel_id=1, replica_groups=mesh['x'=4,'zlo'=8,'y'=4,'zhi'=2,'core'=2] {'x','zlo'}, dimensions={0} | all-to-all | bytes 524288 | tf_op jit(solution)/shard_map/all_to_all | solution.py:185
  140.3 0.0 copy-done.5
  140.3 1.0 fusion.4
  (11 shorter events, 0.1 us)
Async XLA Ops:
  0.0 71.3 %copy-start = (bf16[512,512]{1,0:T(8,128)(2,1)S(1)}, bf16[512,512]{1,0:T(8,128)(2,1)}, u32[]{:S(2)}) copy-start(bf16[512,512]{1,0:T(8,128)(2,1)} %param.12) | copy-start | bytes 1572868
  0.0 1.0 copy-start.3
  0.0 1.4 copy-start.7
  0.0 17.8 %copy-start.9 = (bf16[512,1536]{1,0:T(8,128)(2,1)S(1)}, bf16[512,1536]{1,0:T(8,128)(2,1)}, u32[]{:S(2)}) copy-start(bf16[512,1536]{1,0:T(8,128)(2,1)} %param.11) | copy-start | bytes 4718596
  1.5 30.2 %collective-permute-start.1 = (bf16[256,512]{1,0:T(8,128)(2,1)S(1)}, bf16[256,512]{1,0:T(8,128)(2,1)S(1)}, u32[]{:S(2)}, u32[]{:S(2)}) collective-permute-start(bf16[256,512]{1,0:T(8,128)(2,1)S(1)} %fusion.28), channel_id=1, source_target_pairs={{0,2},{2,0},{1,3},{3,1},{4,6},{6,4},{5,7},{7,5},{8,10},{10,8},{9,1... | collective-permute-start | bytes 786440 | tf_op jit(solution)/shard_map/ppermute | solution.py:157
  18.1 15.9 %collective-permute-start = (bf16[256,512]{1,0:T(8,128)(2,1)S(1)}, bf16[256,512]{1,0:T(8,128)(2,1)S(1)}, u32[]{:S(2)}, u32[]{:S(2)}) collective-permute-start(bf16[256,512]{1,0:T(8,128)(2,1)S(1)} %convolution_convert_fusion.3), channel_id=1, source_target_pairs={{0,1},{1,0},{2,3},{3,2},{4,5},{5,4},{6,7},{7,6},{8,9},{9,8},{10,11... | collective-permute-start | bytes 786440 | tf_op jit(solution)/shard_map/ppermute | solution.py:159
  21.0 15.8 %collective-permute-start.5 = (bf16[256,512]{1,0:T(8,128)(2,1)S(1)}, bf16[256,512]{1,0:T(8,128)(2,1)S(1)}, u32[]{:S(2)}, u32[]{:S(2)}) collective-permute-start(bf16[256,512]{1,0:T(8,128)(2,1)S(1)} %fusion.28), channel_id=1, source_target_pairs={{0,4},{4,8},{8,12},{12,0},{1,5},{5,9},{9,13},{13,1},{2,6},{6,10},{... | collective-permute-start | bytes 786440 | tf_op jit(solution)/shard_map/ppermute | solution.py:122
  24.2 16.2 %collective-permute-start.6 = (bf16[256,512]{1,0:T(8,128)(2,1)S(1)}, bf16[256,512]{1,0:T(8,128)(2,1)S(1)}, u32[]{:S(2)}, u32[]{:S(2)}) collective-permute-start(bf16[256,512]{1,0:T(8,128)(2,1)S(1)} %fusion.28), channel_id=1, source_target_pairs={{0,8},{4,12},{8,0},{12,4},{1,9},{5,13},{9,1},{13,5},{2,10},{6,14},... | collective-permute-start | bytes 786440 | tf_op jit(solution)/shard_map/ppermute | solution.py:122
  28.7 11.6 %collective-permute-start.7 = (bf16[256,512]{1,0:T(8,128)(2,1)S(1)}, bf16[256,512]{1,0:T(8,128)(2,1)S(1)}, u32[]{:S(2)}, u32[]{:S(2)}) collective-permute-start(bf16[256,512]{1,0:T(8,128)(2,1)S(1)} %fusion.28), channel_id=1, source_target_pairs={{0,12},{4,0},{8,4},{12,8},{1,13},{5,1},{9,5},{13,9},{2,14},{6,2},{... | collective-permute-start | bytes 786440 | tf_op jit(solution)/shard_map/ppermute | solution.py:122
  31.7 16.1 %collective-permute-start.2 = (bf16[256,512]{1,0:T(8,128)(2,1)S(1)}, bf16[256,512]{1,0:T(8,128)(2,1)S(1)}, u32[]{:S(2)}, u32[]{:S(2)}) collective-permute-start(bf16[256,512]{1,0:T(8,128)(2,1)S(1)} %collective-permute-done.1), channel_id=1, source_target_pairs={{0,4},{4,8},{8,12},{12,0},{1,5},{5,9},{9,13},{13,1},{2,6},{6,10},{... | collective-permute-start | bytes 786440 | tf_op jit(solution)/shard_map/ppermute | solution.py:122
  34.1 16.0 %collective-permute-start.3 = (bf16[256,512]{1,0:T(8,128)(2,1)S(1)}, bf16[256,512]{1,0:T(8,128)(2,1)S(1)}, u32[]{:S(2)}, u32[]{:S(2)}) collective-permute-start(bf16[256,512]{1,0:T(8,128)(2,1)S(1)} %collective-permute-done.1), channel_id=1, source_target_pairs={{0,8},{4,12},{8,0},{12,4},{1,9},{5,13},{9,1},{13,5},{2,10},{6,14},... | collective-permute-start | bytes 786440 | tf_op jit(solution)/shard_map/ppermute | solution.py:122
  36.8 14.0 %collective-permute-start.4 = (bf16[256,512]{1,0:T(8,128)(2,1)S(1)}, bf16[256,512]{1,0:T(8,128)(2,1)S(1)}, u32[]{:S(2)}, u32[]{:S(2)}) collective-permute-start(bf16[256,512]{1,0:T(8,128)(2,1)S(1)} %collective-permute-done.1), channel_id=1, source_target_pairs={{0,12},{4,0},{8,4},{12,8},{1,13},{5,1},{9,5},{13,9},{2,14},{6,2},{... | collective-permute-start | bytes 786440 | tf_op jit(solution)/shard_map/ppermute | solution.py:122
  57.5 9.3 %collective-permute-start.8 = (f32[256,640]{1,0:T(8,128)S(1)}, f32[256,640]{1,0:T(8,128)S(1)}, u32[]{:S(2)}, u32[]{:S(2)}) collective-permute-start(f32[256,640]{1,0:T(8,128)S(1)} %shard_map.75), channel_id=1, source_target_pairs={{0,1},{1,0},{2,3},{3,2},{4,5},{5,4},{6,7},{7,6},{8,9},{9,8},{10,11... | collective-permute-start | bytes 1966088 | tf_op jit(solution)/shard_map/ppermute | solution.py:167
  65.9 0.8 copy-start.1
  66.7 6.3 %copy-start.8 = (f32[512]{0:T(512)S(1)}, f32[512]{0:T(512)}, u32[]{:S(2)}) copy-start(f32[512]{0:T(512)} %param.13) | copy-start | bytes 6148
  66.7 0.8 copy-start.4
  71.3 21.9 %copy-start.2 = (bf16[512,1536]{1,0:T(8,128)(2,1)S(1)}, bf16[512,1536]{1,0:T(8,128)(2,1)}, u32[]{:S(2)}) copy-start(bf16[512,1536]{1,0:T(8,128)(2,1)} %param.14) | copy-start | bytes 4718596
  73.9 37.7 %all-to-all-start = ((bf16[1,32,8,512]{3,2,0,1:T(8,128)(2,1)}), bf16[1,32,8,512]{3,2,0,1:T(8,128)(2,1)S(1)}, u32[]{:S(2)}, u32[]{:S(2)}) async-start(bf16[1,32,8,512]{3,2,0,1:T(8,128)(2,1)} %fusion.37), calls=%async_computation | async-start | bytes 524288 | tf_op jit(solution)/shard_map/all_to_all | solution.py:175
  113.9 1.2 copy-start.6
  115.8 24.5 %copy-start.5 = (bf16[512,512]{1,0:T(8,128)(2,1)S(1)}, bf16[512,512]{1,0:T(8,128)(2,1)}, u32[]{:S(2)}) copy-start(bf16[512,512]{1,0:T(8,128)(2,1)} %param.15) | copy-start | bytes 1572868

commit v6 on v5

--- a/solution.py
+++ b/solution.py
@@ -77,26 +77,42 @@
     )(query, keys, values, *state)
 
 
-def combine_kernel(a_ref, b_ref, out_ref, *, size):
+def final_kernel(q_ref, k_ref, v_ref, o1_ref, m1_ref, l1_ref, t_ref, out_ref, *, size, rows):
     width = HEADS * size
     for h in range(HEADS):
         cols = slice(h * size, (h + 1) * size)
-        m1, m2 = a_ref[:, width + h : width + h + 1], b_ref[:, width + h : width + h + 1]
-        l1 = a_ref[:, width + STATS + h : width + STATS + h + 1]
-        l2 = b_ref[:, width + STATS + h : width + STATS + h + 1]
-        top = jnp.maximum(m1, m2)
-        f1, f2 = jnp.exp(m1 - top), jnp.exp(m2 - top)
-        summed = a_ref[:, cols] * f1 + b_ref[:, cols] * f2
-        out_ref[:, cols] = (summed / (l1 * f1 + l2 * f2)).astype(out_ref.dtype)
-
-
-def combine(own, theirs):
-    count, packed = own.shape
-    width = packed - 2 * STATS
-    body = lambda *refs: combine_kernel(*refs, size=width // HEADS)
-    return pl.pallas_call(body, out_shape=jax.ShapeDtypeStruct((count, width), jnp.bfloat16))(
-        own, theirs
-    )
+        scores = lax.dot_general(
+            q_ref[rows, cols], k_ref[:, cols], (((1,), (1,)), ((), ())),
+            preferred_element_type=jnp.float32,
+        )
+        before = m1_ref[rows, h : h + 1]
+        theirs = t_ref[:, width + h : width + h + 1]
+        top = jnp.maximum(jnp.maximum(before, theirs), jnp.max(scores, axis=1, keepdims=True))
+        weights = jnp.exp(scores - top)
+        fade, their_fade = jnp.exp(before - top), jnp.exp(theirs - top)
+        total = (
+            l1_ref[rows, h : h + 1] * fade
+            + t_ref[:, width + STATS + h : width + STATS + h + 1] * their_fade
+            + jnp.sum(weights, axis=1, keepdims=True)
+        )
+        summed = (
+            o1_ref[rows, cols] * fade
+            + t_ref[:, cols] * their_fade
+            + jnp.dot(weights.astype(jnp.bfloat16), v_ref[:, cols], preferred_element_type=jnp.float32)
+        )
+        out_ref[:, cols] = (summed / total).astype(out_ref.dtype)
+
+
+def spatial_final(query, keys, values, state, theirs, start, count):
+    width = query.shape[1]
+    body = lambda *refs: final_kernel(
+        *refs, size=width // HEADS, rows=slice(start, start + count)
+    )
+    return pl.pallas_call(
+        body,
+        out_shape=jax.ShapeDtypeStruct((count, width), jnp.bfloat16),
+        compiler_params=pltpu.CompilerParams(vmem_limit_bytes=48 * 1024 * 1024),
+    )(query, keys, values, *state, theirs)
 
 
 def spatial_partial(query, keys, values):
@@ -165,8 +181,7 @@
     far = jnp.dot(far_rows, w_pairs, preferred_element_type=jnp.float32).astype(jnp.bfloat16)
     theirs = spatial_merge(both, far[:, :width], far[:, width:], state, 0, count)
     theirs = lax.ppermute(theirs, "core", swap)
-    own = spatial_merge(both, far[:, :width], far[:, width:], state, count, count)
-    context = combine(own, theirs)
+    context = spatial_final(both, far[:, :width], far[:, width:], state, theirs, count, count)
     after = resid + jnp.dot(context, w_spatial_out, preferred_element_type=jnp.float32)
     second = layer_norm(after, norm_temporal).astype(jnp.bfloat16)
     owners = lax.axis_size(("x", "zlo"))

time: 143 us -> 140 us (0.979)
  Pallas kernels: 20.1 us -> 18.4 us
  local copies, waits for them, and re-layouts: 5.23 us -> 3.61 us
  waiting for transfers between devices: 20.5 us -> 22 us
    pallas_call x2 -> x1, Pallas kernels: 10.3 us -> 5.24 us  [spatial_merge(): pl.pallas_call(body, out_shape=jax.ShapeDtypeStruct((count, width + 2 * S...]
    pallas_call x1, Pallas kernels: 3.74 us -> 7.09 us  [spatial_final(): pl.pallas_call(body, out_shape=jax.ShapeDtypeStruct((count, width), jnp.b...]
    ppermute x1, waiting for transfers between devices: 0.01 us -> 1.7 us  [layer(): theirs = lax.ppermute(theirs, 'core', swap)]
    unnamed x20 -> x16, local copies, waits for them, and re-layouts: 2.7 us -> 1.07 us
  transfers between devices with their start and end apart: 10 -> 10, of which waited for: 3 -> 4; matrix products, arithmetic and copies ran while one was open for 2% -> 2% of each run, Pallas kernels for 8% -> 4%
where the time goes in v6:
time: 140 us; the launch traced here: 138 us
  starting transfers between devices  60.3 us (43%)
  blocking collectives  23.9 us (17%)
  waiting for transfers between devices  22 us (16%)
  Pallas kernels  18.4 us (13%)
  matrix products  6.38 us (5%)
  local copies, waits for them, and re-layouts  3.61 us (3%)
  other arithmetic  3.28 us (2%)
    all_to_all x1, blocking collectives, layer(): lax.all_to_all(context_t, ('x', 'zlo'), split_axis=0, concat_axis=1, tile...  23.9 us
    ppermute x6, starting transfers between devices, spread_y(): pieces.append(lax.ppermute(rows, 'y', pairs))  19.2 us
    all_to_all x1, starting transfers between devices, layer(): lax.all_to_all(second, ('x', 'zlo'), split_axis=1, concat_axis=0, tiled=T...  18.6 us
    all_to_all x1, waiting for transfers between devices, layer(): lax.all_to_all(second, ('x', 'zlo'), split_axis=1, concat_axis=0, tiled=T...  17.4 us
    ppermute x1, starting transfers between devices, layer(): partner = lax.ppermute(normed, 'zhi', [(0, 1), (1, 0)])  16.3 us
    pallas_call x1, Pallas kernels, spatial_final(): pl.pallas_call(body, out_shape=jax.ShapeDtypeStruct((count, width), jnp.b...  7.09 us
    pallas_call x1, Pallas kernels, _attention_call(): pl.pallas_call(body, out_shape=shapes, compiler_params=pltpu.CompilerPara...  6.07 us
    pallas_call x1, Pallas kernels, spatial_merge(): pl.pallas_call(body, out_shape=jax.ShapeDtypeStruct((count, width + 2 * S...  5.24 us
  transfers between devices with their start and end apart: 10, of which 4 were waited for; matrix products, arithmetic and copies ran while one was open for 2% of the time, Pallas kernels for 4%

profile of v6, /device:TPU:1, one launch (start us, length us, event | category | flops | bytes accessed | tf_op | source)
XLA Modules:
  0.0 138.3 jit_solution(9670482276793550691)
XLA Ops:
  0.0 0.0 copy-start
  0.0 0.0 copy-start.2
  0.0 0.0 copy-start.5
  0.0 0.0 copy-start.7
  0.0 1.0 copy-done.2
  1.0 0.1 convert_reduce_fusion
  1.1 0.2 fusion.26
  1.4 0.0 copy-done.5
  1.4 0.1 fusion.28
  1.5 16.3 %collective-permute-start.1 = (bf16[256,512]{1,0:T(8,128)(2,1)S(1)}, bf16[256,512]{1,0:T(8,128)(2,1)S(1)}, u32[]{:S(2)}, u32[]{:S(2)}) collective-permute-start(bf16[256,512]{1,0:T(8,128)(2,1)S(1)} %fusion.28), channel_id=1, source_target_pairs={{0,2},{2,0},{1,3},{3,1},{4,6},{6,4},{5,7},{7,5},{8,10},{10,8},{9,1... | collective-permute-start | bytes 786440 | tf_op jit(solution)/shard_map/ppermute | solution.py:173
  17.8 0.0 copy-done.7
  17.8 0.3 convolution_convert_fusion.3
  18.1 2.9 %collective-permute-start = (bf16[256,512]{1,0:T(8,128)(2,1)S(1)}, bf16[256,512]{1,0:T(8,128)(2,1)S(1)}, u32[]{:S(2)}, u32[]{:S(2)}) collective-permute-start(bf16[256,512]{1,0:T(8,128)(2,1)S(1)} %convolution_convert_fusion.3), channel_id=1, source_target_pairs={{0,1},{1,0},{2,3},{3,2},{4,5},{5,4},{6,7},{7,6},{8,9},{9,8},{10,11... | collective-permute-start | bytes 786440 | tf_op jit(solution)/shard_map/ppermute | solution.py:175
  21.0 3.2 %collective-permute-start.5 = (bf16[256,512]{1,0:T(8,128)(2,1)S(1)}, bf16[256,512]{1,0:T(8,128)(2,1)S(1)}, u32[]{:S(2)}, u32[]{:S(2)}) collective-permute-start(bf16[256,512]{1,0:T(8,128)(2,1)S(1)} %fusion.28), channel_id=1, source_target_pairs={{0,4},{4,8},{8,12},{12,0},{1,5},{5,9},{9,13},{13,1},{2,6},{6,10},{... | collective-permute-start | bytes 786440 | tf_op jit(solution)/shard_map/ppermute | solution.py:138
  24.2 4.5 %collective-permute-start.6 = (bf16[256,512]{1,0:T(8,128)(2,1)S(1)}, bf16[256,512]{1,0:T(8,128)(2,1)S(1)}, u32[]{:S(2)}, u32[]{:S(2)}) collective-permute-start(bf16[256,512]{1,0:T(8,128)(2,1)S(1)} %fusion.28), channel_id=1, source_target_pairs={{0,8},{4,12},{8,0},{12,4},{1,9},{5,13},{9,1},{13,5},{2,10},{6,14},... | collective-permute-start | bytes 786440 | tf_op jit(solution)/shard_map/ppermute | solution.py:138
  28.7 3.0 %collective-permute-start.7 = (bf16[256,512]{1,0:T(8,128)(2,1)S(1)}, bf16[256,512]{1,0:T(8,128)(2,1)S(1)}, u32[]{:S(2)}, u32[]{:S(2)}) collective-permute-start(bf16[256,512]{1,0:T(8,128)(2,1)S(1)} %fusion.28), channel_id=1, source_target_pairs={{0,12},{4,0},{8,4},{12,8},{1,13},{5,1},{9,5},{13,9},{2,14},{6,2},{... | collective-permute-start | bytes 786440 | tf_op jit(solution)/shard_map/ppermute | solution.py:138
  31.7 0.0 collective-permute-done.1
  31.7 2.3 %collective-permute-start.2 = (bf16[256,512]{1,0:T(8,128)(2,1)S(1)}, bf16[256,512]{1,0:T(8,128)(2,1)S(1)}, u32[]{:S(2)}, u32[]{:S(2)}) collective-permute-start(bf16[256,512]{1,0:T(8,128)(2,1)S(1)} %collective-permute-done.1), channel_id=1, source_target_pairs={{0,4},{4,8},{8,12},{12,0},{1,5},{5,9},{9,13},{13,1},{2,6},{6,10},{... | collective-permute-start | bytes 786440 | tf_op jit(solution)/shard_map/ppermute | solution.py:138
  34.0 0.0 collective-permute-done
  34.1 2.7 %collective-permute-start.3 = (bf16[256,512]{1,0:T(8,128)(2,1)S(1)}, bf16[256,512]{1,0:T(8,128)(2,1)S(1)}, u32[]{:S(2)}, u32[]{:S(2)}) collective-permute-start(bf16[256,512]{1,0:T(8,128)(2,1)S(1)} %collective-permute-done.1), channel_id=1, source_target_pairs={{0,8},{4,12},{8,0},{12,4},{1,9},{5,13},{9,1},{13,5},{2,10},{6,14},... | collective-permute-start | bytes 786440 | tf_op jit(solution)/shard_map/ppermute | solution.py:138
  36.8 0.0 collective-permute-done.5
  36.8 3.5 %collective-permute-start.4 = (bf16[256,512]{1,0:T(8,128)(2,1)S(1)}, bf16[256,512]{1,0:T(8,128)(2,1)S(1)}, u32[]{:S(2)}, u32[]{:S(2)}) collective-permute-start(bf16[256,512]{1,0:T(8,128)(2,1)S(1)} %collective-permute-done.1), channel_id=1, source_target_pairs={{0,12},{4,0},{8,4},{12,8},{1,13},{5,1},{9,5},{13,9},{2,14},{6,2},{... | collective-permute-start | bytes 786440 | tf_op jit(solution)/shard_map/ppermute | solution.py:138
  40.3 0.0 collective-permute-done.6
  40.4 0.0 collective-permute-done.7
  40.4 1.2 convolution_convert_fusion.1
  41.6 0.2 fusion.44
  41.8 6.1 %shard_map.73 = (f32[512,512]{1,0:T(8,128)S(1)}, f32[512,8]{1,0:T(8,128)S(1)}, f32[512,8]{1,0:T(8,128)S(1)}) custom-call(bf16[512,512]{1,0:T(8,128)(2,1)S(1)} %pad_maximum_fusion.refs_0_, bf16[1024,512]{1,0:T(8,128)(2,1)S(1)} %get-tuple-element.24.refs_1_, bf16[1024,512]{1,0:T(8,128)(2,1)S(1)} %get-tuple-element.23.refs_2_), custom_call_target="tpu_custom_call" | custom-call | tf_op jit(solution)/shard_map/pallas_call | solution.py:73
  47.9 0.0 collective-permute-done.2
  47.9 2.2 %collective-permute-done.3 = bf16[256,512]{1,0:T(8,128)(2,1)S(1)} collective-permute-done((bf16[256,512]{1,0:T(8,128)(2,1)S(1)}, bf16[256,512]{1,0:T(8,128)(2,1)S(1)}, u32[]{:S(2)}, u32[]{:S(2)}) %collective-permute-start.3) | collective-permute-done | bytes 262176 | tf_op jit(solution)/shard_map/ppermute | solution.py:138
  50.0 0.8 collective-permute-done.4
  50.8 1.2 convolution_convert_fusion.2
  52.1 0.2 fusion.45
  52.3 5.2 %shard_map.74 = f32[256,640]{1,0:T(8,128)S(1)} custom-call(bf16[512,512]{1,0:T(8,128)(2,1)S(1)} %pad_maximum_fusion.refs_0_, bf16[1024,512]{1,0:T(8,128)(2,1)S(1)} %get-tuple-element.26.refs_1_, bf16[1024,512]{1,0:T(8,128)(2,1)S(1)} %get-tuple-element.25.refs_2_, f32[512,512]{1,0:T(8,128)S(1)} %get-tuple-element.20.refs_3_, ...), custom_call_target="tpu_custom_call" | custom-call | tf_op jit(solution)/shard_map/pallas_call | solution.py:126
  57.5 3.3 %collective-permute-start.8 = (f32[256,640]{1,0:T(8,128)S(1)}, f32[256,640]{1,0:T(8,128)S(1)}, u32[]{:S(2)}, u32[]{:S(2)}) collective-permute-start(f32[256,640]{1,0:T(8,128)S(1)} %shard_map.74), channel_id=1, source_target_pairs={{0,1},{1,0},{2,3},{3,2},{4,5},{5,4},{6,7},{7,6},{8,9},{9,8},{10,11... | collective-permute-start | bytes 1966088 | tf_op jit(solution)/shard_map/ppermute | solution.py:183
  60.8 1.7 %collective-permute-done.8.refs_6_ = f32[256,640]{1,0:T(8,128)S(1)} collective-permute-done((f32[256,640]{1,0:T(8,128)S(1)}, f32[256,640]{1,0:T(8,128)S(1)}, u32[]{:S(2)}, u32[]{:S(2)}) %collective-permute-start.8) | collective-permute-done | bytes 655392 | tf_op jit(solution)/shard_map/ppermute | solution.py:183
  62.6 7.1 %shard_map.75 = bf16[256,512]{1,0:T(8,128)(2,1)S(1)} custom-call(bf16[512,512]{1,0:T(8,128)(2,1)S(1)} %pad_maximum_fusion.refs_0_, bf16[1024,512]{1,0:T(8,128)(2,1)S(1)} %get-tuple-element.26.refs_1_, bf16[1024,512]{1,0:T(8,128)(2,1)S(1)} %get-tuple-element.25.refs_2_, f32[512,512]{1,0:T(8,128)S(1)} %get-tuple-element.20.refs_3_, ...), custom_call_target="tpu_custom_call" | custom-call | tf_op jit(solution)/shard_map/pallas_call | solution.py:111
  69.6 0.0 copy-done
  69.7 0.0 copy-start.6
  69.7 0.0 copy-start.1
  69.7 0.4 fusion.47
  70.1 0.2 multiply_reduce_fusion
  70.3 0.0 copy-done.6
  70.3 0.9 fusion.37
  71.2 18.6 %all-to-all-start = ((bf16[1,32,8,512]{3,2,0,1:T(8,128)(2,1)}), bf16[1,32,8,512]{3,2,0,1:T(8,128)(2,1)S(1)}, u32[]{:S(2)}, u32[]{:S(2)}) async-start(bf16[1,32,8,512]{3,2,0,1:T(8,128)(2,1)} %fusion.37), calls=%async_computation | async-start | bytes 524288 | tf_op jit(solution)/shard_map/all_to_all | solution.py:190
  89.8 0.6 compare_reduce_fusion
  90.5 0.0 copy-done.1
  90.5 0.8 fusion.29
  91.2 17.4 %all-to-all-done = bf16[1,32,8,512]{3,2,0,1:T(8,128)(2,1)S(1)} async-done(((bf16[1,32,8,512]{3,2,0,1:T(8,128)(2,1)}), bf16[1,32,8,512]{3,2,0,1:T(8,128)(2,1)S(1)}, u32[]{:S(2)}, u32[]{:S(2)}) %all-to-all-start) | async-done | bytes 262176 | tf_op jit(solution)/shard_map/all_to_all | solution.py:190
  108.6 0.6 fusion
  109.2 0.1 fusion.46
  109.2 0.3 reshape.102
  109.5 0.3 reshape.103
  109.8 1.1 reshape.101
  110.9 0.0 copy-start.4
  110.9 0.9 fusion.48
  111.8 0.3 fusion.19
  112.1 0.0 copy-done.4
  112.1 0.8 fusion.2
  112.8 0.0 copy-start.3
  112.8 0.2 copy.19
  113.0 0.3 convert_element_type.56
  113.4 23.9 %all_to_all.8 = bf16[32,1,8,512]{3,2,1,0:T(8,128)(2,1)S(1)} all-to-all(bf16[32,1,8,512]{3,2,1,0:T(8,128)(2,1)S(1)} %bitcast.45), channel_id=1, replica_groups=mesh['x'=4,'zlo'=8,'y'=4,'zhi'=2,'core'=2] {'x','zlo'}, dimensions={0} | all-to-all | bytes 524288 | tf_op jit(solution)/shard_map/all_to_all | solution.py:200
  137.3 0.0 copy-done.3
  137.3 1.0 fusion.4
  (6 shorter events, 0.1 us)
Async XLA Ops:
  0.0 69.7 %copy-start = (bf16[512,512]{1,0:T(8,128)(2,1)S(1)}, bf16[512,512]{1,0:T(8,128)(2,1)}, u32[]{:S(2)}) copy-start(bf16[512,512]{1,0:T(8,128)(2,1)} %param.12) | copy-start | bytes 1572868
  0.0 1.0 copy-start.2
  0.0 1.4 copy-start.5
  0.0 17.8 %copy-start.7 = (bf16[512,1536]{1,0:T(8,128)(2,1)S(1)}, bf16[512,1536]{1,0:T(8,128)(2,1)}, u32[]{:S(2)}) copy-start(bf16[512,1536]{1,0:T(8,128)(2,1)} %param.11) | copy-start | bytes 4718596
  1.5 30.2 %collective-permute-start.1 = (bf16[256,512]{1,0:T(8,128)(2,1)S(1)}, bf16[256,512]{1,0:T(8,128)(2,1)S(1)}, u32[]{:S(2)}, u32[]{:S(2)}) collective-permute-start(bf16[256,512]{1,0:T(8,128)(2,1)S(1)} %fusion.28), channel_id=1, source_target_pairs={{0,2},{2,0},{1,3},{3,1},{4,6},{6,4},{5,7},{7,5},{8,10},{10,8},{9,1... | collective-permute-start | bytes 786440 | tf_op jit(solution)/shard_map/ppermute | solution.py:173
  18.1 15.9 %collective-permute-start = (bf16[256,512]{1,0:T(8,128)(2,1)S(1)}, bf16[256,512]{1,0:T(8,128)(2,1)S(1)}, u32[]{:S(2)}, u32[]{:S(2)}) collective-permute-start(bf16[256,512]{1,0:T(8,128)(2,1)S(1)} %convolution_convert_fusion.3), channel_id=1, source_target_pairs={{0,1},{1,0},{2,3},{3,2},{4,5},{5,4},{6,7},{7,6},{8,9},{9,8},{10,11... | collective-permute-start | bytes 786440 | tf_op jit(solution)/shard_map/ppermute | solution.py:175
  21.0 15.8 %collective-permute-start.5 = (bf16[256,512]{1,0:T(8,128)(2,1)S(1)}, bf16[256,512]{1,0:T(8,128)(2,1)S(1)}, u32[]{:S(2)}, u32[]{:S(2)}) collective-permute-start(bf16[256,512]{1,0:T(8,128)(2,1)S(1)} %fusion.28), channel_id=1, source_target_pairs={{0,4},{4,8},{8,12},{12,0},{1,5},{5,9},{9,13},{13,1},{2,6},{6,10},{... | collective-permute-start | bytes 786440 | tf_op jit(solution)/shard_map/ppermute | solution.py:138
  24.2 16.2 %collective-permute-start.6 = (bf16[256,512]{1,0:T(8,128)(2,1)S(1)}, bf16[256,512]{1,0:T(8,128)(2,1)S(1)}, u32[]{:S(2)}, u32[]{:S(2)}) collective-permute-start(bf16[256,512]{1,0:T(8,128)(2,1)S(1)} %fusion.28), channel_id=1, source_target_pairs={{0,8},{4,12},{8,0},{12,4},{1,9},{5,13},{9,1},{13,5},{2,10},{6,14},... | collective-permute-start | bytes 786440 | tf_op jit(solution)/shard_map/ppermute | solution.py:138
  28.7 11.6 %collective-permute-start.7 = (bf16[256,512]{1,0:T(8,128)(2,1)S(1)}, bf16[256,512]{1,0:T(8,128)(2,1)S(1)}, u32[]{:S(2)}, u32[]{:S(2)}) collective-permute-start(bf16[256,512]{1,0:T(8,128)(2,1)S(1)} %fusion.28), channel_id=1, source_target_pairs={{0,12},{4,0},{8,4},{12,8},{1,13},{5,1},{9,5},{13,9},{2,14},{6,2},{... | collective-permute-start | bytes 786440 | tf_op jit(solution)/shard_map/ppermute | solution.py:138
  31.7 16.1 %collective-permute-start.2 = (bf16[256,512]{1,0:T(8,128)(2,1)S(1)}, bf16[256,512]{1,0:T(8,128)(2,1)S(1)}, u32[]{:S(2)}, u32[]{:S(2)}) collective-permute-start(bf16[256,512]{1,0:T(8,128)(2,1)S(1)} %collective-permute-done.1), channel_id=1, source_target_pairs={{0,4},{4,8},{8,12},{12,0},{1,5},{5,9},{9,13},{13,1},{2,6},{6,10},{... | collective-permute-start | bytes 786440 | tf_op jit(solution)/shard_map/ppermute | solution.py:138
  34.1 16.0 %collective-permute-start.3 = (bf16[256,512]{1,0:T(8,128)(2,1)S(1)}, bf16[256,512]{1,0:T(8,128)(2,1)S(1)}, u32[]{:S(2)}, u32[]{:S(2)}) collective-permute-start(bf16[256,512]{1,0:T(8,128)(2,1)S(1)} %collective-permute-done.1), channel_id=1, source_target_pairs={{0,8},{4,12},{8,0},{12,4},{1,9},{5,13},{9,1},{13,5},{2,10},{6,14},... | collective-permute-start | bytes 786440 | tf_op jit(solution)/shard_map/ppermute | solution.py:138
  36.8 14.0 %collective-permute-start.4 = (bf16[256,512]{1,0:T(8,128)(2,1)S(1)}, bf16[256,512]{1,0:T(8,128)(2,1)S(1)}, u32[]{:S(2)}, u32[]{:S(2)}) collective-permute-start(bf16[256,512]{1,0:T(8,128)(2,1)S(1)} %collective-permute-done.1), channel_id=1, source_target_pairs={{0,12},{4,0},{8,4},{12,8},{1,13},{5,1},{9,5},{13,9},{2,14},{6,2},{... | collective-permute-start | bytes 786440 | tf_op jit(solution)/shard_map/ppermute | solution.py:138
  57.5 5.1 %collective-permute-start.8 = (f32[256,640]{1,0:T(8,128)S(1)}, f32[256,640]{1,0:T(8,128)S(1)}, u32[]{:S(2)}, u32[]{:S(2)}) collective-permute-start(f32[256,640]{1,0:T(8,128)S(1)} %shard_map.74), channel_id=1, source_target_pairs={{0,1},{1,0},{2,3},{3,2},{4,5},{5,4},{6,7},{7,6},{8,9},{9,8},{10,11... | collective-permute-start | bytes 1966088 | tf_op jit(solution)/shard_map/ppermute | solution.py:183
  69.7 0.7 copy-start.6
  69.7 20.8 %copy-start.1 = (bf16[512,1536]{1,0:T(8,128)(2,1)S(1)}, bf16[512,1536]{1,0:T(8,128)(2,1)}, u32[]{:S(2)}) copy-start(bf16[512,1536]{1,0:T(8,128)(2,1)} %param.14) | copy-start | bytes 4718596
  71.2 37.4 %all-to-all-start = ((bf16[1,32,8,512]{3,2,0,1:T(8,128)(2,1)}), bf16[1,32,8,512]{3,2,0,1:T(8,128)(2,1)S(1)}, u32[]{:S(2)}, u32[]{:S(2)}) async-start(bf16[1,32,8,512]{3,2,0,1:T(8,128)(2,1)} %fusion.37), calls=%async_computation | async-start | bytes 524288 | tf_op jit(solution)/shard_map/all_to_all | solution.py:190
  110.9 1.2 copy-start.4
  112.8 24.5 %copy-start.3 = (bf16[512,512]{1,0:T(8,128)(2,1)S(1)}, bf16[512,512]{1,0:T(8,128)(2,1)}, u32[]{:S(2)}) copy-start(bf16[512,512]{1,0:T(8,128)(2,1)} %param.15) | copy-start | bytes 1572868

commit v7 on v6

--- a/solution.py
+++ b/solution.py
@@ -103,13 +103,27 @@
         out_ref[:, cols] = (summed / total).astype(out_ref.dtype)
 
 
+def _whole(array):
+    return pl.BlockSpec(array.shape, lambda i: (0,) * array.ndim)
+
+
+def _row_specs(query, keys, start, count):
+    block = start // count
+    width = query.shape[1]
+    rows = lambda cols: pl.BlockSpec((count, cols), lambda i: (block, 0))
+    return [rows(width), _whole(keys), _whole(keys), rows(width), rows(HEADS), rows(HEADS)]
+
+
 def spatial_final(query, keys, values, state, theirs, start, count):
     width = query.shape[1]
     body = lambda *refs: final_kernel(
-        *refs, size=width // HEADS, rows=slice(start, start + count)
+        *refs, size=width // HEADS, rows=slice(None)
     )
     return pl.pallas_call(
         body,
+        grid=(1,),
+        in_specs=_row_specs(query, keys, start, count) + [_whole(theirs)],
+        out_specs=pl.BlockSpec((count, width), lambda i: (0, 0)),
         out_shape=jax.ShapeDtypeStruct((count, width), jnp.bfloat16),
         compiler_params=pltpu.CompilerParams(vmem_limit_bytes=48 * 1024 * 1024),
     )(query, keys, values, *state, theirs)
@@ -122,9 +136,12 @@
 def spatial_merge(query, keys, values, state, start, count):
     width = query.shape[1]
     size = width // HEADS
-    body = lambda *refs: merge_kernel(*refs, size=size, rows=slice(start, start + count))
+    body = lambda *refs: merge_kernel(*refs, size=size, rows=slice(None))
     return pl.pallas_call(
         body,
+        grid=(1,),
+        in_specs=_row_specs(query, keys, start, count),
+        out_specs=pl.BlockSpec((count, width + 2 * STATS), lambda i: (0, 0)),
         out_shape=jax.ShapeDtypeStruct((count, width + 2 * STATS), jnp.float32),
         compiler_params=pltpu.CompilerParams(vmem_limit_bytes=48 * 1024 * 1024),
     )(query, keys, values, *state)
@@ -133,7 +150,7 @@
 def spread_y(rows):
     ring = lax.axis_size("y")
     pieces = [rows]
-    for shift in range(1, ring):
+    for shift in sorted(range(1, ring), key=lambda s: -min(s, ring - s)):
         pairs = [(i, (i + shift) % ring) for i in range(ring)]
         pieces.append(lax.ppermute(rows, "y", pairs))
     return jnp.concatenate(pieces, axis=0)

time: 140 us -> 139 us (level); the launches traced: 138 us -> 139 us
  starting transfers between devices: 60.3 us -> 62.5 us
  waiting for transfers between devices: 22 us -> 20.3 us
    ppermute x6, waiting for transfers between devices: 2.97 us -> 1.23 us  [spread_y(): pieces.append(lax.ppermute(rows, 'y', pairs))]
    ppermute x1, starting transfers between devices: 3.35 us -> 4.81 us  [layer(): theirs = lax.ppermute(theirs, 'core', swap)]
  transfers between devices with their start and end apart: 10 -> 10, of which waited for: 4 -> 3; matrix products, arithmetic and copies ran while one was open for 2% -> 2% of each run, Pallas kernels for 4% -> 4%
where the time goes in v7:
time: 139 us
  starting transfers between devices  62.5 us (45%)
  blocking collectives  23.9 us (17%)
  waiting for transfers between devices  20.3 us (15%)
  Pallas kernels  18.4 us (13%)
  matrix products  6.39 us (5%)
  local copies, waits for them, and re-layouts  3.61 us (3%)
  other arithmetic  3.28 us (2%)
    all_to_all x1, blocking collectives, layer(): lax.all_to_all(context_t, ('x', 'zlo'), split_axis=0, concat_axis=1, tile...  23.9 us
    ppermute x6, starting transfers between devices, spread_y(): pieces.append(lax.ppermute(rows, 'y', pairs))  19.7 us
    all_to_all x1, starting transfers between devices, layer(): lax.all_to_all(second, ('x', 'zlo'), split_axis=1, concat_axis=0, tiled=T...  18.8 us
    all_to_all x1, waiting for transfers between devices, layer(): lax.all_to_all(second, ('x', 'zlo'), split_axis=1, concat_axis=0, tiled=T...  17.4 us
    ppermute x1, starting transfers between devices, layer(): partner = lax.ppermute(normed, 'zhi', [(0, 1), (1, 0)])  16.3 us
    pallas_call x1, Pallas kernels, spatial_final(): pl.pallas_call(body, grid=(1,), in_specs=_row_specs(query, keys, start, c...  7.09 us
    pallas_call x1, Pallas kernels, _attention_call(): pl.pallas_call(body, out_shape=shapes, compiler_params=pltpu.CompilerPara...  6.07 us
    pallas_call x1, Pallas kernels, spatial_merge(): pl.pallas_call(body, grid=(1,), in_specs=_row_specs(query, keys, start, c...  5.25 us
  transfers between devices with their start and end apart: 10, of which 3 were waited for; matrix products, arithmetic and copies ran while one was open for 2% of the time, Pallas kernels for 4%

profile of v7, /device:TPU:1, one launch (start us, length us, event | category | flops | bytes accessed | tf_op | source)
XLA Modules:
  0.0 138.8 jit_solution(5213108619969170975)
XLA Ops:
  0.0 0.0 copy-start
  0.0 0.0 copy-start.2
  0.0 0.0 copy-start.5
  0.0 0.0 copy-start.7
  0.0 1.0 copy-done.2
  1.0 0.1 convert_reduce_fusion
  1.1 0.2 fusion.26
  1.4 0.0 copy-done.5
  1.4 0.1 fusion.28
  1.5 16.3 %collective-permute-start.1 = (bf16[256,512]{1,0:T(8,128)(2,1)S(1)}, bf16[256,512]{1,0:T(8,128)(2,1)S(1)}, u32[]{:S(2)}, u32[]{:S(2)}) collective-permute-start(bf16[256,512]{1,0:T(8,128)(2,1)S(1)} %fusion.28), channel_id=1, source_target_pairs={{0,2},{2,0},{1,3},{3,1},{4,6},{6,4},{5,7},{7,5},{8,10},{10,8},{9,1... | collective-permute-start | bytes 786440 | tf_op jit(solution)/shard_map/ppermute | solution.py:190
  17.8 0.0 copy-done.7
  17.8 0.3 convolution_convert_fusion.3
  18.1 2.9 %collective-permute-start = (bf16[256,512]{1,0:T(8,128)(2,1)S(1)}, bf16[256,512]{1,0:T(8,128)(2,1)S(1)}, u32[]{:S(2)}, u32[]{:S(2)}) collective-permute-start(bf16[256,512]{1,0:T(8,128)(2,1)S(1)} %convolution_convert_fusion.3), channel_id=1, source_target_pairs={{0,1},{1,0},{2,3},{3,2},{4,5},{5,4},{6,7},{7,6},{8,9},{9,8},{10,11... | collective-permute-start | bytes 786440 | tf_op jit(solution)/shard_map/ppermute | solution.py:192
  21.0 4.8 %collective-permute-start.5 = (bf16[256,512]{1,0:T(8,128)(2,1)S(1)}, bf16[256,512]{1,0:T(8,128)(2,1)S(1)}, u32[]{:S(2)}, u32[]{:S(2)}) collective-permute-start(bf16[256,512]{1,0:T(8,128)(2,1)S(1)} %fusion.28), channel_id=1, source_target_pairs={{0,8},{4,12},{8,0},{12,4},{1,9},{5,13},{9,1},{13,5},{2,10},{6,14},... | collective-permute-start | bytes 786440 | tf_op jit(solution)/shard_map/ppermute | solution.py:155
  25.8 2.3 %collective-permute-start.6 = (bf16[256,512]{1,0:T(8,128)(2,1)S(1)}, bf16[256,512]{1,0:T(8,128)(2,1)S(1)}, u32[]{:S(2)}, u32[]{:S(2)}) collective-permute-start(bf16[256,512]{1,0:T(8,128)(2,1)S(1)} %fusion.28), channel_id=1, source_target_pairs={{0,4},{4,8},{8,12},{12,0},{1,5},{5,9},{9,13},{13,1},{2,6},{6,10},{... | collective-permute-start | bytes 786440 | tf_op jit(solution)/shard_map/ppermute | solution.py:155
  28.1 4.2 %collective-permute-start.7 = (bf16[256,512]{1,0:T(8,128)(2,1)S(1)}, bf16[256,512]{1,0:T(8,128)(2,1)S(1)}, u32[]{:S(2)}, u32[]{:S(2)}) collective-permute-start(bf16[256,512]{1,0:T(8,128)(2,1)S(1)} %fusion.28), channel_id=1, source_target_pairs={{0,12},{4,0},{8,4},{12,8},{1,13},{5,1},{9,5},{13,9},{2,14},{6,2},{... | collective-permute-start | bytes 786440 | tf_op jit(solution)/shard_map/ppermute | solution.py:155
  32.3 0.0 collective-permute-done.1
  32.3 1.9 %collective-permute-start.2 = (bf16[256,512]{1,0:T(8,128)(2,1)S(1)}, bf16[256,512]{1,0:T(8,128)(2,1)S(1)}, u32[]{:S(2)}, u32[]{:S(2)}) collective-permute-start(bf16[256,512]{1,0:T(8,128)(2,1)S(1)} %collective-permute-done.1), channel_id=1, source_target_pairs={{0,8},{4,12},{8,0},{12,4},{1,9},{5,13},{9,1},{13,5},{2,10},{6,14},... | collective-permute-start | bytes 786440 | tf_op jit(solution)/shard_map/ppermute | solution.py:155
  34.3 0.0 collective-permute-done
  34.3 2.5 %collective-permute-start.3 = (bf16[256,512]{1,0:T(8,128)(2,1)S(1)}, bf16[256,512]{1,0:T(8,128)(2,1)S(1)}, u32[]{:S(2)}, u32[]{:S(2)}) collective-permute-start(bf16[256,512]{1,0:T(8,128)(2,1)S(1)} %collective-permute-done.1), channel_id=1, source_target_pairs={{0,4},{4,8},{8,12},{12,0},{1,5},{5,9},{9,13},{13,1},{2,6},{6,10},{... | collective-permute-start | bytes 786440 | tf_op jit(solution)/shard_map/ppermute | solution.py:155
  36.8 0.0 collective-permute-done.5
  36.8 4.0 %collective-permute-start.4 = (bf16[256,512]{1,0:T(8,128)(2,1)S(1)}, bf16[256,512]{1,0:T(8,128)(2,1)S(1)}, u32[]{:S(2)}, u32[]{:S(2)}) collective-permute-start(bf16[256,512]{1,0:T(8,128)(2,1)S(1)} %collective-permute-done.1), channel_id=1, source_target_pairs={{0,12},{4,0},{8,4},{12,8},{1,13},{5,1},{9,5},{13,9},{2,14},{6,2},{... | collective-permute-start | bytes 786440 | tf_op jit(solution)/shard_map/ppermute | solution.py:155
  40.8 0.0 collective-permute-done.6
  40.9 0.0 collective-permute-done.7
  40.9 1.2 convolution_convert_fusion.1
  42.1 0.2 fusion.44
  42.3 6.1 %shard_map.73 = (f32[512,512]{1,0:T(8,128)S(1)}, f32[512,8]{1,0:T(8,128)S(1)}, f32[512,8]{1,0:T(8,128)S(1)}) custom-call(bf16[512,512]{1,0:T(8,128)(2,1)S(1)} %pad_maximum_fusion.refs_0_, bf16[1024,512]{1,0:T(8,128)(2,1)S(1)} %get-tuple-element.24.refs_1_, bf16[1024,512]{1,0:T(8,128)(2,1)S(1)} %get-tuple-element.23.refs_2_), custom_call_target="tpu_custom_call" | custom-call | tf_op jit(solution)/shard_map/pallas_call | solution.py:73
  48.4 0.0 collective-permute-done.2
  48.4 1.2 collective-permute-done.3
  49.6 0.0 collective-permute-done.4
  49.6 1.2 convolution_convert_fusion.2
  50.8 0.2 fusion.45
  51.0 5.3 %shard_map.74 = f32[256,640]{1,0:T(8,128)S(1)} custom-call(bf16[512,512]{1,0:T(8,128)(2,1)S(1)} %pad_maximum_fusion.refs_0_, bf16[1024,512]{1,0:T(8,128)(2,1)S(1)} %get-tuple-element.26.refs_1_, bf16[1024,512]{1,0:T(8,128)(2,1)S(1)} %get-tuple-element.25.refs_2_, f32[512,512]{1,0:T(8,128)S(1)} %get-tuple-element.20.refs_3_, ...), custom_call_target="tpu_custom_call" | custom-call | tf_op jit(solution)/shard_map/pallas_call | solution.py:140
  56.3 4.8 %collective-permute-start.8 = (f32[256,640]{1,0:T(8,128)S(1)}, f32[256,640]{1,0:T(8,128)S(1)}, u32[]{:S(2)}, u32[]{:S(2)}) collective-permute-start(f32[256,640]{1,0:T(8,128)S(1)} %shard_map.74), channel_id=1, source_target_pairs={{0,1},{1,0},{2,3},{3,2},{4,5},{5,4},{6,7},{7,6},{8,9},{9,8},{10,11... | collective-permute-start | bytes 1966088 | tf_op jit(solution)/shard_map/ppermute | solution.py:200
  61.1 1.7 %collective-permute-done.8.refs_6_ = f32[256,640]{1,0:T(8,128)S(1)} collective-permute-done((f32[256,640]{1,0:T(8,128)S(1)}, f32[256,640]{1,0:T(8,128)S(1)}, u32[]{:S(2)}, u32[]{:S(2)}) %collective-permute-start.8) | collective-permute-done | bytes 655392 | tf_op jit(solution)/shard_map/ppermute | solution.py:200
  62.8 7.1 %shard_map.75 = bf16[256,512]{1,0:T(8,128)(2,1)S(1)} custom-call(bf16[512,512]{1,0:T(8,128)(2,1)S(1)} %pad_maximum_fusion.refs_0_, bf16[1024,512]{1,0:T(8,128)(2,1)S(1)} %get-tuple-element.26.refs_1_, bf16[1024,512]{1,0:T(8,128)(2,1)S(1)} %get-tuple-element.25.refs_2_, f32[512,512]{1,0:T(8,128)S(1)} %get-tuple-element.20.refs_3_, ...), custom_call_target="tpu_custom_call" | custom-call | tf_op jit(solution)/shard_map/pallas_call | solution.py:122
  69.9 0.0 copy-done
  69.9 0.0 copy-start.6
  69.9 0.0 copy-start.1
  69.9 0.4 fusion.47
  70.3 0.2 multiply_reduce_fusion
  70.5 0.0 copy-done.6
  70.6 0.9 fusion.37
  71.4 18.8 %all-to-all-start = ((bf16[1,32,8,512]{3,2,0,1:T(8,128)(2,1)}), bf16[1,32,8,512]{3,2,0,1:T(8,128)(2,1)S(1)}, u32[]{:S(2)}, u32[]{:S(2)}) async-start(bf16[1,32,8,512]{3,2,0,1:T(8,128)(2,1)} %fusion.37), calls=%async_computation | async-start | bytes 524288 | tf_op jit(solution)/shard_map/all_to_all | solution.py:207
  90.3 0.6 compare_reduce_fusion
  90.9 0.0 copy-done.1
  90.9 0.8 fusion.29
  91.7 17.4 %all-to-all-done = bf16[1,32,8,512]{3,2,0,1:T(8,128)(2,1)S(1)} async-done(((bf16[1,32,8,512]{3,2,0,1:T(8,128)(2,1)}), bf16[1,32,8,512]{3,2,0,1:T(8,128)(2,1)S(1)}, u32[]{:S(2)}, u32[]{:S(2)}) %all-to-all-start) | async-done | bytes 262176 | tf_op jit(solution)/shard_map/all_to_all | solution.py:207
  109.1 0.6 fusion
  109.6 0.1 fusion.46
  109.7 0.3 reshape.102
  110.0 0.3 reshape.103
  110.3 1.1 reshape.101
  111.4 0.0 copy-start.4
  111.4 0.9 fusion.48
  112.2 0.3 fusion.19
  112.5 0.0 copy-done.4
  112.5 0.8 fusion.2
  113.3 0.0 copy-start.3
  113.3 0.2 copy.19
  113.5 0.3 convert_element_type.56
  113.8 23.9 %all_to_all.8 = bf16[32,1,8,512]{3,2,1,0:T(8,128)(2,1)S(1)} all-to-all(bf16[32,1,8,512]{3,2,1,0:T(8,128)(2,1)S(1)} %bitcast.45), channel_id=1, replica_groups=mesh['x'=4,'zlo'=8,'y'=4,'zhi'=2,'core'=2] {'x','zlo'}, dimensions={0} | all-to-all | bytes 524288 | tf_op jit(solution)/shard_map/all_to_all | solution.py:217
  137.7 0.0 copy-done.3
  137.7 1.0 fusion.4
  (6 shorter events, 0.1 us)
Async XLA Ops:
  0.0 69.9 %copy-start = (bf16[512,512]{1,0:T(8,128)(2,1)S(1)}, bf16[512,512]{1,0:T(8,128)(2,1)}, u32[]{:S(2)}) copy-start(bf16[512,512]{1,0:T(8,128)(2,1)} %param.12) | copy-start | bytes 1572868
  0.0 1.0 copy-start.2
  0.0 1.4 copy-start.5
  0.0 17.8 %copy-start.7 = (bf16[512,1536]{1,0:T(8,128)(2,1)S(1)}, bf16[512,1536]{1,0:T(8,128)(2,1)}, u32[]{:S(2)}) copy-start(bf16[512,1536]{1,0:T(8,128)(2,1)} %param.11) | copy-start | bytes 4718596
  1.5 30.8 %collective-permute-start.1 = (bf16[256,512]{1,0:T(8,128)(2,1)S(1)}, bf16[256,512]{1,0:T(8,128)(2,1)S(1)}, u32[]{:S(2)}, u32[]{:S(2)}) collective-permute-start(bf16[256,512]{1,0:T(8,128)(2,1)S(1)} %fusion.28), channel_id=1, source_target_pairs={{0,2},{2,0},{1,3},{3,1},{4,6},{6,4},{5,7},{7,5},{8,10},{10,8},{9,1... | collective-permute-start | bytes 786440 | tf_op jit(solution)/shard_map/ppermute | solution.py:190
  18.1 16.2 %collective-permute-start = (bf16[256,512]{1,0:T(8,128)(2,1)S(1)}, bf16[256,512]{1,0:T(8,128)(2,1)S(1)}, u32[]{:S(2)}, u32[]{:S(2)}) collective-permute-start(bf16[256,512]{1,0:T(8,128)(2,1)S(1)} %convolution_convert_fusion.3), channel_id=1, source_target_pairs={{0,1},{1,0},{2,3},{3,2},{4,5},{5,4},{6,7},{7,6},{8,9},{9,8},{10,11... | collective-permute-start | bytes 786440 | tf_op jit(solution)/shard_map/ppermute | solution.py:192
  21.0 15.8 %collective-permute-start.5 = (bf16[256,512]{1,0:T(8,128)(2,1)S(1)}, bf16[256,512]{1,0:T(8,128)(2,1)S(1)}, u32[]{:S(2)}, u32[]{:S(2)}) collective-permute-start(bf16[256,512]{1,0:T(8,128)(2,1)S(1)} %fusion.28), channel_id=1, source_target_pairs={{0,8},{4,12},{8,0},{12,4},{1,9},{5,13},{9,1},{13,5},{2,10},{6,14},... | collective-permute-start | bytes 786440 | tf_op jit(solution)/shard_map/ppermute | solution.py:155
  25.8 15.0 %collective-permute-start.6 = (bf16[256,512]{1,0:T(8,128)(2,1)S(1)}, bf16[256,512]{1,0:T(8,128)(2,1)S(1)}, u32[]{:S(2)}, u32[]{:S(2)}) collective-permute-start(bf16[256,512]{1,0:T(8,128)(2,1)S(1)} %fusion.28), channel_id=1, source_target_pairs={{0,4},{4,8},{8,12},{12,0},{1,5},{5,9},{9,13},{13,1},{2,6},{6,10},{... | collective-permute-start | bytes 786440 | tf_op jit(solution)/shard_map/ppermute | solution.py:155
  28.1 12.7 %collective-permute-start.7 = (bf16[256,512]{1,0:T(8,128)(2,1)S(1)}, bf16[256,512]{1,0:T(8,128)(2,1)S(1)}, u32[]{:S(2)}, u32[]{:S(2)}) collective-permute-start(bf16[256,512]{1,0:T(8,128)(2,1)S(1)} %fusion.28), channel_id=1, source_target_pairs={{0,12},{4,0},{8,4},{12,8},{1,13},{5,1},{9,5},{13,9},{2,14},{6,2},{... | collective-permute-start | bytes 786440 | tf_op jit(solution)/shard_map/ppermute | solution.py:155
  32.3 16.0 %collective-permute-start.2 = (bf16[256,512]{1,0:T(8,128)(2,1)S(1)}, bf16[256,512]{1,0:T(8,128)(2,1)S(1)}, u32[]{:S(2)}, u32[]{:S(2)}) collective-permute-start(bf16[256,512]{1,0:T(8,128)(2,1)S(1)} %collective-permute-done.1), channel_id=1, source_target_pairs={{0,8},{4,12},{8,0},{12,4},{1,9},{5,13},{9,1},{13,5},{2,10},{6,14},... | collective-permute-start | bytes 786440 | tf_op jit(solution)/shard_map/ppermute | solution.py:155
  34.3 15.3 %collective-permute-start.3 = (bf16[256,512]{1,0:T(8,128)(2,1)S(1)}, bf16[256,512]{1,0:T(8,128)(2,1)S(1)}, u32[]{:S(2)}, u32[]{:S(2)}) collective-permute-start(bf16[256,512]{1,0:T(8,128)(2,1)S(1)} %collective-permute-done.1), channel_id=1, source_target_pairs={{0,4},{4,8},{8,12},{12,0},{1,5},{5,9},{9,13},{13,1},{2,6},{6,10},{... | collective-permute-start | bytes 786440 | tf_op jit(solution)/shard_map/ppermute | solution.py:155
  36.8 12.8 %collective-permute-start.4 = (bf16[256,512]{1,0:T(8,128)(2,1)S(1)}, bf16[256,512]{1,0:T(8,128)(2,1)S(1)}, u32[]{:S(2)}, u32[]{:S(2)}) collective-permute-start(bf16[256,512]{1,0:T(8,128)(2,1)S(1)} %collective-permute-done.1), channel_id=1, source_target_pairs={{0,12},{4,0},{8,4},{12,8},{1,13},{5,1},{9,5},{13,9},{2,14},{6,2},{... | collective-permute-start | bytes 786440 | tf_op jit(solution)/shard_map/ppermute | solution.py:155
  56.3 6.5 %collective-permute-start.8 = (f32[256,640]{1,0:T(8,128)S(1)}, f32[256,640]{1,0:T(8,128)S(1)}, u32[]{:S(2)}, u32[]{:S(2)}) collective-permute-start(f32[256,640]{1,0:T(8,128)S(1)} %shard_map.74), channel_id=1, source_target_pairs={{0,1},{1,0},{2,3},{3,2},{4,5},{5,4},{6,7},{7,6},{8,9},{9,8},{10,11... | collective-permute-start | bytes 1966088 | tf_op jit(solution)/shard_map/ppermute | solution.py:200
  69.9 0.7 copy-start.6
  69.9 21.0 %copy-start.1 = (bf16[512,1536]{1,0:T(8,128)(2,1)S(1)}, bf16[512,1536]{1,0:T(8,128)(2,1)}, u32[]{:S(2)}) copy-start(bf16[512,1536]{1,0:T(8,128)(2,1)} %param.14) | copy-start | bytes 4718596
  71.4 37.6 %all-to-all-start = ((bf16[1,32,8,512]{3,2,0,1:T(8,128)(2,1)}), bf16[1,32,8,512]{3,2,0,1:T(8,128)(2,1)S(1)}, u32[]{:S(2)}, u32[]{:S(2)}) async-start(bf16[1,32,8,512]{3,2,0,1:T(8,128)(2,1)} %fusion.37), calls=%async_computation | async-start | bytes 524288 | tf_op jit(solution)/shard_map/all_to_all | solution.py:207
  111.4 1.2 copy-start.4
  113.3 24.5 %copy-start.3 = (bf16[512,512]{1,0:T(8,128)(2,1)S(1)}, bf16[512,512]{1,0:T(8,128)(2,1)}, u32[]{:S(2)}) copy-start(bf16[512,512]{1,0:T(8,128)(2,1)} %param.15) | copy-start | bytes 1572868
